TPU v7x, 512 devices: a whole 4x8x8 slice. The times are simulated.
512 devices in a mesh: blk: 64 (over z, y_hi, core), grp: 8 (over x, y_lo).
Axes of the slice: x: 4, y: 8 (y_hi: 4, y_lo: 2; y = y_hi * 2 + y_lo), z: 8, core: 2. Of those that a mesh axis runs over, the one named last changes fastest.
Arguments:
- queries: bfloat16 [131072, 2048], P(('blk', 'grp')), may hold values from -100 to 100
- keys: bfloat16 [131072, 1024], P(('blk', 'grp')), may hold values from -4 to 4
- values: bfloat16 [131072, 1024], P(('blk', 'grp')), may hold values from -6 to 6
Outputs:
- attended: bfloat16 [131072, 2048], P(('blk', 'grp'))
All inputs are finite; a program needn't handle non-finite values.
Results may differ from a plain program's by a relative error of at most 0.0049.
Values may be sent and summed in bfloat16 or wider, within the bound.
No kernel may reach another device: no remote copies, remote signals or barrier semaphores. Data moves between devices by JAX's collectives and lax.ppermute only.
A program may use at most 64 MiB of HBM per device.

v0:
```python
import jax
import jax.numpy as jnp
from jax import lax
from jax.sharding import PartitionSpec as P

HEADS = 16
KV_HEADS = 8
HEAD_DIM = 128
WINDOW = 1024


def from_behind(x, axis, by):
    peers = lax.axis_size(axis)
    pairs = [(i, i + by) for i in range(peers) if 0 <= i + by < peers]
    return lax.ppermute(x, axis, pairs)


def attend_block(query_rows, key_win, value_win, block_index):
    tok_rows = query_rows.shape[0]
    group_size = HEADS // KV_HEADS
    span_rows = key_win.shape[0]
    row_ids = jnp.arange(tok_rows, dtype=jnp.int32)[:, None]
    col_ids = jnp.arange(span_rows, dtype=jnp.int32)[None, :]
    position = block_index * tok_rows - WINDOW + col_ids
    allowed = (col_ids > row_ids) & (col_ids <= row_ids + WINDOW) & (position >= 0)

    def head_group(head_index):
        query_part = lax.dynamic_slice_in_dim(
            query_rows, head_index * group_size * HEAD_DIM, group_size * HEAD_DIM, 1
        )
        query_part = query_part.reshape(tok_rows, group_size, HEAD_DIM)
        key_part = lax.dynamic_slice_in_dim(key_win, head_index * HEAD_DIM, HEAD_DIM, 1)
        value_part = lax.dynamic_slice_in_dim(value_win, head_index * HEAD_DIM, HEAD_DIM, 1)
        score = jnp.einsum(
            "thd,kd->htk", query_part, key_part, preferred_element_type=jnp.float32
        ) * HEAD_DIM ** (-0.5)
        score = jnp.where(allowed[None], score, jnp.float32(-1e30))
        largest = jnp.max(score, axis=2, keepdims=True)
        expo = jnp.where(allowed[None], jnp.exp(score - largest), jnp.float32(0.0))
        total = jnp.sum(expo, axis=2, keepdims=True)
        weight = (expo / total).astype(jnp.bfloat16)
        output = jnp.einsum("htk,kd->thd", weight, value_part, preferred_element_type=jnp.float32)
        return output.astype(jnp.bfloat16).reshape(tok_rows, group_size * HEAD_DIM)

    parts = lax.map(head_group, jnp.arange(KV_HEADS, dtype=jnp.int32))
    return jnp.transpose(parts, (1, 0, 2)).reshape(tok_rows, HEADS * HEAD_DIM)


def body(queries, keys, values):
    tok_rows = queries.shape[0]
    back_blocks = WINDOW // tok_rows
    block_index = lax.axis_index(("blk", "grp"))
    pieces_k = []
    pieces_v = []
    for offset in range(back_blocks, 0, -1):
        moved_k, moved_v = from_behind((keys, values), ("blk", "grp"), offset)
        pieces_k.append(moved_k)
        pieces_v.append(moved_v)
    key_win = jnp.concatenate(pieces_k + [keys], axis=0)
    value_win = jnp.concatenate(pieces_v + [values], axis=0)
    return attend_block(queries, key_win, value_win, block_index)


def solution(mesh):
    placed = (P(("blk", "grp"), None), P(("blk", "grp"), None), P(("blk", "grp"), None))
    return jax.shard_map(
        body, mesh=mesh, in_specs=placed, out_specs=P(("blk", "grp"), None), check_vma=False
    )
```

profile of v0, /device:TPU:95, one launch (start us, length us, event | category | flops | bytes accessed | tf_op | source)
XLA Modules:
  0.0 191.8 jit_solution(11916820409449374037)
XLA Ops:
  0.0 1.3 copy.13
  1.3 5.9 %collective-permute-start = (bf16[256,1024]{0,1:T(8,128)(2,1)S(1)}, bf16[256,1024]{0,1:T(8,128)(2,1)}, u32[]{:S(2)}, u32[]{:S(2)}) collective-permute-start(bf16[256,1024]{0,1:T(8,128)(2,1)S(1)} %copy.13), channel_id=1, source_target_pairs={{0,4},{1,5},{2,6},{3,7},{4,8},{5,9},{6,10},{7,11},{8,12},{9,13},{1... | collective-permute-start | bytes 1572872 | tf_op jit(solution)/shard_map/ppermute | solution.py:15
  7.2 3.9 %collective-permute-start.1 = (bf16[256,1024]{0,1:T(8,128)(2,1)S(1)}, bf16[256,1024]{0,1:T(8,128)(2,1)}, u32[]{:S(2)}, u32[]{:S(2)}) collective-permute-start(bf16[256,1024]{0,1:T(8,128)(2,1)S(1)} %copy.13), channel_id=1, source_target_pairs={{0,3},{1,4},{2,5},{3,6},{4,7},{5,8},{6,9},{7,10},{8,11},{9,12},{10... | collective-permute-start | bytes 1572872 | tf_op jit(solution)/shard_map/ppermute | solution.py:15
  11.2 2.8 %collective-permute-start.2 = (bf16[256,1024]{0,1:T(8,128)(2,1)S(1)}, bf16[256,1024]{0,1:T(8,128)(2,1)}, u32[]{:S(2)}, u32[]{:S(2)}) collective-permute-start(bf16[256,1024]{0,1:T(8,128)(2,1)S(1)} %copy.13), channel_id=1, source_target_pairs={{0,2},{1,3},{2,4},{3,5},{4,6},{5,7},{6,8},{7,9},{8,10},{9,11},{10,... | collective-permute-start | bytes 1572872 | tf_op jit(solution)/shard_map/ppermute | solution.py:15
  14.0 1.9 %collective-permute-start.3 = (bf16[256,1024]{0,1:T(8,128)(2,1)S(1)}, bf16[256,1024]{0,1:T(8,128)(2,1)S(1)}, u32[]{:S(2)}, u32[]{:S(2)}) collective-permute-start(bf16[256,1024]{0,1:T(8,128)(2,1)S(1)} %copy.13), channel_id=1, source_target_pairs={{0,1},{1,2},{2,3},{3,4},{4,5},{5,6},{6,7},{7,8},{8,9},{9,10},{10,1... | collective-permute-start | bytes 1572872 | tf_op jit(solution)/shard_map/ppermute | solution.py:15
  15.9 5.3 %collective-permute-start.4 = (bf16[256,1024]{1,0:T(8,128)(2,1)}, bf16[256,1024]{1,0:T(8,128)(2,1)S(1)}, u32[]{:S(2)}, u32[]{:S(2)}) collective-permute-start(bf16[256,1024]{1,0:T(8,128)(2,1)} %param.6), channel_id=1, source_target_pairs={{0,4},{1,5},{2,6},{3,7},{4,8},{5,9},{6,10},{7,11},{8,12},{9,13},{1... | collective-permute-start | bytes 1572872 | tf_op jit(solution)/shard_map/ppermute | solution.py:15
  21.2 13.5 %collective-permute-start.5 = (bf16[256,1024]{1,0:T(8,128)(2,1)}, bf16[256,1024]{1,0:T(8,128)(2,1)S(1)}, u32[]{:S(2)}, u32[]{:S(2)}) collective-permute-start(bf16[256,1024]{1,0:T(8,128)(2,1)} %param.6), channel_id=1, source_target_pairs={{0,3},{1,4},{2,5},{3,6},{4,7},{5,8},{6,9},{7,10},{8,11},{9,12},{10... | collective-permute-start | bytes 1572872 | tf_op jit(solution)/shard_map/ppermute | solution.py:15
  34.7 1.1 constant_dynamic-update-slice_fusion.5
  35.8 8.2 %collective-permute-done.1 = bf16[256,1024]{0,1:T(8,128)(2,1)} collective-permute-done((bf16[256,1024]{0,1:T(8,128)(2,1)S(1)}, bf16[256,1024]{0,1:T(8,128)(2,1)}, u32[]{:S(2)}, u32[]{:S(2)}) %collective-permute-start.1) | collective-permute-done | bytes 524320 | tf_op jit(solution)/shard_map/ppermute | solution.py:15
  43.9 22.3 %collective-permute-start.6 = (bf16[256,1024]{1,0:T(8,128)(2,1)}, bf16[256,1024]{1,0:T(8,128)(2,1)S(1)}, u32[]{:S(2)}, u32[]{:S(2)}) collective-permute-start(bf16[256,1024]{1,0:T(8,128)(2,1)} %param.6), channel_id=1, source_target_pairs={{0,2},{1,3},{2,4},{3,5},{4,6},{5,7},{6,8},{7,9},{8,10},{9,11},{10,... | collective-permute-start | bytes 1572872 | tf_op jit(solution)/shard_map/ppermute | solution.py:15
  66.2 1.1 constant_dynamic-update-slice_fusion.4
  67.3 16.5 %collective-permute-start.7 = (bf16[256,1024]{1,0:T(8,128)(2,1)S(1)}, bf16[256,1024]{1,0:T(8,128)(2,1)S(1)}, u32[]{:S(2)}, u32[]{:S(2)}) collective-permute-start(bf16[256,1024]{1,0:T(8,128)(2,1)S(1)} %copy-done), channel_id=1, source_target_pairs={{0,1},{1,2},{2,3},{3,4},{4,5},{5,6},{6,7},{7,8},{8,9},{9,10},{10,1... | collective-permute-start | bytes 1572872 | tf_op jit(solution)/shard_map/ppermute | solution.py:15
  83.8 1.1 constant_dynamic-update-slice_fusion.3
  84.9 1.7 collective-permute-done.3
  86.9 29.0 %collective-permute-done.7 = bf16[256,1024]{1,0:T(8,128)(2,1)S(1)} collective-permute-done((bf16[256,1024]{1,0:T(8,128)(2,1)S(1)}, bf16[256,1024]{1,0:T(8,128)(2,1)S(1)}, u32[]{:S(2)}, u32[]{:S(2)}) %collective-permute-start.7) | collective-permute-done | bytes 524320 | tf_op jit(solution)/shard_map/ppermute | solution.py:15
  116.0 1.5 copy-done.2
  117.5 72.9 %while.13 = (s32[]{:T(128)}, bf16[8,256,256]{1,2,0:T(8,128)(2,1)S(1)}, s32[8]{0:T(128)S(1)}, bf16[1280,1024]{0,1:T(8,128)(2,1)}, bf16[1280,1024]{1,0:T(8,128)(2,...) while((s32[]{:T(128)}, ...), condition=%wide.region_3.4_spmd.clone, body=%wide.region_0.3_spmd.clone.sunk | while | flops 341509376 | bytes 7936509 | solution.py:45
  117.5 0.6 dynamic_slice.51
  118.6 0.9 constant_dynamic-slice_fusion.2
  119.6 0.1 copy.25
  120.3 0.3 fusion.40
  120.6 3.7 %fusion.41 = (f32[2,256]{1,0:T(2,128)S(1)}, f32[2,256,1280]{1,2,0:T(8,128)}) fusion(bf16[256,2,128]{0,2,1:T(8,128)(2,1)S(1)} %bitcast.48, pred[256,1280]{0,1:T(8,128)(4,1)S(1)} %fusion.40, bf16[1280,1024]{1,0:T(8,128)(2,1)} %get-tuple-element.226, s32[]{:T(128)S(6)} %select_n.43), kind=kOutput, calls=%fused_computation.39.clone.1 | convolution fusion | flops 171050240 | bytes 3737604 | tf_op jit(solution)/shard_map/while/body/eval_jaxpr/sub | solution.py:39
  124.3 2.2 %fusion.42 = bf16[128,2,256]{2,0,1:T(8,128)(2,1)S(1)} fusion(f32[2,256,1280]{1,2,0:T(8,128)} %get-tuple-element.192, f32[2,256]{1,0:T(2,128)S(1)} %get-tuple-element.193, bf16[1280,1024]{0,1:T(8,128)(2,1)} %get-tuple-element.225, s32[]{:T(128)S(6)} %select_n.43), kind=kOutput, calls=%fused_computation.14.clone.1 | convolution fusion | flops 169148416 | bytes 3082244 | tf_op jit(solution)/shard_map/while/body/eval_jaxpr/htk,kd->thd/dot_general | solution.py:42
  126.6 0.6 dynamic_slice.51
  127.8 0.9 constant_dynamic-slice_fusion.2
  128.7 0.1 copy.25
  129.4 0.3 fusion.40
  129.7 3.7 %fusion.41 = (f32[2,256]{1,0:T(2,128)S(1)}, f32[2,256,1280]{1,2,0:T(8,128)}) fusion(bf16[256,2,128]{0,2,1:T(8,128)(2,1)S(1)} %bitcast.48, pred[256,1280]{0,1:T(8,128)(4,1)S(1)} %fusion.40, bf16[1280,1024]{1,0:T(8,128)(2,1)} %get-tuple-element.226, s32[]{:T(128)S(6)} %select_n.43), kind=kOutput, calls=%fused_computation.39.clone.1 | convolution fusion | flops 171050240 | bytes 3737604 | tf_op jit(solution)/shard_map/while/body/eval_jaxpr/sub | solution.py:39
  133.5 2.2 %fusion.42 = bf16[128,2,256]{2,0,1:T(8,128)(2,1)S(1)} fusion(f32[2,256,1280]{1,2,0:T(8,128)} %get-tuple-element.192, f32[2,256]{1,0:T(2,128)S(1)} %get-tuple-element.193, bf16[1280,1024]{0,1:T(8,128)(2,1)} %get-tuple-element.225, s32[]{:T(128)S(6)} %select_n.43), kind=kOutput, calls=%fused_computation.14.clone.1 | convolution fusion | flops 169148416 | bytes 3082244 | tf_op jit(solution)/shard_map/while/body/eval_jaxpr/htk,kd->thd/dot_general | solution.py:42
  135.7 0.6 dynamic_slice.51
  136.9 0.9 constant_dynamic-slice_fusion.2
  137.8 0.1 copy.25
  138.5 0.3 fusion.40
  138.8 3.7 %fusion.41 = (f32[2,256]{1,0:T(2,128)S(1)}, f32[2,256,1280]{1,2,0:T(8,128)}) fusion(bf16[256,2,128]{0,2,1:T(8,128)(2,1)S(1)} %bitcast.48, pred[256,1280]{0,1:T(8,128)(4,1)S(1)} %fusion.40, bf16[1280,1024]{1,0:T(8,128)(2,1)} %get-tuple-element.226, s32[]{:T(128)S(6)} %select_n.43), kind=kOutput, calls=%fused_computation.39.clone.1 | convolution fusion | flops 171050240 | bytes 3737604 | tf_op jit(solution)/shard_map/while/body/eval_jaxpr/sub | solution.py:39
  142.6 2.2 %fusion.42 = bf16[128,2,256]{2,0,1:T(8,128)(2,1)S(1)} fusion(f32[2,256,1280]{1,2,0:T(8,128)} %get-tuple-element.192, f32[2,256]{1,0:T(2,128)S(1)} %get-tuple-element.193, bf16[1280,1024]{0,1:T(8,128)(2,1)} %get-tuple-element.225, s32[]{:T(128)S(6)} %select_n.43), kind=kOutput, calls=%fused_computation.14.clone.1 | convolution fusion | flops 169148416 | bytes 3082244 | tf_op jit(solution)/shard_map/while/body/eval_jaxpr/htk,kd->thd/dot_general | solution.py:42
  144.8 0.6 dynamic_slice.51
  146.0 0.9 constant_dynamic-slice_fusion.2
  146.9 0.1 copy.25
  147.6 0.3 fusion.40
  147.9 3.7 %fusion.41 = (f32[2,256]{1,0:T(2,128)S(1)}, f32[2,256,1280]{1,2,0:T(8,128)}) fusion(bf16[256,2,128]{0,2,1:T(8,128)(2,1)S(1)} %bitcast.48, pred[256,1280]{0,1:T(8,128)(4,1)S(1)} %fusion.40, bf16[1280,1024]{1,0:T(8,128)(2,1)} %get-tuple-element.226, s32[]{:T(128)S(6)} %select_n.43), kind=kOutput, calls=%fused_computation.39.clone.1 | convolution fusion | flops 171050240 | bytes 3737604 | tf_op jit(solution)/shard_map/while/body/eval_jaxpr/sub | solution.py:39
  151.7 2.2 %fusion.42 = bf16[128,2,256]{2,0,1:T(8,128)(2,1)S(1)} fusion(f32[2,256,1280]{1,2,0:T(8,128)} %get-tuple-element.192, f32[2,256]{1,0:T(2,128)S(1)} %get-tuple-element.193, bf16[1280,1024]{0,1:T(8,128)(2,1)} %get-tuple-element.225, s32[]{:T(128)S(6)} %select_n.43), kind=kOutput, calls=%fused_computation.14.clone.1 | convolution fusion | flops 169148416 | bytes 3082244 | tf_op jit(solution)/shard_map/while/body/eval_jaxpr/htk,kd->thd/dot_general | solution.py:42
  153.9 0.6 dynamic_slice.51
  155.1 0.9 constant_dynamic-slice_fusion.2
  156.0 0.1 copy.25
  156.7 0.3 fusion.40
  157.1 3.7 %fusion.41 = (f32[2,256]{1,0:T(2,128)S(1)}, f32[2,256,1280]{1,2,0:T(8,128)}) fusion(bf16[256,2,128]{0,2,1:T(8,128)(2,1)S(1)} %bitcast.48, pred[256,1280]{0,1:T(8,128)(4,1)S(1)} %fusion.40, bf16[1280,1024]{1,0:T(8,128)(2,1)} %get-tuple-element.226, s32[]{:T(128)S(6)} %select_n.43), kind=kOutput, calls=%fused_computation.39.clone.1 | convolution fusion | flops 171050240 | bytes 3737604 | tf_op jit(solution)/shard_map/while/body/eval_jaxpr/sub | solution.py:39
  160.8 2.2 %fusion.42 = bf16[128,2,256]{2,0,1:T(8,128)(2,1)S(1)} fusion(f32[2,256,1280]{1,2,0:T(8,128)} %get-tuple-element.192, f32[2,256]{1,0:T(2,128)S(1)} %get-tuple-element.193, bf16[1280,1024]{0,1:T(8,128)(2,1)} %get-tuple-element.225, s32[]{:T(128)S(6)} %select_n.43), kind=kOutput, calls=%fused_computation.14.clone.1 | convolution fusion | flops 169148416 | bytes 3082244 | tf_op jit(solution)/shard_map/while/body/eval_jaxpr/htk,kd->thd/dot_general | solution.py:42
  163.1 0.6 dynamic_slice.51
  164.2 0.9 constant_dynamic-slice_fusion.2
  165.2 0.1 copy.25
  165.9 0.3 fusion.40
  166.2 3.7 %fusion.41 = (f32[2,256]{1,0:T(2,128)S(1)}, f32[2,256,1280]{1,2,0:T(8,128)}) fusion(bf16[256,2,128]{0,2,1:T(8,128)(2,1)S(1)} %bitcast.48, pred[256,1280]{0,1:T(8,128)(4,1)S(1)} %fusion.40, bf16[1280,1024]{1,0:T(8,128)(2,1)} %get-tuple-element.226, s32[]{:T(128)S(6)} %select_n.43), kind=kOutput, calls=%fused_computation.39.clone.1 | convolution fusion | flops 171050240 | bytes 3737604 | tf_op jit(solution)/shard_map/while/body/eval_jaxpr/sub | solution.py:39
  169.9 2.2 %fusion.42 = bf16[128,2,256]{2,0,1:T(8,128)(2,1)S(1)} fusion(f32[2,256,1280]{1,2,0:T(8,128)} %get-tuple-element.192, f32[2,256]{1,0:T(2,128)S(1)} %get-tuple-element.193, bf16[1280,1024]{0,1:T(8,128)(2,1)} %get-tuple-element.225, s32[]{:T(128)S(6)} %select_n.43), kind=kOutput, calls=%fused_computation.14.clone.1 | convolution fusion | flops 169148416 | bytes 3082244 | tf_op jit(solution)/shard_map/while/body/eval_jaxpr/htk,kd->thd/dot_general | solution.py:42
  172.2 0.6 dynamic_slice.51
  173.4 0.9 constant_dynamic-slice_fusion.2
  175.0 0.3 fusion.40
  175.3 3.7 %fusion.41 = (f32[2,256]{1,0:T(2,128)S(1)}, f32[2,256,1280]{1,2,0:T(8,128)}) fusion(bf16[256,2,128]{0,2,1:T(8,128)(2,1)S(1)} %bitcast.48, pred[256,1280]{0,1:T(8,128)(4,1)S(1)} %fusion.40, bf16[1280,1024]{1,0:T(8,128)(2,1)} %get-tuple-element.226, s32[]{:T(128)S(6)} %select_n.43), kind=kOutput, calls=%fused_computation.39.clone.1 | convolution fusion | flops 171050240 | bytes 3737604 | tf_op jit(solution)/shard_map/while/body/eval_jaxpr/sub | solution.py:39
  179.1 2.2 %fusion.42 = bf16[128,2,256]{2,0,1:T(8,128)(2,1)S(1)} fusion(f32[2,256,1280]{1,2,0:T(8,128)} %get-tuple-element.192, f32[2,256]{1,0:T(2,128)S(1)} %get-tuple-element.193, bf16[1280,1024]{0,1:T(8,128)(2,1)} %get-tuple-element.225, s32[]{:T(128)S(6)} %select_n.43), kind=kOutput, calls=%fused_computation.14.clone.1 | convolution fusion | flops 169148416 | bytes 3082244 | tf_op jit(solution)/shard_map/while/body/eval_jaxpr/htk,kd->thd/dot_general | solution.py:42
  181.3 0.6 dynamic_slice.51
  182.5 0.9 constant_dynamic-slice_fusion.2
  184.1 0.3 fusion.40
  184.4 3.7 %fusion.41 = (f32[2,256]{1,0:T(2,128)S(1)}, f32[2,256,1280]{1,2,0:T(8,128)}) fusion(bf16[256,2,128]{0,2,1:T(8,128)(2,1)S(1)} %bitcast.48, pred[256,1280]{0,1:T(8,128)(4,1)S(1)} %fusion.40, bf16[1280,1024]{1,0:T(8,128)(2,1)} %get-tuple-element.226, s32[]{:T(128)S(6)} %select_n.43), kind=kOutput, calls=%fused_computation.39.clone.1 | convolution fusion | flops 171050240 | bytes 3737604 | tf_op jit(solution)/shard_map/while/body/eval_jaxpr/sub | solution.py:39
  188.2 2.2 %fusion.42 = bf16[128,2,256]{2,0,1:T(8,128)(2,1)S(1)} fusion(f32[2,256,1280]{1,2,0:T(8,128)} %get-tuple-element.192, f32[2,256]{1,0:T(2,128)S(1)} %get-tuple-element.193, bf16[1280,1024]{0,1:T(8,128)(2,1)} %get-tuple-element.225, s32[]{:T(128)S(6)} %select_n.43), kind=kOutput, calls=%fused_computation.14.clone.1 | convolution fusion | flops 169148416 | bytes 3082244 | tf_op jit(solution)/shard_map/while/body/eval_jaxpr/htk,kd->thd/dot_general | solution.py:42
  190.4 1.4 copy.22
  (31 shorter events, 0.6 us)
Async XLA Ops:
  0.0 67.3 %copy-start = (bf16[256,1024]{1,0:T(8,128)(2,1)S(1)}, bf16[256,1024]{1,0:T(8,128)(2,1)}, u32[]{:S(2)}) copy-start(bf16[256,1024]{1,0:T(8,128)(2,1)} %param.6) | copy-start | bytes 1572868
  1.3 19.9 %collective-permute-start = (bf16[256,1024]{0,1:T(8,128)(2,1)S(1)}, bf16[256,1024]{0,1:T(8,128)(2,1)}, u32[]{:S(2)}, u32[]{:S(2)}) collective-permute-start(bf16[256,1024]{0,1:T(8,128)(2,1)S(1)} %copy.13), channel_id=1, source_target_pairs={{0,4},{1,5},{2,6},{3,7},{4,8},{5,9},{6,10},{7,11},{8,12},{9,13},{1... | collective-permute-start | bytes 1572872 | tf_op jit(solution)/shard_map/ppermute | solution.py:15
  7.2 36.7 %collective-permute-start.1 = (bf16[256,1024]{0,1:T(8,128)(2,1)S(1)}, bf16[256,1024]{0,1:T(8,128)(2,1)}, u32[]{:S(2)}, u32[]{:S(2)}) collective-permute-start(bf16[256,1024]{0,1:T(8,128)(2,1)S(1)} %copy.13), channel_id=1, source_target_pairs={{0,3},{1,4},{2,5},{3,6},{4,7},{5,8},{6,9},{7,10},{8,11},{9,12},{10... | collective-permute-start | bytes 1572872 | tf_op jit(solution)/shard_map/ppermute | solution.py:15
  11.2 56.2 %collective-permute-start.2 = (bf16[256,1024]{0,1:T(8,128)(2,1)S(1)}, bf16[256,1024]{0,1:T(8,128)(2,1)}, u32[]{:S(2)}, u32[]{:S(2)}) collective-permute-start(bf16[256,1024]{0,1:T(8,128)(2,1)S(1)} %copy.13), channel_id=1, source_target_pairs={{0,2},{1,3},{2,4},{3,5},{4,6},{5,7},{6,8},{7,9},{8,10},{9,11},{10,... | collective-permute-start | bytes 1572872 | tf_op jit(solution)/shard_map/ppermute | solution.py:15
  14.0 72.7 %collective-permute-start.3 = (bf16[256,1024]{0,1:T(8,128)(2,1)S(1)}, bf16[256,1024]{0,1:T(8,128)(2,1)S(1)}, u32[]{:S(2)}, u32[]{:S(2)}) collective-permute-start(bf16[256,1024]{0,1:T(8,128)(2,1)S(1)} %copy.13), channel_id=1, source_target_pairs={{0,1},{1,2},{2,3},{3,4},{4,5},{5,6},{6,7},{7,8},{8,9},{9,10},{10,1... | collective-permute-start | bytes 1572872 | tf_op jit(solution)/shard_map/ppermute | solution.py:15
  15.9 70.8 %collective-permute-start.4 = (bf16[256,1024]{1,0:T(8,128)(2,1)}, bf16[256,1024]{1,0:T(8,128)(2,1)S(1)}, u32[]{:S(2)}, u32[]{:S(2)}) collective-permute-start(bf16[256,1024]{1,0:T(8,128)(2,1)} %param.6), channel_id=1, source_target_pairs={{0,4},{1,5},{2,6},{3,7},{4,8},{5,9},{6,10},{7,11},{8,12},{9,13},{1... | collective-permute-start | bytes 1572872 | tf_op jit(solution)/shard_map/ppermute | solution.py:15
  21.2 65.6 %collective-permute-start.5 = (bf16[256,1024]{1,0:T(8,128)(2,1)}, bf16[256,1024]{1,0:T(8,128)(2,1)S(1)}, u32[]{:S(2)}, u32[]{:S(2)}) collective-permute-start(bf16[256,1024]{1,0:T(8,128)(2,1)} %param.6), channel_id=1, source_target_pairs={{0,3},{1,4},{2,5},{3,6},{4,7},{5,8},{6,9},{7,10},{8,11},{9,12},{10... | collective-permute-start | bytes 1572872 | tf_op jit(solution)/shard_map/ppermute | solution.py:15
  43.9 42.9 %collective-permute-start.6 = (bf16[256,1024]{1,0:T(8,128)(2,1)}, bf16[256,1024]{1,0:T(8,128)(2,1)S(1)}, u32[]{:S(2)}, u32[]{:S(2)}) collective-permute-start(bf16[256,1024]{1,0:T(8,128)(2,1)} %param.6), channel_id=1, source_target_pairs={{0,2},{1,3},{2,4},{3,5},{4,6},{5,7},{6,8},{7,9},{8,10},{9,11},{10,... | collective-permute-start | bytes 1572872 | tf_op jit(solution)/shard_map/ppermute | solution.py:15
  67.3 48.5 %collective-permute-start.7 = (bf16[256,1024]{1,0:T(8,128)(2,1)S(1)}, bf16[256,1024]{1,0:T(8,128)(2,1)S(1)}, u32[]{:S(2)}, u32[]{:S(2)}) collective-permute-start(bf16[256,1024]{1,0:T(8,128)(2,1)S(1)} %copy-done), channel_id=1, source_target_pairs={{0,1},{1,2},{2,3},{3,4},{4,5},{5,6},{6,7},{7,8},{8,9},{9,10},{10,1... | collective-permute-start | bytes 1572872 | tf_op jit(solution)/shard_map/ppermute | solution.py:15
  86.7 29.2 %copy-start.1 = (bf16[1280,1024]{0,1:T(8,128)(2,1)}, bf16[1280,1024]{0,1:T(8,128)(2,1)S(1)}, u32[]{:S(2)}) copy-start(bf16[1280,1024]{0,1:T(8,128)(2,1)S(1)} %constant_dynamic-update-slice_fusion.1) | copy-start | bytes 7864324
  116.0 1.5 copy-start.2
where the time goes:
time: 193 us; the launch traced here: 192 us
  starting transfers between devices  72.1 us (37%)
  matrix products  47.6 us (25%)
  waiting for transfers between devices  38.9 us (20%)
  local copies, waits for them, and re-layouts  20.7 us (11%)
  loops' own time  9.73 us (5%)
  other arithmetic  2.62 us (1%)
    ppermute x8, starting transfers between devices, from_behind(): return lax.ppermute(x, axis, pairs)  72.1 us
    ppermute x8, waiting for transfers between devices, from_behind(): return lax.ppermute(x, axis, pairs)  38.9 us
    sub x8, matrix products, head_group(): expo = jnp.where(allowed[None], jnp.exp(score - largest), jnp.float32(0.0))  29.9 us
    dot_general x8, matrix products, head_group(): jnp.einsum('htk,kd->thd', weight, value_part, preferred_element_type=jnp....  17.7 us
    another operation x1, loops' own time, attend_block(): parts = lax.map(head_group, jnp.arange(KV_HEADS, dtype=jnp.int32))  9.73 us
    dynamic_slice x16, local copies, waits for them, and re-layouts, head_group(): lax.dynamic_slice_in_dim(query_rows, head_index * group_size * HEAD_DIM,...  8.14 us
    unnamed x15, local copies, waits for them, and re-layouts  6.21 us
    dynamic_slice x8, local copies, waits for them, and re-layouts, attend_block(): parts = lax.map(head_group, jnp.arange(KV_HEADS, dtype=jnp.int32))  4.73 us
  transfers between devices with their start and end apart: 8, of which 3 were waited for; matrix products, arithmetic and copies ran while one was open for 2% of the time, Pallas kernels for 0%

commit v1 on v0

v1 whole, which is shorter than its diff:
```python
import jax
import jax.numpy as jnp
from jax import lax
from jax.experimental import pallas as pl
from jax.experimental.pallas import tpu as pltpu
from jax.sharding import PartitionSpec as P

HEADS = 16
KV_HEADS = 8
HEAD_DIM = 128
WINDOW = 1024
NEG = -1e30


def from_behind(x, axis, by):
    peers = lax.axis_size(axis)
    pairs = [(i, i + by) for i in range(peers) if 0 <= i + by < peers]
    return lax.ppermute(x, axis, pairs)


def attend_kernel(valid_ref, q_ref, *refs):
    nblk = (len(refs) - 1) // 2
    k_refs, v_refs, o_ref = refs[:nblk], refs[nblk:2 * nblk], refs[-1]
    tok = q_ref.shape[0]
    row = lax.broadcasted_iota(jnp.int32, (tok, tok), 0)
    col = lax.broadcasted_iota(jnp.int32, (tok, tok), 1)
    group = HEADS // KV_HEADS
    for a in range(group):
        qa = q_ref[:, a * HEAD_DIM:(a + 1) * HEAD_DIM]
        scores = []
        for j in range(nblk):
            s = lax.dot_general(
                qa, k_refs[j][...], (((1,), (1,)), ((), ())),
                preferred_element_type=jnp.float32,
            ) * HEAD_DIM ** (-0.5)
            if j == 0:
                s = jnp.where((col > row) & (valid_ref[0] > 0), s, NEG)
            elif j == nblk - 1:
                s = jnp.where(col <= row, s, NEG)
            else:
                s = jnp.where(valid_ref[j] > 0, s, NEG)
            scores.append(s)
        largest = scores[0].max(axis=1, keepdims=True)
        for s in scores[1:]:
            largest = jnp.maximum(largest, s.max(axis=1, keepdims=True))
        expos = [jnp.exp(s - largest) for s in scores]
        total = expos[0].sum(axis=1, keepdims=True)
        for e in expos[1:]:
            total = total + e.sum(axis=1, keepdims=True)
        inv = 1.0 / total
        out = None
        for j in range(nblk):
            w = (expos[j] * inv).astype(jnp.bfloat16)
            part = jnp.dot(w, v_refs[j][...], preferred_element_type=jnp.float32)
            out = part if out is None else out + part
        o_ref[:, a * HEAD_DIM:(a + 1) * HEAD_DIM] = out.astype(o_ref.dtype)


def attend(valid, queries, k_blocks, v_blocks):
    tok = queries.shape[0]
    group = HEADS // KV_HEADS
    nblk = len(k_blocks)
    kv_spec = pl.BlockSpec((tok, HEAD_DIM), lambda h: (0, h))
    q_spec = pl.BlockSpec((tok, group * HEAD_DIM), lambda h: (0, h))
    flops = 4 * HEADS * tok * tok * nblk * HEAD_DIM
    nbytes = 2 * (2 * queries.size + 2 * nblk * k_blocks[0].size)
    return pl.pallas_call(
        attend_kernel,
        grid=(KV_HEADS,),
        in_specs=[pl.BlockSpec(memory_space=pltpu.SMEM), q_spec]
        + [kv_spec] * (2 * nblk),
        out_specs=q_spec,
        out_shape=jax.ShapeDtypeStruct(queries.shape, queries.dtype),
        cost_estimate=pl.CostEstimate(
            flops=flops, transcendentals=HEADS * tok * tok * nblk, bytes_accessed=nbytes
        ),
    )(valid, queries, *k_blocks, *v_blocks)


def body(queries, keys, values):
    tok_rows = queries.shape[0]
    back_blocks = WINDOW // tok_rows
    block_index = lax.axis_index(("blk", "grp"))
    pieces_k = []
    pieces_v = []
    for offset in range(back_blocks, 0, -1):
        moved_k, moved_v = from_behind((keys, values), ("blk", "grp"), offset)
        pieces_k.append(moved_k)
        pieces_v.append(moved_v)
    nblk = back_blocks + 1
    valid = (block_index + jnp.arange(nblk, dtype=jnp.int32) >= back_blocks).astype(jnp.int32)
    return attend(valid, queries, pieces_k + [keys], pieces_v + [values])


def solution(mesh):
    placed = (P(("blk", "grp"), None), P(("blk", "grp"), None), P(("blk", "grp"), None))
    return jax.shard_map(
        body, mesh=mesh, in_specs=placed, out_specs=P(("blk", "grp"), None), check_vma=False
    )
```

time: 193 us -> 127 us (0.66)
  the two profiles are of different devices: /device:TPU:95 before, /device:TPU:159 now
where the time goes in v1:
time: 127 us
  waiting for transfers between devices  57 us (45%)
  starting transfers between devices  53.6 us (42%)
  Pallas kernels  15.6 us (12%)
    ppermute x8, waiting for transfers between devices, from_behind(): return lax.ppermute(x, axis, pairs)  57 us
    ppermute x8, starting transfers between devices, from_behind(): return lax.ppermute(x, axis, pairs)  53.6 us
    pallas_call x1, Pallas kernels, attend(): pl.pallas_call(attend_kernel, grid=(KV_HEADS,), in_specs=[pl.BlockSpec(me...  15.6 us
  transfers between devices with their start and end apart: 8, of which 3 were waited for; matrix products, arithmetic and copies ran while one was open for 0% of the time, Pallas kernels for 0%

profile of v1, /device:TPU:159, one launch (start us, length us, event | category | flops | bytes accessed | tf_op | source)
XLA Modules:
  0.0 127.0 jit_solution(13725019427573689577)
XLA Ops:
  0.0 5.0 %collective-permute-start.2 = (bf16[256,1024]{1,0:T(8,128)(2,1)}, bf16[256,1024]{1,0:T(8,128)(2,1)S(1)}, u32[]{:S(2)}, u32[]{:S(2)}) collective-permute-start(bf16[256,1024]{1,0:T(8,128)(2,1)} %refs_4_.1), channel_id=1, source_target_pairs={{0,2},{1,3},{2,4},{3,5},{4,6},{5,7},{6,8},{7,9},{8,10},{9,11},{10,... | collective-permute-start | bytes 1572872 | tf_op jit(solution)/shard_map/ppermute | solution.py:18
  5.0 4.2 %collective-permute-start.1 = (bf16[256,1024]{1,0:T(8,128)(2,1)}, bf16[256,1024]{1,0:T(8,128)(2,1)S(1)}, u32[]{:S(2)}, u32[]{:S(2)}) collective-permute-start(bf16[256,1024]{1,0:T(8,128)(2,1)} %refs_4_.1), channel_id=1, source_target_pairs={{0,3},{1,4},{2,5},{3,6},{4,7},{5,8},{6,9},{7,10},{8,11},{9,12},{10... | collective-permute-start | bytes 1572872 | tf_op jit(solution)/shard_map/ppermute | solution.py:18
  9.2 3.5 %collective-permute-start = (bf16[256,1024]{1,0:T(8,128)(2,1)}, bf16[256,1024]{1,0:T(8,128)(2,1)S(1)}, u32[]{:S(2)}, u32[]{:S(2)}) collective-permute-start(bf16[256,1024]{1,0:T(8,128)(2,1)} %refs_4_.1), channel_id=1, source_target_pairs={{0,4},{1,5},{2,6},{3,7},{4,8},{5,9},{6,10},{7,11},{8,12},{9,13},{1... | collective-permute-start | bytes 1572872 | tf_op jit(solution)/shard_map/ppermute | solution.py:18
  12.7 2.3 %collective-permute-start.3 = (bf16[256,1024]{1,0:T(8,128)(2,1)}, bf16[256,1024]{1,0:T(8,128)(2,1)S(1)}, u32[]{:S(2)}, u32[]{:S(2)}) collective-permute-start(bf16[256,1024]{1,0:T(8,128)(2,1)} %refs_4_.1), channel_id=1, source_target_pairs={{0,1},{1,2},{2,3},{3,4},{4,5},{5,6},{6,7},{7,8},{8,9},{9,10},{10,1... | collective-permute-start | bytes 1572872 | tf_op jit(solution)/shard_map/ppermute | solution.py:18
  15.0 3.3 %collective-permute-start.6 = (bf16[256,1024]{1,0:T(8,128)(2,1)}, bf16[256,1024]{1,0:T(8,128)(2,1)S(1)}, u32[]{:S(2)}, u32[]{:S(2)}) collective-permute-start(bf16[256,1024]{1,0:T(8,128)(2,1)} %refs_9_.1), channel_id=1, source_target_pairs={{0,2},{1,3},{2,4},{3,5},{4,6},{5,7},{6,8},{7,9},{8,10},{9,11},{10,... | collective-permute-start | bytes 1572872 | tf_op jit(solution)/shard_map/ppermute | solution.py:18
  18.3 13.4 %collective-permute-done.2.refs_2_ = bf16[256,1024]{1,0:T(8,128)(2,1)S(1)} collective-permute-done((bf16[256,1024]{1,0:T(8,128)(2,1)}, bf16[256,1024]{1,0:T(8,128)(2,1)S(1)}, u32[]{:S(2)}, u32[]{:S(2)}) %collective-permute-start.2) | collective-permute-done | bytes 524320 | tf_op jit(solution)/shard_map/ppermute | solution.py:18
  31.8 0.0 copy-start
  31.8 28.5 %collective-permute-start.5 = (bf16[256,1024]{1,0:T(8,128)(2,1)}, bf16[256,1024]{1,0:T(8,128)(2,1)S(1)}, u32[]{:S(2)}, u32[]{:S(2)}) collective-permute-start(bf16[256,1024]{1,0:T(8,128)(2,1)} %refs_9_.1), channel_id=1, source_target_pairs={{0,3},{1,4},{2,5},{3,6},{4,7},{5,8},{6,9},{7,10},{8,11},{9,12},{10... | collective-permute-start | bytes 1572872 | tf_op jit(solution)/shard_map/ppermute | solution.py:18
  60.3 0.0 collective-permute-done.1.refs_1_
  60.3 0.0 copy-start.1
  60.3 1.9 %collective-permute-start.4 = (bf16[256,1024]{1,0:T(8,128)(2,1)}, bf16[256,1024]{1,0:T(8,128)(2,1)}, u32[]{:S(2)}, u32[]{:S(2)}) collective-permute-start(bf16[256,1024]{1,0:T(8,128)(2,1)} %refs_9_.1), channel_id=1, source_target_pairs={{0,4},{1,5},{2,6},{3,7},{4,8},{5,9},{6,10},{7,11},{8,12},{9,13},{1... | collective-permute-start | bytes 1572872 | tf_op jit(solution)/shard_map/ppermute | solution.py:18
  62.2 0.0 collective-permute-done.refs_0_
  62.2 0.0 copy-start.2
  62.2 4.9 %collective-permute-start.7 = (bf16[256,1024]{1,0:T(8,128)(2,1)}, bf16[256,1024]{1,0:T(8,128)(2,1)}, u32[]{:S(2)}, u32[]{:S(2)}) collective-permute-start(bf16[256,1024]{1,0:T(8,128)(2,1)} %refs_9_.1), channel_id=1, source_target_pairs={{0,1},{1,2},{2,3},{3,4},{4,5},{5,6},{6,7},{7,8},{8,9},{9,10},{10,1... | collective-permute-start | bytes 1572872 | tf_op jit(solution)/shard_map/ppermute | solution.py:18
  67.1 0.6 compare_convert_fusion.valid_ref
  67.7 19.7 %collective-permute-done.3.refs_3_ = bf16[256,1024]{1,0:T(8,128)(2,1)S(1)} collective-permute-done((bf16[256,1024]{1,0:T(8,128)(2,1)}, bf16[256,1024]{1,0:T(8,128)(2,1)S(1)}, u32[]{:S(2)}, u32[]{:S(2)}) %collective-permute-start.3) | collective-permute-done | bytes 524320 | tf_op jit(solution)/shard_map/ppermute | solution.py:18
  87.4 0.0 copy-start.3
  87.4 0.0 collective-permute-done.6.refs_7_
  87.5 0.0 copy-start.4
  87.5 0.0 collective-permute-done.5.refs_6_
  87.5 0.0 copy-start.5
  87.5 0.0 collective-permute-done.4.refs_5_
  87.5 23.9 %collective-permute-done.7.refs_8_ = bf16[256,1024]{1,0:T(8,128)(2,1)} collective-permute-done((bf16[256,1024]{1,0:T(8,128)(2,1)}, bf16[256,1024]{1,0:T(8,128)(2,1)}, u32[]{:S(2)}, u32[]{:S(2)}) %collective-permute-start.7) | collective-permute-done | bytes 524320 | tf_op jit(solution)/shard_map/ppermute | solution.py:18
  111.4 0.0 copy-done
  111.4 0.0 copy-done.1
  111.4 0.0 copy-done.2
  111.4 0.0 copy-done.3
  111.4 0.0 copy-done.4
  111.4 0.0 copy-done.5
  111.4 15.6 %shard_map.37 = bf16[256,2048]{1,0:T(8,128)(2,1)} custom-call(s32[5]{0:T(128)} %compare_convert_fusion.valid_ref, bf16[256,2048]{1,0:T(8,128)(2,1)} %q_ref.1, bf16[256,1024]{1,0:T(8,128)(2,1)} %copy-done.2, bf16[256,1024]{1,0:T(8,128)(2,1)} %copy-done.1, bf16[256,1024]{1,0:T(8,128)(2,1)} %copy-done, bf16[256,1024]{1,0:T(8,128)(2,1)} %copy-done.3, ...), custom_call_target="tpu_custom_call" | custom-call | flops 2684354560 | bytes 7340032 | tf_op jit(solution)/shard_map/pallas_call | solution.py:67
Async XLA Ops:
  0.0 31.8 %collective-permute-start.2 = (bf16[256,1024]{1,0:T(8,128)(2,1)}, bf16[256,1024]{1,0:T(8,128)(2,1)S(1)}, u32[]{:S(2)}, u32[]{:S(2)}) collective-permute-start(bf16[256,1024]{1,0:T(8,128)(2,1)} %refs_4_.1), channel_id=1, source_target_pairs={{0,2},{1,3},{2,4},{3,5},{4,6},{5,7},{6,8},{7,9},{8,10},{9,11},{10,... | collective-permute-start | bytes 1572872 | tf_op jit(solution)/shard_map/ppermute | solution.py:18
  5.0 55.3 %collective-permute-start.1 = (bf16[256,1024]{1,0:T(8,128)(2,1)}, bf16[256,1024]{1,0:T(8,128)(2,1)S(1)}, u32[]{:S(2)}, u32[]{:S(2)}) collective-permute-start(bf16[256,1024]{1,0:T(8,128)(2,1)} %refs_4_.1), channel_id=1, source_target_pairs={{0,3},{1,4},{2,5},{3,6},{4,7},{5,8},{6,9},{7,10},{8,11},{9,12},{10... | collective-permute-start | bytes 1572872 | tf_op jit(solution)/shard_map/ppermute | solution.py:18
  9.2 53.0 %collective-permute-start = (bf16[256,1024]{1,0:T(8,128)(2,1)}, bf16[256,1024]{1,0:T(8,128)(2,1)S(1)}, u32[]{:S(2)}, u32[]{:S(2)}) collective-permute-start(bf16[256,1024]{1,0:T(8,128)(2,1)} %refs_4_.1), channel_id=1, source_target_pairs={{0,4},{1,5},{2,6},{3,7},{4,8},{5,9},{6,10},{7,11},{8,12},{9,13},{1... | collective-permute-start | bytes 1572872 | tf_op jit(solution)/shard_map/ppermute | solution.py:18
  12.7 74.8 %collective-permute-start.3 = (bf16[256,1024]{1,0:T(8,128)(2,1)}, bf16[256,1024]{1,0:T(8,128)(2,1)S(1)}, u32[]{:S(2)}, u32[]{:S(2)}) collective-permute-start(bf16[256,1024]{1,0:T(8,128)(2,1)} %refs_4_.1), channel_id=1, source_target_pairs={{0,1},{1,2},{2,3},{3,4},{4,5},{5,6},{6,7},{7,8},{8,9},{9,10},{10,1... | collective-permute-start | bytes 1572872 | tf_op jit(solution)/shard_map/ppermute | solution.py:18
  15.0 72.5 %collective-permute-start.6 = (bf16[256,1024]{1,0:T(8,128)(2,1)}, bf16[256,1024]{1,0:T(8,128)(2,1)S(1)}, u32[]{:S(2)}, u32[]{:S(2)}) collective-permute-start(bf16[256,1024]{1,0:T(8,128)(2,1)} %refs_9_.1), channel_id=1, source_target_pairs={{0,2},{1,3},{2,4},{3,5},{4,6},{5,7},{6,8},{7,9},{8,10},{9,11},{10,... | collective-permute-start | bytes 1572872 | tf_op jit(solution)/shard_map/ppermute | solution.py:18
  31.8 79.6 %copy-start = (bf16[256,1024]{1,0:T(8,128)(2,1)}, bf16[256,1024]{1,0:T(8,128)(2,1)S(1)}, u32[]{:S(2)}) copy-start(bf16[256,1024]{1,0:T(8,128)(2,1)S(1)} %collective-permute-done.2.refs_2_) | copy-start | bytes 1572868
  31.8 55.7 %collective-permute-start.5 = (bf16[256,1024]{1,0:T(8,128)(2,1)}, bf16[256,1024]{1,0:T(8,128)(2,1)S(1)}, u32[]{:S(2)}, u32[]{:S(2)}) collective-permute-start(bf16[256,1024]{1,0:T(8,128)(2,1)} %refs_9_.1), channel_id=1, source_target_pairs={{0,3},{1,4},{2,5},{3,6},{4,7},{5,8},{6,9},{7,10},{8,11},{9,12},{10... | collective-permute-start | bytes 1572872 | tf_op jit(solution)/shard_map/ppermute | solution.py:18
  60.3 51.1 %copy-start.1 = (bf16[256,1024]{1,0:T(8,128)(2,1)}, bf16[256,1024]{1,0:T(8,128)(2,1)S(1)}, u32[]{:S(2)}) copy-start(bf16[256,1024]{1,0:T(8,128)(2,1)S(1)} %collective-permute-done.1.refs_1_) | copy-start | bytes 1572868
  60.3 27.2 %collective-permute-start.4 = (bf16[256,1024]{1,0:T(8,128)(2,1)}, bf16[256,1024]{1,0:T(8,128)(2,1)}, u32[]{:S(2)}, u32[]{:S(2)}) collective-permute-start(bf16[256,1024]{1,0:T(8,128)(2,1)} %refs_9_.1), channel_id=1, source_target_pairs={{0,4},{1,5},{2,6},{3,7},{4,8},{5,9},{6,10},{7,11},{8,12},{9,13},{1... | collective-permute-start | bytes 1572872 | tf_op jit(solution)/shard_map/ppermute | solution.py:18
  62.2 49.1 %copy-start.2 = (bf16[256,1024]{1,0:T(8,128)(2,1)}, bf16[256,1024]{1,0:T(8,128)(2,1)S(1)}, u32[]{:S(2)}) copy-start(bf16[256,1024]{1,0:T(8,128)(2,1)S(1)} %collective-permute-done.refs_0_) | copy-start | bytes 1572868
  62.2 49.1 %collective-permute-start.7 = (bf16[256,1024]{1,0:T(8,128)(2,1)}, bf16[256,1024]{1,0:T(8,128)(2,1)}, u32[]{:S(2)}, u32[]{:S(2)}) collective-permute-start(bf16[256,1024]{1,0:T(8,128)(2,1)} %refs_9_.1), channel_id=1, source_target_pairs={{0,1},{1,2},{2,3},{3,4},{4,5},{5,6},{6,7},{7,8},{8,9},{9,10},{10,1... | collective-permute-start | bytes 1572872 | tf_op jit(solution)/shard_map/ppermute | solution.py:18
  87.4 23.9 %copy-start.3 = (bf16[256,1024]{1,0:T(8,128)(2,1)}, bf16[256,1024]{1,0:T(8,128)(2,1)S(1)}, u32[]{:S(2)}) copy-start(bf16[256,1024]{1,0:T(8,128)(2,1)S(1)} %collective-permute-done.3.refs_3_) | copy-start | bytes 1572868
  87.5 23.9 %copy-start.4 = (bf16[256,1024]{1,0:T(8,128)(2,1)}, bf16[256,1024]{1,0:T(8,128)(2,1)S(1)}, u32[]{:S(2)}) copy-start(bf16[256,1024]{1,0:T(8,128)(2,1)S(1)} %collective-permute-done.6.refs_7_) | copy-start | bytes 1572868
  87.5 23.9 %copy-start.5 = (bf16[256,1024]{1,0:T(8,128)(2,1)}, bf16[256,1024]{1,0:T(8,128)(2,1)S(1)}, u32[]{:S(2)}) copy-start(bf16[256,1024]{1,0:T(8,128)(2,1)S(1)} %collective-permute-done.5.refs_6_) | copy-start | bytes 1572868

commit v2 on v1

--- a/solution.py
+++ b/solution.py
@@ -77,19 +77,30 @@
     )(valid, queries, *k_blocks, *v_blocks)
 
 
+def shifted(x, axis, pairs):
+    return lax.ppermute(x, axis, pairs)
+
+
 def body(queries, keys, values):
-    tok_rows = queries.shape[0]
-    back_blocks = WINDOW // tok_rows
-    block_index = lax.axis_index(("blk", "grp"))
-    pieces_k = []
-    pieces_v = []
-    for offset in range(back_blocks, 0, -1):
-        moved_k, moved_v = from_behind((keys, values), ("blk", "grp"), offset)
-        pieces_k.append(moved_k)
-        pieces_v.append(moved_v)
+    axis = ("blk", "grp")
+    n = lax.axis_size(axis)
+    block_index = lax.axis_index(axis)
+    own = (keys, values)
+    ahead2 = [(i, i + 2) for i in range(n) if i + 2 < n]
+    x1 = shifted(own, axis, ahead2)
+    y1 = shifted(own, axis, [(i, i + 1) for i in range(0, n, 2)])
+    x2 = shifted(x1, axis, ahead2)
+    y2 = shifted(x1, axis, [(i, i ^ 1) for i in range(n)])
+    y3 = shifted(x2, axis, [(i, i - 1) for i in range(1, n, 2)])
+    odd = (block_index % 2) == 1
+    b1 = [jnp.where(odd, a, b) for a, b in zip(y1, y2)]
+    b3 = [jnp.where(odd, a, b) for a, b in zip(y2, y3)]
+    back_blocks = WINDOW // queries.shape[0]
     nblk = back_blocks + 1
     valid = (block_index + jnp.arange(nblk, dtype=jnp.int32) >= back_blocks).astype(jnp.int32)
-    return attend(valid, queries, pieces_k + [keys], pieces_v + [values])
+    k_blocks = [x2[0], b3[0], x1[0], b1[0], keys]
+    v_blocks = [x2[1], b3[1], x1[1], b1[1], values]
+    return attend(valid, queries, k_blocks, v_blocks)
 
 
 def solution(mesh):

time: 127 us -> 116 us (0.913)
  the two profiles are of different devices: /device:TPU:159 before, /device:TPU:207 now
where the time goes in v2:
time: 116 us; the launch traced here: 115 us
  starting transfers between devices  50.9 us (44%)
  waiting for transfers between devices  46.1 us (40%)
  Pallas kernels  15.5 us (13%)
  other arithmetic  2.7 us (2%)
    ppermute x10, starting transfers between devices, shifted(): return lax.ppermute(x, axis, pairs)  50.9 us
    ppermute x10, waiting for transfers between devices, shifted(): return lax.ppermute(x, axis, pairs)  46.1 us
    pallas_call x1, Pallas kernels, attend(): pl.pallas_call(attend_kernel, grid=(KV_HEADS,), in_specs=[pl.BlockSpec(me...  15.5 us
  transfers between devices with their start and end apart: 10, of which 6 were waited for; matrix products, arithmetic and copies ran while one was open for 1% of the time, Pallas kernels for 0%

profile of v2, /device:TPU:207, one launch (start us, length us, event | category | flops | bytes accessed | tf_op | source)
XLA Modules:
  0.0 115.4 jit_solution(4974078049374609158)
XLA Ops:
  0.0 4.7 %collective-permute-start = (bf16[256,1024]{1,0:T(8,128)(2,1)}, bf16[256,1024]{1,0:T(8,128)(2,1)}, u32[]{:S(2)}, u32[]{:S(2)}) collective-permute-start(bf16[256,1024]{1,0:T(8,128)(2,1)} %refs_4_.1), channel_id=1, source_target_pairs={{0,2},{1,3},{2,4},{3,5},{4,6},{5,7},{6,8},{7,9},{8,10},{9,11},{10,... | collective-permute-start | bytes 1572872 | tf_op jit(solution)/shard_map/ppermute | solution.py:81
  4.7 3.4 %collective-permute-start.5 = (bf16[256,1024]{1,0:T(8,128)(2,1)}, bf16[256,1024]{1,0:T(8,128)(2,1)}, u32[]{:S(2)}, u32[]{:S(2)}) collective-permute-start(bf16[256,1024]{1,0:T(8,128)(2,1)} %refs_9_.1), channel_id=1, source_target_pairs={{0,2},{1,3},{2,4},{3,5},{4,6},{5,7},{6,8},{7,9},{8,10},{9,11},{10,... | collective-permute-start | bytes 1572872 | tf_op jit(solution)/shard_map/ppermute | solution.py:81
  8.1 14.3 %collective-permute-done.refs_2_ = bf16[256,1024]{1,0:T(8,128)(2,1)} collective-permute-done((bf16[256,1024]{1,0:T(8,128)(2,1)}, bf16[256,1024]{1,0:T(8,128)(2,1)}, u32[]{:S(2)}, u32[]{:S(2)}) %collective-permute-start) | collective-permute-done | bytes 524320 | tf_op jit(solution)/shard_map/ppermute | solution.py:81
  22.4 7.4 %collective-permute-start.1 = (bf16[256,1024]{1,0:T(8,128)(2,1)}, bf16[256,1024]{1,0:T(8,128)(2,1)}, u32[]{:S(2)}, u32[]{:S(2)}) collective-permute-start(bf16[256,1024]{1,0:T(8,128)(2,1)} %collective-permute-done.refs_2_), channel_id=1, source_target_pairs={{0,2},{1,3},{2,4},{3,5},{4,6},{5,7},{6,8},{7,9},{8,10},{9,11},{10,... | collective-permute-start | bytes 1572872 | tf_op jit(solution)/shard_map/ppermute | solution.py:81
  29.8 1.3 %collective-permute-start.4 = (bf16[256,1024]{1,0:T(8,128)(2,1)}, bf16[256,1024]{1,0:T(8,128)(2,1)S(1)}, u32[]{:S(2)}, u32[]{:S(2)}) collective-permute-start(bf16[256,1024]{1,0:T(8,128)(2,1)} %refs_4_.1), channel_id=1, source_target_pairs={{0,1},{2,3},{4,5},{6,7},{8,9},{10,11},{12,13},{14,15},{16,17},{18,... | collective-permute-start | bytes 1572872 | tf_op jit(solution)/shard_map/ppermute | solution.py:81
  31.1 0.0 collective-permute-done.5.refs_7_
  31.1 5.4 %collective-permute-start.6 = (bf16[256,1024]{1,0:T(8,128)(2,1)}, bf16[256,1024]{1,0:T(8,128)(2,1)}, u32[]{:S(2)}, u32[]{:S(2)}) collective-permute-start(bf16[256,1024]{1,0:T(8,128)(2,1)} %collective-permute-done.5.refs_7_), channel_id=1, source_target_pairs={{0,2},{1,3},{2,4},{3,5},{4,6},{5,7},{6,8},{7,9},{8,10},{9,11},{10,... | collective-permute-start | bytes 1572872 | tf_op jit(solution)/shard_map/ppermute | solution.py:81
  36.6 1.9 %collective-permute-start.2 = (bf16[256,1024]{1,0:T(8,128)(2,1)}, bf16[256,1024]{1,0:T(8,128)(2,1)S(1)}, u32[]{:S(2)}, u32[]{:S(2)}) collective-permute-start(bf16[256,1024]{1,0:T(8,128)(2,1)} %collective-permute-done.refs_2_), channel_id=1, source_target_pairs={{0,1},{1,0},{2,3},{3,2},{4,5},{5,4},{6,7},{7,6},{8,9},{9,8},{10,11... | collective-permute-start | bytes 1572872 | tf_op jit(solution)/shard_map/ppermute | solution.py:81
  38.5 0.4 collective-permute-done.1.refs_0_
  38.9 13.0 %collective-permute-start.3 = (bf16[256,1024]{1,0:T(8,128)(2,1)}, bf16[256,1024]{1,0:T(8,128)(2,1)S(1)}, u32[]{:S(2)}, u32[]{:S(2)}) collective-permute-start(bf16[256,1024]{1,0:T(8,128)(2,1)} %collective-permute-done.1.refs_0_), channel_id=1, source_target_pairs={{1,0},{3,2},{5,4},{7,6},{9,8},{11,10},{13,12},{15,14},{17,16},{19,... | collective-permute-start | bytes 1572872 | tf_op jit(solution)/shard_map/ppermute | solution.py:81
  51.8 1.3 %collective-permute-start.9 = (bf16[256,1024]{1,0:T(8,128)(2,1)}, bf16[256,1024]{1,0:T(8,128)(2,1)S(1)}, u32[]{:S(2)}, u32[]{:S(2)}) collective-permute-start(bf16[256,1024]{1,0:T(8,128)(2,1)} %refs_9_.1), channel_id=1, source_target_pairs={{0,1},{2,3},{4,5},{6,7},{8,9},{10,11},{12,13},{14,15},{16,17},{18,... | collective-permute-start | bytes 1572872 | tf_op jit(solution)/shard_map/ppermute | solution.py:81
  53.1 11.4 %collective-permute-done.4 = bf16[256,1024]{1,0:T(8,128)(2,1)S(1)} collective-permute-done((bf16[256,1024]{1,0:T(8,128)(2,1)}, bf16[256,1024]{1,0:T(8,128)(2,1)S(1)}, u32[]{:S(2)}, u32[]{:S(2)}) %collective-permute-start.4) | collective-permute-done | bytes 524320 | tf_op jit(solution)/shard_map/ppermute | solution.py:81
  64.5 1.9 %collective-permute-start.7 = (bf16[256,1024]{1,0:T(8,128)(2,1)}, bf16[256,1024]{1,0:T(8,128)(2,1)S(1)}, u32[]{:S(2)}, u32[]{:S(2)}) collective-permute-start(bf16[256,1024]{1,0:T(8,128)(2,1)} %collective-permute-done.5.refs_7_), channel_id=1, source_target_pairs={{0,1},{1,0},{2,3},{3,2},{4,5},{5,4},{6,7},{7,6},{8,9},{9,8},{10,11... | collective-permute-start | bytes 1572872 | tf_op jit(solution)/shard_map/ppermute | solution.py:81
  66.5 0.0 collective-permute-done.6.refs_5_
  66.5 10.6 %collective-permute-start.8 = (bf16[256,1024]{1,0:T(8,128)(2,1)}, bf16[256,1024]{1,0:T(8,128)(2,1)S(1)}, u32[]{:S(2)}, u32[]{:S(2)}) collective-permute-start(bf16[256,1024]{1,0:T(8,128)(2,1)} %collective-permute-done.6.refs_5_), channel_id=1, source_target_pairs={{1,0},{3,2},{5,4},{7,6},{9,8},{11,10},{13,12},{15,14},{17,16},{19,... | collective-permute-start | bytes 1572872 | tf_op jit(solution)/shard_map/ppermute | solution.py:81
  77.1 0.5 compare_convert_fusion.valid_ref
  77.6 9.4 %collective-permute-done.2 = bf16[256,1024]{1,0:T(8,128)(2,1)S(1)} collective-permute-done((bf16[256,1024]{1,0:T(8,128)(2,1)}, bf16[256,1024]{1,0:T(8,128)(2,1)S(1)}, u32[]{:S(2)}, u32[]{:S(2)}) %collective-permute-start.2) | collective-permute-done | bytes 524320 | tf_op jit(solution)/shard_map/ppermute | solution.py:81
  87.0 0.0 collective-permute-done.3
  87.0 1.1 broadcast_select_fusion.2
  88.1 5.0 %collective-permute-done.9 = bf16[256,1024]{1,0:T(8,128)(2,1)S(1)} collective-permute-done((bf16[256,1024]{1,0:T(8,128)(2,1)}, bf16[256,1024]{1,0:T(8,128)(2,1)S(1)}, u32[]{:S(2)}, u32[]{:S(2)}) %collective-permute-start.9) | collective-permute-done | bytes 524320 | tf_op jit(solution)/shard_map/ppermute | solution.py:81
  93.1 5.6 %collective-permute-done.7 = bf16[256,1024]{1,0:T(8,128)(2,1)S(1)} collective-permute-done((bf16[256,1024]{1,0:T(8,128)(2,1)}, bf16[256,1024]{1,0:T(8,128)(2,1)S(1)}, u32[]{:S(2)}, u32[]{:S(2)}) %collective-permute-start.7) | collective-permute-done | bytes 524320 | tf_op jit(solution)/shard_map/ppermute | solution.py:81
  98.8 0.0 collective-permute-done.8
  98.8 1.1 broadcast_select_fusion
  99.8 15.5 %shard_map.37 = bf16[256,2048]{1,0:T(8,128)(2,1)} custom-call(s32[5]{0:T(128)} %compare_convert_fusion.valid_ref, bf16[256,2048]{1,0:T(8,128)(2,1)} %q_ref.1, bf16[256,1024]{1,0:T(8,128)(2,1)} %collective-permute-done.1.refs_0_, bf16[256,1024]{1,0:T(8,128)(2,1)} %get-tuple-element.8.refs_1_, bf16[256,1024]{1,0:T(8,128)(2,1)} %collective-permute-done.refs_2_, ...), custom_call_target="tpu_custom_call" | custom-call | flops 2684354560 | bytes 7340032 | tf_op jit(solution)/shard_map/pallas_call | solution.py:67
Async XLA Ops:
  0.0 22.4 %collective-permute-start = (bf16[256,1024]{1,0:T(8,128)(2,1)}, bf16[256,1024]{1,0:T(8,128)(2,1)}, u32[]{:S(2)}, u32[]{:S(2)}) collective-permute-start(bf16[256,1024]{1,0:T(8,128)(2,1)} %refs_4_.1), channel_id=1, source_target_pairs={{0,2},{1,3},{2,4},{3,5},{4,6},{5,7},{6,8},{7,9},{8,10},{9,11},{10,... | collective-permute-start | bytes 1572872 | tf_op jit(solution)/shard_map/ppermute | solution.py:81
  4.7 26.4 %collective-permute-start.5 = (bf16[256,1024]{1,0:T(8,128)(2,1)}, bf16[256,1024]{1,0:T(8,128)(2,1)}, u32[]{:S(2)}, u32[]{:S(2)}) collective-permute-start(bf16[256,1024]{1,0:T(8,128)(2,1)} %refs_9_.1), channel_id=1, source_target_pairs={{0,2},{1,3},{2,4},{3,5},{4,6},{5,7},{6,8},{7,9},{8,10},{9,11},{10,... | collective-permute-start | bytes 1572872 | tf_op jit(solution)/shard_map/ppermute | solution.py:81
  22.4 16.5 %collective-permute-start.1 = (bf16[256,1024]{1,0:T(8,128)(2,1)}, bf16[256,1024]{1,0:T(8,128)(2,1)}, u32[]{:S(2)}, u32[]{:S(2)}) collective-permute-start(bf16[256,1024]{1,0:T(8,128)(2,1)} %collective-permute-done.refs_2_), channel_id=1, source_target_pairs={{0,2},{1,3},{2,4},{3,5},{4,6},{5,7},{6,8},{7,9},{8,10},{9,11},{10,... | collective-permute-start | bytes 1572872 | tf_op jit(solution)/shard_map/ppermute | solution.py:81
  29.8 34.7 %collective-permute-start.4 = (bf16[256,1024]{1,0:T(8,128)(2,1)}, bf16[256,1024]{1,0:T(8,128)(2,1)S(1)}, u32[]{:S(2)}, u32[]{:S(2)}) collective-permute-start(bf16[256,1024]{1,0:T(8,128)(2,1)} %refs_4_.1), channel_id=1, source_target_pairs={{0,1},{2,3},{4,5},{6,7},{8,9},{10,11},{12,13},{14,15},{16,17},{18,... | collective-permute-start | bytes 1572872 | tf_op jit(solution)/shard_map/ppermute | solution.py:81
  31.1 35.3 %collective-permute-start.6 = (bf16[256,1024]{1,0:T(8,128)(2,1)}, bf16[256,1024]{1,0:T(8,128)(2,1)}, u32[]{:S(2)}, u32[]{:S(2)}) collective-permute-start(bf16[256,1024]{1,0:T(8,128)(2,1)} %collective-permute-done.5.refs_7_), channel_id=1, source_target_pairs={{0,2},{1,3},{2,4},{3,5},{4,6},{5,7},{6,8},{7,9},{8,10},{9,11},{10,... | collective-permute-start | bytes 1572872 | tf_op jit(solution)/shard_map/ppermute | solution.py:81
  36.6 50.4 %collective-permute-start.2 = (bf16[256,1024]{1,0:T(8,128)(2,1)}, bf16[256,1024]{1,0:T(8,128)(2,1)S(1)}, u32[]{:S(2)}, u32[]{:S(2)}) collective-permute-start(bf16[256,1024]{1,0:T(8,128)(2,1)} %collective-permute-done.refs_2_), channel_id=1, source_target_pairs={{0,1},{1,0},{2,3},{3,2},{4,5},{5,4},{6,7},{7,6},{8,9},{9,8},{10,11... | collective-permute-start | bytes 1572872 | tf_op jit(solution)/shard_map/ppermute | solution.py:81
  38.9 48.1 %collective-permute-start.3 = (bf16[256,1024]{1,0:T(8,128)(2,1)}, bf16[256,1024]{1,0:T(8,128)(2,1)S(1)}, u32[]{:S(2)}, u32[]{:S(2)}) collective-permute-start(bf16[256,1024]{1,0:T(8,128)(2,1)} %collective-permute-done.1.refs_0_), channel_id=1, source_target_pairs={{1,0},{3,2},{5,4},{7,6},{9,8},{11,10},{13,12},{15,14},{17,16},{19,... | collective-permute-start | bytes 1572872 | tf_op jit(solution)/shard_map/ppermute | solution.py:81
  51.8 41.3 %collective-permute-start.9 = (bf16[256,1024]{1,0:T(8,128)(2,1)}, bf16[256,1024]{1,0:T(8,128)(2,1)S(1)}, u32[]{:S(2)}, u32[]{:S(2)}) collective-permute-start(bf16[256,1024]{1,0:T(8,128)(2,1)} %refs_9_.1), channel_id=1, source_target_pairs={{0,1},{2,3},{4,5},{6,7},{8,9},{10,11},{12,13},{14,15},{16,17},{18,... | collective-permute-start | bytes 1572872 | tf_op jit(solution)/shard_map/ppermute | solution.py:81
  64.5 34.2 %collective-permute-start.7 = (bf16[256,1024]{1,0:T(8,128)(2,1)}, bf16[256,1024]{1,0:T(8,128)(2,1)S(1)}, u32[]{:S(2)}, u32[]{:S(2)}) collective-permute-start(bf16[256,1024]{1,0:T(8,128)(2,1)} %collective-permute-done.5.refs_7_), channel_id=1, source_target_pairs={{0,1},{1,0},{2,3},{3,2},{4,5},{5,4},{6,7},{7,6},{8,9},{9,8},{10,11... | collective-permute-start | bytes 1572872 | tf_op jit(solution)/shard_map/ppermute | solution.py:81
  66.5 32.3 %collective-permute-start.8 = (bf16[256,1024]{1,0:T(8,128)(2,1)}, bf16[256,1024]{1,0:T(8,128)(2,1)S(1)}, u32[]{:S(2)}, u32[]{:S(2)}) collective-permute-start(bf16[256,1024]{1,0:T(8,128)(2,1)} %collective-permute-done.6.refs_5_), channel_id=1, source_target_pairs={{1,0},{3,2},{5,4},{7,6},{9,8},{11,10},{13,12},{15,14},{17,16},{19,... | collective-permute-start | bytes 1572872 | tf_op jit(solution)/shard_map/ppermute | solution.py:81

commit v3 on v2

--- a/solution.py
+++ b/solution.py
@@ -60,21 +60,26 @@
     tok = queries.shape[0]
     group = HEADS // KV_HEADS
     nblk = len(k_blocks)
-    kv_spec = pl.BlockSpec((tok, HEAD_DIM), lambda h: (0, h))
+    k_spec = pl.BlockSpec((tok, HEAD_DIM), lambda h: (0, h))
+    v_spec = pl.BlockSpec((tok, HEAD_DIM), lambda h: (0, KV_HEADS + h))
     q_spec = pl.BlockSpec((tok, group * HEAD_DIM), lambda h: (0, h))
     flops = 4 * HEADS * tok * tok * nblk * HEAD_DIM
-    nbytes = 2 * (2 * queries.size + 2 * nblk * k_blocks[0].size)
+    nbytes = 2 * (2 * queries.size + nblk * k_blocks[0].size)
     return pl.pallas_call(
         attend_kernel,
         grid=(KV_HEADS,),
         in_specs=[pl.BlockSpec(memory_space=pltpu.SMEM), q_spec]
-        + [kv_spec] * (2 * nblk),
+        + [k_spec] * nblk + [v_spec] * nblk,
         out_specs=q_spec,
         out_shape=jax.ShapeDtypeStruct(queries.shape, queries.dtype),
         cost_estimate=pl.CostEstimate(
             flops=flops, transcendentals=HEADS * tok * tok * nblk, bytes_accessed=nbytes
         ),
     )(valid, queries, *k_blocks, *v_blocks)
+
+
+def attend_kv(valid, queries, kv_blocks):
+    return attend(valid, queries, kv_blocks, kv_blocks)
 
 
 def shifted(x, axis, pairs):
@@ -85,7 +90,7 @@
     axis = ("blk", "grp")
     n = lax.axis_size(axis)
     block_index = lax.axis_index(axis)
-    own = (keys, values)
+    own = jnp.concatenate([keys, values], axis=1)
     ahead2 = [(i, i + 2) for i in range(n) if i + 2 < n]
     x1 = shifted(own, axis, ahead2)
     y1 = shifted(own, axis, [(i, i + 1) for i in range(0, n, 2)])
@@ -93,14 +98,12 @@
     y2 = shifted(x1, axis, [(i, i ^ 1) for i in range(n)])
     y3 = shifted(x2, axis, [(i, i - 1) for i in range(1, n, 2)])
     odd = (block_index % 2) == 1
-    b1 = [jnp.where(odd, a, b) for a, b in zip(y1, y2)]
-    b3 = [jnp.where(odd, a, b) for a, b in zip(y2, y3)]
+    b1 = jnp.where(odd, y1, y2)
+    b3 = jnp.where(odd, y2, y3)
     back_blocks = WINDOW // queries.shape[0]
     nblk = back_blocks + 1
     valid = (block_index + jnp.arange(nblk, dtype=jnp.int32) >= back_blocks).astype(jnp.int32)
-    k_blocks = [x2[0], b3[0], x1[0], b1[0], keys]
-    v_blocks = [x2[1], b3[1], x1[1], b1[1], values]
-    return attend(valid, queries, k_blocks, v_blocks)
+    return attend_kv(valid, queries, [x2, b3, x1, b1, own])
 
 
 def solution(mesh):

time: 116 us -> 122 us (1.052)
  the two profiles are of different devices: /device:TPU:207 before, /device:TPU:255 now
where the time goes in v3:
time: 122 us
  waiting for transfers between devices  60 us (49%)
  starting transfers between devices  41.6 us (34%)
  Pallas kernels  15.6 us (13%)
  other arithmetic  3.64 us (3%)
  local copies, waits for them, and re-layouts  1.24 us (1%)
    ppermute x5, waiting for transfers between devices, shifted(): return lax.ppermute(x, axis, pairs)  60 us
    ppermute x5, starting transfers between devices, shifted(): return lax.ppermute(x, axis, pairs)  41.6 us
    pallas_call x1, Pallas kernels, attend(): pl.pallas_call(attend_kernel, grid=(KV_HEADS,), in_specs=[pl.BlockSpec(me...  15.6 us
    select_n x1, other arithmetic, body(): b1 = jnp.where(odd, y1, y2)  3.05 us
  transfers between devices with their start and end apart: 5, of which 4 were waited for; matrix products, arithmetic and copies ran while one was open for 0% of the time, Pallas kernels for 0%

profile of v3, /device:TPU:255, one launch (start us, length us, event | category | flops | bytes accessed | tf_op | source)
XLA Modules:
  0.0 122.1 jit_solution(3976209958565526391)
XLA Ops:
  0.0 0.0 copy-start.3
  0.0 1.1 constant_dynamic-update-slice_fusion.1
  1.1 0.1 copy-done.3
  1.2 0.0 copy-start
  1.3 5.9 %collective-permute-start = (bf16[256,2048]{1,0:T(8,128)(2,1)S(1)}, bf16[256,2048]{1,0:T(8,128)(2,1)S(1)}, u32[]{:S(2)}, u32[]{:S(2)}) collective-permute-start(bf16[256,2048]{1,0:T(8,128)(2,1)S(1)} %constant_dynamic-update-slice_fusion.refs_4_.refs_9_), channel_id=1, source_target_pairs={{0,2},{1,3},{2,4},{3,5},{4,6},{5,7},{6,8},{7,9},{8,10},{9,11},{10,... | collective-permute-start | bytes 3145736 | tf_op jit(solution)/shard_map/ppermute | solution.py:86
  7.2 22.8 %collective-permute-done.refs_2_.refs_7_ = bf16[256,2048]{1,0:T(8,128)(2,1)S(1)} collective-permute-done((bf16[256,2048]{1,0:T(8,128)(2,1)S(1)}, bf16[256,2048]{1,0:T(8,128)(2,1)S(1)}, u32[]{:S(2)}, u32[]{:S(2)}) %collective-permute-start) | collective-permute-done | bytes 1048608 | tf_op jit(solution)/shard_map/ppermute | solution.py:86
  30.0 0.0 copy-start.1
  30.0 10.8 %collective-permute-start.1 = (bf16[256,2048]{1,0:T(8,128)(2,1)S(1)}, bf16[256,2048]{1,0:T(8,128)(2,1)S(1)}, u32[]{:S(2)}, u32[]{:S(2)}) collective-permute-start(bf16[256,2048]{1,0:T(8,128)(2,1)S(1)} %collective-permute-done.refs_2_.refs_7_), channel_id=1, source_target_pairs={{0,2},{1,3},{2,4},{3,5},{4,6},{5,7},{6,8},{7,9},{8,10},{9,11},{10,... | collective-permute-start | bytes 3145736 | tf_op jit(solution)/shard_map/ppermute | solution.py:86
  40.8 1.3 %collective-permute-start.4 = (bf16[256,2048]{1,0:T(8,128)(2,1)S(1)}, bf16[256,2048]{1,0:T(8,128)(2,1)}, u32[]{:S(2)}, u32[]{:S(2)}) collective-permute-start(bf16[256,2048]{1,0:T(8,128)(2,1)S(1)} %constant_dynamic-update-slice_fusion.refs_4_.refs_9_), channel_id=1, source_target_pairs={{0,1},{2,3},{4,5},{6,7},{8,9},{10,11},{12,13},{14,15},{16,17},{18,... | collective-permute-start | bytes 3145736 | tf_op jit(solution)/shard_map/ppermute | solution.py:86
  42.1 5.0 %collective-permute-start.2 = (bf16[256,2048]{1,0:T(8,128)(2,1)S(1)}, bf16[256,2048]{1,0:T(8,128)(2,1)}, u32[]{:S(2)}, u32[]{:S(2)}) collective-permute-start(bf16[256,2048]{1,0:T(8,128)(2,1)S(1)} %collective-permute-done.refs_2_.refs_7_), channel_id=1, source_target_pairs={{0,1},{1,0},{2,3},{3,2},{4,5},{5,4},{6,7},{7,6},{8,9},{9,8},{10,11... | collective-permute-start | bytes 3145736 | tf_op jit(solution)/shard_map/ppermute | solution.py:86
  47.1 9.3 %collective-permute-done.1.refs_0_.refs_5_ = bf16[256,2048]{1,0:T(8,128)(2,1)S(1)} collective-permute-done((bf16[256,2048]{1,0:T(8,128)(2,1)S(1)}, bf16[256,2048]{1,0:T(8,128)(2,1)S(1)}, u32[]{:S(2)}, u32[]{:S(2)}) %collective-permute-start.1) | collective-permute-done | bytes 1048608 | tf_op jit(solution)/shard_map/ppermute | solution.py:86
  56.4 0.0 copy-start.2
  56.4 18.6 %collective-permute-start.3 = (bf16[256,2048]{1,0:T(8,128)(2,1)S(1)}, bf16[256,2048]{1,0:T(8,128)(2,1)}, u32[]{:S(2)}, u32[]{:S(2)}) collective-permute-start(bf16[256,2048]{1,0:T(8,128)(2,1)S(1)} %collective-permute-done.1.refs_0_.refs_5_), channel_id=1, source_target_pairs={{1,0},{3,2},{5,4},{7,6},{9,8},{11,10},{13,12},{15,14},{17,16},{19,... | collective-permute-start | bytes 3145736 | tf_op jit(solution)/shard_map/ppermute | solution.py:86
  75.0 0.6 compare_convert_fusion.valid_ref
  75.6 16.6 %collective-permute-done.4 = bf16[256,2048]{1,0:T(8,128)(2,1)} collective-permute-done((bf16[256,2048]{1,0:T(8,128)(2,1)S(1)}, bf16[256,2048]{1,0:T(8,128)(2,1)}, u32[]{:S(2)}, u32[]{:S(2)}) %collective-permute-start.4) | collective-permute-done | bytes 1048608 | tf_op jit(solution)/shard_map/ppermute | solution.py:86
  92.2 11.2 %collective-permute-done.2 = bf16[256,2048]{1,0:T(8,128)(2,1)} collective-permute-done((bf16[256,2048]{1,0:T(8,128)(2,1)S(1)}, bf16[256,2048]{1,0:T(8,128)(2,1)}, u32[]{:S(2)}, u32[]{:S(2)}) %collective-permute-start.2) | collective-permute-done | bytes 1048608 | tf_op jit(solution)/shard_map/ppermute | solution.py:86
  103.4 0.0 collective-permute-done.3
  103.4 3.1 %broadcast_select_fusion = (bf16[256,2048]{1,0:T(8,128)(2,1)}, bf16[256,2048]{1,0:T(8,128)(2,1)}) fusion(bf16[256,2048]{1,0:T(8,128)(2,1)} %collective-permute-done.4, bf16[256,2048]{1,0:T(8,128)(2,1)} %collective-permute-done.2, pred[]{:T(512)S(6)} %eq.5, bf16[256,2048]{1,0:T(8,128)(2,1)} %collective-permute-done.3), kind=kLoop, calls=%fused_computation | loop fusion | flops 1048576 | bytes 5242881 | tf_op jit(solution)/shard_map/jit(_where)/select_n | solution.py:101
  106.5 0.0 copy-done
  106.5 0.0 copy-done.1
  106.5 0.0 copy-done.2
  106.5 15.6 %shard_map.37 = bf16[256,2048]{1,0:T(8,128)(2,1)} custom-call(s32[5]{0:T(128)} %compare_convert_fusion.valid_ref, bf16[256,2048]{1,0:T(8,128)(2,1)} %q_ref.1, bf16[256,2048]{1,0:T(8,128)(2,1)} %copy-done.2, bf16[256,2048]{1,0:T(8,128)(2,1)} %get-tuple-element.6.refs_1_.refs_6_, bf16[256,2048]{1,0:T(8,128)(2,1)} %copy-done.1, ...), custom_call_target="tpu_custom_call" | custom-call | flops 2684354560 | bytes 7340032 | tf_op jit(solution)/shard_map/pallas_call | solution.py:68
  (1 shorter events, 0.0 us)
Async XLA Ops:
  0.0 1.2 copy-start.3
  1.2 105.2 %copy-start = (bf16[256,2048]{1,0:T(8,128)(2,1)}, bf16[256,2048]{1,0:T(8,128)(2,1)S(1)}, u32[]{:S(2)}) copy-start(bf16[256,2048]{1,0:T(8,128)(2,1)S(1)} %constant_dynamic-update-slice_fusion.refs_4_.refs_9_) | copy-start | bytes 3145732
  1.3 28.8 %collective-permute-start = (bf16[256,2048]{1,0:T(8,128)(2,1)S(1)}, bf16[256,2048]{1,0:T(8,128)(2,1)S(1)}, u32[]{:S(2)}, u32[]{:S(2)}) collective-permute-start(bf16[256,2048]{1,0:T(8,128)(2,1)S(1)} %constant_dynamic-update-slice_fusion.refs_4_.refs_9_), channel_id=1, source_target_pairs={{0,2},{1,3},{2,4},{3,5},{4,6},{5,7},{6,8},{7,9},{8,10},{9,11},{10,... | collective-permute-start | bytes 3145736 | tf_op jit(solution)/shard_map/ppermute | solution.py:86
  30.0 76.5 %copy-start.1 = (bf16[256,2048]{1,0:T(8,128)(2,1)}, bf16[256,2048]{1,0:T(8,128)(2,1)S(1)}, u32[]{:S(2)}) copy-start(bf16[256,2048]{1,0:T(8,128)(2,1)S(1)} %collective-permute-done.refs_2_.refs_7_) | copy-start | bytes 3145732
  30.0 26.3 %collective-permute-start.1 = (bf16[256,2048]{1,0:T(8,128)(2,1)S(1)}, bf16[256,2048]{1,0:T(8,128)(2,1)S(1)}, u32[]{:S(2)}, u32[]{:S(2)}) collective-permute-start(bf16[256,2048]{1,0:T(8,128)(2,1)S(1)} %collective-permute-done.refs_2_.refs_7_), channel_id=1, source_target_pairs={{0,2},{1,3},{2,4},{3,5},{4,6},{5,7},{6,8},{7,9},{8,10},{9,11},{10,... | collective-permute-start | bytes 3145736 | tf_op jit(solution)/shard_map/ppermute | solution.py:86
  40.8 51.4 %collective-permute-start.4 = (bf16[256,2048]{1,0:T(8,128)(2,1)S(1)}, bf16[256,2048]{1,0:T(8,128)(2,1)}, u32[]{:S(2)}, u32[]{:S(2)}) collective-permute-start(bf16[256,2048]{1,0:T(8,128)(2,1)S(1)} %constant_dynamic-update-slice_fusion.refs_4_.refs_9_), channel_id=1, source_target_pairs={{0,1},{2,3},{4,5},{6,7},{8,9},{10,11},{12,13},{14,15},{16,17},{18,... | collective-permute-start | bytes 3145736 | tf_op jit(solution)/shard_map/ppermute | solution.py:86
  42.1 61.3 %collective-permute-start.2 = (bf16[256,2048]{1,0:T(8,128)(2,1)S(1)}, bf16[256,2048]{1,0:T(8,128)(2,1)}, u32[]{:S(2)}, u32[]{:S(2)}) collective-permute-start(bf16[256,2048]{1,0:T(8,128)(2,1)S(1)} %collective-permute-done.refs_2_.refs_7_), channel_id=1, source_target_pairs={{0,1},{1,0},{2,3},{3,2},{4,5},{5,4},{6,7},{7,6},{8,9},{9,8},{10,11... | collective-permute-start | bytes 3145736 | tf_op jit(solution)/shard_map/ppermute | solution.py:86
  56.4 50.1 %copy-start.2 = (bf16[256,2048]{1,0:T(8,128)(2,1)}, bf16[256,2048]{1,0:T(8,128)(2,1)S(1)}, u32[]{:S(2)}) copy-start(bf16[256,2048]{1,0:T(8,128)(2,1)S(1)} %collective-permute-done.1.refs_0_.refs_5_) | copy-start | bytes 3145732
  56.4 47.1 %collective-permute-start.3 = (bf16[256,2048]{1,0:T(8,128)(2,1)S(1)}, bf16[256,2048]{1,0:T(8,128)(2,1)}, u32[]{:S(2)}, u32[]{:S(2)}) collective-permute-start(bf16[256,2048]{1,0:T(8,128)(2,1)S(1)} %collective-permute-done.1.refs_0_.refs_5_), channel_id=1, source_target_pairs={{1,0},{3,2},{5,4},{7,6},{9,8},{11,10},{13,12},{15,14},{17,16},{19,... | collective-permute-start | bytes 3145736 | tf_op jit(solution)/shard_map/ppermute | solution.py:86

commit v4 on v3

v4 whole, which is shorter than its diff:
```python
import functools

import jax
import jax.numpy as jnp
from jax import lax
from jax.experimental import pallas as pl
from jax.experimental.pallas import tpu as pltpu
from jax.sharding import PartitionSpec as P

HEADS = 16
KV_HEADS = 8
HEAD_DIM = 128
WINDOW = 1024
NEG = -1e30
GROUP = HEADS // KV_HEADS

LOWER, UPPER, WHOLE = 0, 1, 2


def step_kernel(kinds, first, last, valid_ref, q_ref, *refs):
    nblk = len(kinds)
    k_refs, v_refs = refs[:nblk], refs[nblk:2 * nblk]
    rest = refs[2 * nblk:]
    if not first:
        m_in, l_in, acc_in = rest[:3]
        rest = rest[3:]
    tok = q_ref.shape[0]
    h = pl.program_id(0)
    row = lax.broadcasted_iota(jnp.int32, (tok, tok), 0)
    col = lax.broadcasted_iota(jnp.int32, (tok, tok), 1)
    lane = lax.broadcasted_iota(jnp.int32, (tok, HEADS), 1)
    for a in range(GROUP):
        qa = q_ref[:, a * HEAD_DIM:(a + 1) * HEAD_DIM]
        here = lane == h * GROUP + a
        scores = []
        for j, kind in enumerate(kinds):
            s = lax.dot_general(
                qa, k_refs[j][...], (((1,), (1,)), ((), ())),
                preferred_element_type=jnp.float32,
            ) * HEAD_DIM ** (-0.5)
            keep = valid_ref[j] > 0
            if kind == LOWER:
                keep = (col <= row) & keep
            elif kind == UPPER:
                keep = (col > row) & keep
            scores.append(jnp.where(keep, s, NEG))
        largest = scores[0].max(axis=1, keepdims=True)
        for s in scores[1:]:
            largest = jnp.maximum(largest, s.max(axis=1, keepdims=True))
        if not first:
            m_old = jnp.sum(jnp.where(here, m_in[...], 0.0), axis=1, keepdims=True)
            l_old = jnp.sum(jnp.where(here, l_in[...], 0.0), axis=1, keepdims=True)
            largest = jnp.maximum(largest, m_old)
        expos = [jnp.exp(s - largest) for s in scores]
        total = expos[0].sum(axis=1, keepdims=True)
        for e in expos[1:]:
            total = total + e.sum(axis=1, keepdims=True)
        acc = None
        for j in range(nblk):
            hi = expos[j].astype(jnp.bfloat16)
            lo = (expos[j] - hi.astype(jnp.float32)).astype(jnp.bfloat16)
            vj = v_refs[j][...]
            part = jnp.dot(hi, vj, preferred_element_type=jnp.float32) + jnp.dot(
                lo, vj, preferred_element_type=jnp.float32
            )
            acc = part if acc is None else acc + part
        cols = slice(a * HEAD_DIM, (a + 1) * HEAD_DIM)
        if not first:
            scale = jnp.exp(m_old - largest)
            total = total + scale * l_old
            acc = acc + scale * acc_in[:, cols]
        if last:
            rest[0][:, cols] = (acc * (1.0 / total)).astype(rest[0].dtype)
        else:
            m_out, l_out, acc_out = rest
            acc_out[:, cols] = acc
            m_out[...] = jnp.where(here, largest, m_out[...])
            l_out[...] = jnp.where(here, total, l_out[...])


def attend_step(kinds, first, last, valid, queries, kv_blocks, state):
    tok = queries.shape[0]
    nblk = len(kinds)
    k_spec = pl.BlockSpec((tok, HEAD_DIM), lambda h: (0, h))
    v_spec = pl.BlockSpec((tok, HEAD_DIM), lambda h: (0, KV_HEADS + h))
    q_spec = pl.BlockSpec((tok, GROUP * HEAD_DIM), lambda h: (0, h))
    stat_spec = pl.BlockSpec((tok, HEADS), lambda h: (0, 0))
    in_specs = [pl.BlockSpec(memory_space=pltpu.SMEM), q_spec]
    in_specs += [k_spec] * nblk + [v_spec] * nblk
    args = [valid, queries, *kv_blocks, *kv_blocks]
    if not first:
        in_specs += [stat_spec, stat_spec, q_spec]
        args += list(state)
    if last:
        out_specs = q_spec
        out_shape = jax.ShapeDtypeStruct(queries.shape, queries.dtype)
    else:
        out_specs = [stat_spec, stat_spec, q_spec]
        out_shape = [
            jax.ShapeDtypeStruct((tok, HEADS), jnp.float32),
            jax.ShapeDtypeStruct((tok, HEADS), jnp.float32),
            jax.ShapeDtypeStruct(queries.shape, jnp.float32),
        ]
    flops = 4 * HEADS * tok * tok * nblk * HEAD_DIM
    nbytes = 2 * queries.size * (2 if last else 1) + 2 * nblk * kv_blocks[0].size
    nbytes += (0 if first else 4 * queries.size) + (0 if last else 4 * queries.size)
    return pl.pallas_call(
        functools.partial(step_kernel, tuple(kinds), first, last),
        grid=(KV_HEADS,),
        in_specs=in_specs,
        out_specs=out_specs,
        out_shape=out_shape,
        cost_estimate=pl.CostEstimate(
            flops=flops, transcendentals=HEADS * tok * tok * nblk, bytes_accessed=nbytes
        ),
    )(*args)


def shifted(x, axis, pairs):
    return lax.ppermute(x, axis, pairs)


def flags(*conds):
    return jnp.stack([c.astype(jnp.int32) for c in conds])


def body(queries, keys, values):
    axis = ("blk", "grp")
    n = lax.axis_size(axis)
    d = lax.axis_index(axis)
    odd = (d % 2) == 1
    own = jnp.concatenate([keys, values], axis=1)
    ahead2 = [(i, i + 2) for i in range(n) if i + 2 < n]
    x1 = shifted(own, axis, ahead2)
    y1 = shifted(own, axis, [(i, i + 1) for i in range(0, n, 2)])
    x1, y1 = lax.optimization_barrier((x1, y1))
    x2 = shifted(x1, axis, ahead2)
    y2 = shifted(x1, axis, [(i, i ^ 1) for i in range(n)])
    y3 = shifted(x2, axis, [(i, i - 1) for i in range(1, n, 2)])

    v1 = flags(d >= 0, d >= 2, odd)
    state = attend_step((LOWER, WHOLE, WHOLE), True, False, v1, queries, [own, x1, y1], None)
    v2 = flags(d >= 4, d >= jnp.where(odd, 3, 1))
    state = attend_step((UPPER, WHOLE), False, False, v2, queries, [x2, y2], state)
    v3 = flags(jnp.logical_not(odd) & (d >= 3))
    return attend_step((WHOLE,), False, True, v3, queries, [y3], state)


def solution(mesh):
    placed = (P(("blk", "grp"), None), P(("blk", "grp"), None), P(("blk", "grp"), None))
    return jax.shard_map(
        body, mesh=mesh, in_specs=placed, out_specs=P(("blk", "grp"), None), check_vma=False
    )
```

time: 122 us -> 130 us (1.066)
  the two profiles are of different devices: /device:TPU:255 before, /device:TPU:504 now
where the time goes in v4:
time: 130 us
  starting transfers between devices  71.6 us (55%)
  Pallas kernels  31.2 us (24%)
  waiting for transfers between devices  22.4 us (17%)
  local copies, waits for them, and re-layouts  3.14 us (2%)
    ppermute x5, starting transfers between devices, shifted(): return lax.ppermute(x, axis, pairs)  71.6 us
    pallas_call x3, Pallas kernels, attend_step(): pl.pallas_call(functools.partial(step_kernel, tuple(kinds), first, last),...  31.2 us
    ppermute x5, waiting for transfers between devices, shifted(): return lax.ppermute(x, axis, pairs)  22.4 us
  transfers between devices with their start and end apart: 5, of which 2 were waited for; matrix products, arithmetic and copies ran while one was open for 1% of the time, Pallas kernels for 18%

profile of v4, /device:TPU:504, one launch (start us, length us, event | category | flops | bytes accessed | tf_op | source)
XLA Modules:
  0.0 129.7 jit_solution(18349549283554260668)
XLA Ops:
  0.0 1.1 constant_dynamic-update-slice_fusion.1
  1.1 1.1 constant_dynamic-update-slice_fusion.refs_0_.refs_3_
  2.2 0.0 copy-start
  2.2 1.3 collective-permute-start.1
  3.5 3.4 %collective-permute-start = (bf16[256,2048]{1,0:T(8,128)(2,1)S(1)}, bf16[256,2048]{1,0:T(8,128)(2,1)}, u32[]{:S(2)}, u32[]{:S(2)}) collective-permute-start(bf16[256,2048]{1,0:T(8,128)(2,1)S(1)} %constant_dynamic-update-slice_fusion.refs_0_.refs_3_), channel_id=1, source_target_pairs={{0,2},{1,3},{2,4},{3,5},{4,6},{5,7},{6,8},{7,9},{8,10},{9,11},{10,... | collective-permute-start | bytes 3145736 | tf_op jit(solution)/shard_map/ppermute | solution.py:120
  6.9 22.1 %collective-permute-done.1.refs_2_.refs_5_ = bf16[256,2048]{1,0:T(8,128)(2,1)S(1)} collective-permute-done((bf16[256,2048]{1,0:T(8,128)(2,1)S(1)}, bf16[256,2048]{1,0:T(8,128)(2,1)S(1)}, u32[]{:S(2)}, u32[]{:S(2)}) %collective-permute-start.1) | collective-permute-done | bytes 1048608 | tf_op jit(solution)/shard_map/ppermute | solution.py:120
  29.0 0.0 copy-start.3
  29.0 0.3 collective-permute-done.refs_1_.refs_4_
  29.3 4.5 %collective-permute-start.2 = (bf16[256,2048]{1,0:T(8,128)(2,1)}, bf16[256,2048]{1,0:T(8,128)(2,1)S(1)}, u32[]{:S(2)}, u32[]{:S(2)}) collective-permute-start(bf16[256,2048]{1,0:T(8,128)(2,1)} %collective-permute-done.refs_1_.refs_4_), channel_id=1, source_target_pairs={{0,2},{1,3},{2,4},{3,5},{4,6},{5,7},{6,8},{7,9},{8,10},{9,11},{10,... | collective-permute-start | bytes 3145736 | tf_op jit(solution)/shard_map/ppermute | solution.py:120
  33.8 45.0 %collective-permute-start.4 = (bf16[256,2048]{1,0:T(8,128)(2,1)}, bf16[256,2048]{1,0:T(8,128)(2,1)}, u32[]{:S(2)}, u32[]{:S(2)}) collective-permute-start(bf16[256,2048]{1,0:T(8,128)(2,1)} %collective-permute-done.refs_1_.refs_4_), channel_id=1, source_target_pairs={{0,1},{1,0},{2,3},{3,2},{4,5},{5,4},{6,7},{7,6},{8,9},{9,8},{10,11... | collective-permute-start | bytes 3145736 | tf_op jit(solution)/shard_map/ppermute | solution.py:120
  78.8 0.0 collective-permute-done.2.refs_0_.refs_2_
  78.8 0.0 copy-done.3
  78.8 0.0 copy-start.1
  78.8 17.4 %collective-permute-start.3 = (bf16[256,2048]{1,0:T(8,128)(2,1)S(1)}, bf16[256,2048]{1,0:T(8,128)(2,1)S(1)}, u32[]{:S(2)}, u32[]{:S(2)}) collective-permute-start(bf16[256,2048]{1,0:T(8,128)(2,1)S(1)} %collective-permute-done.2.refs_0_.refs_2_), channel_id=1, source_target_pairs={{1,0},{3,2},{5,4},{7,6},{9,8},{11,10},{13,12},{15,14},{17,16},{19,... | collective-permute-start | bytes 3145736 | tf_op jit(solution)/shard_map/ppermute | solution.py:120
  96.3 0.6 add_convert_fusion.valid_ref
  96.8 0.7 add_convert_fusion.1.valid_ref
  97.5 0.0 copy-done
  97.5 12.2 %shard_map.37 = (f32[256,16]{1,0:T(8,128)}, f32[256,16]{1,0:T(8,128)}, f32[256,2048]{1,0:T(8,128)}) custom-call(s32[3]{0:T(128)} %add_convert_fusion.1.valid_ref, bf16[256,2048]{1,0:T(8,128)(2,1)} %q_ref.5, bf16[256,2048]{1,0:T(8,128)(2,1)} %copy-done, bf16[256,2048]{1,0:T(8,128)(2,1)} %collective-permute-done.refs_1_.refs_4_, bf16[256,2048]{1,0:T(8,128)(2,1)} %copy-done.3, ...), custom_call_target="tpu_custom_call" | custom-call | flops 1610612736 | bytes 6291456 | tf_op jit(solution)/shard_map/pallas_call | solution.py:107
  109.7 0.0 copy-done.1
  109.7 0.0 collective-permute-done.4.refs_1_.refs_3_
  109.7 10.7 %shard_map.38 = (f32[256,16]{1,0:T(8,128)}, f32[256,16]{1,0:T(8,128)}, f32[256,2048]{1,0:T(8,128)}) custom-call(s32[2]{0:T(128)} %add_convert_fusion.valid_ref, bf16[256,2048]{1,0:T(8,128)(2,1)} %q_ref.5, bf16[256,2048]{1,0:T(8,128)(2,1)} %copy-done.1, bf16[256,2048]{1,0:T(8,128)(2,1)} %collective-permute-done.4.refs_1_.refs_3_, ...), custom_call_target="tpu_custom_call" | custom-call | flops 1073741824 | bytes 7340032 | tf_op jit(solution)/shard_map/pallas_call | solution.py:107
  120.4 0.0 collective-permute-done.3.refs_0_.refs_1_
  120.4 0.0 copy-start.2
  120.4 1.0 copy-done.2
  121.4 8.3 %shard_map.39 = bf16[256,2048]{1,0:T(8,128)(2,1)} custom-call(s32[1]{0:T(128)} %bitcast.valid_ref, bf16[256,2048]{1,0:T(8,128)(2,1)} %q_ref.5, bf16[256,2048]{1,0:T(8,128)(2,1)} %copy-done.2, bf16[256,2048]{1,0:T(8,128)(2,1)} %copy-done.2, f32[256,16]{1,0:T(8,128)} %get-tuple-element.18.refs_2_, f32[256,16]{1,0:T(8,128)} %get-tuple-element.19.refs_3_, ...), custom_call_target="tpu_custom_call" | custom-call | flops 536870912 | bytes 5242880 | tf_op jit(solution)/shard_map/pallas_call | solution.py:107
Async XLA Ops:
  2.2 95.3 %copy-start = (bf16[256,2048]{1,0:T(8,128)(2,1)}, bf16[256,2048]{1,0:T(8,128)(2,1)S(1)}, u32[]{:S(2)}) copy-start(bf16[256,2048]{1,0:T(8,128)(2,1)S(1)} %constant_dynamic-update-slice_fusion.refs_0_.refs_3_) | copy-start | bytes 3145732
  2.2 26.8 %collective-permute-start.1 = (bf16[256,2048]{1,0:T(8,128)(2,1)S(1)}, bf16[256,2048]{1,0:T(8,128)(2,1)S(1)}, u32[]{:S(2)}, u32[]{:S(2)}) collective-permute-start(bf16[256,2048]{1,0:T(8,128)(2,1)S(1)} %constant_dynamic-update-slice_fusion.refs_0_.refs_3_), channel_id=1, source_target_pairs={{0,1},{2,3},{4,5},{6,7},{8,9},{10,11},{12,13},{14,15},{16,17},{18,... | collective-permute-start | bytes 3145736 | tf_op jit(solution)/shard_map/ppermute | solution.py:120
  3.5 25.8 %collective-permute-start = (bf16[256,2048]{1,0:T(8,128)(2,1)S(1)}, bf16[256,2048]{1,0:T(8,128)(2,1)}, u32[]{:S(2)}, u32[]{:S(2)}) collective-permute-start(bf16[256,2048]{1,0:T(8,128)(2,1)S(1)} %constant_dynamic-update-slice_fusion.refs_0_.refs_3_), channel_id=1, source_target_pairs={{0,2},{1,3},{2,4},{3,5},{4,6},{5,7},{6,8},{7,9},{8,10},{9,11},{10,... | collective-permute-start | bytes 3145736 | tf_op jit(solution)/shard_map/ppermute | solution.py:120
  29.0 49.8 %copy-start.3 = (bf16[256,2048]{1,0:T(8,128)(2,1)}, bf16[256,2048]{1,0:T(8,128)(2,1)S(1)}, u32[]{:S(2)}) copy-start(bf16[256,2048]{1,0:T(8,128)(2,1)S(1)} %collective-permute-done.1.refs_2_.refs_5_) | copy-start | bytes 3145732
  29.3 49.5 %collective-permute-start.2 = (bf16[256,2048]{1,0:T(8,128)(2,1)}, bf16[256,2048]{1,0:T(8,128)(2,1)S(1)}, u32[]{:S(2)}, u32[]{:S(2)}) collective-permute-start(bf16[256,2048]{1,0:T(8,128)(2,1)} %collective-permute-done.refs_1_.refs_4_), channel_id=1, source_target_pairs={{0,2},{1,3},{2,4},{3,5},{4,6},{5,7},{6,8},{7,9},{8,10},{9,11},{10,... | collective-permute-start | bytes 3145736 | tf_op jit(solution)/shard_map/ppermute | solution.py:120
  33.8 75.9 %collective-permute-start.4 = (bf16[256,2048]{1,0:T(8,128)(2,1)}, bf16[256,2048]{1,0:T(8,128)(2,1)}, u32[]{:S(2)}, u32[]{:S(2)}) collective-permute-start(bf16[256,2048]{1,0:T(8,128)(2,1)} %collective-permute-done.refs_1_.refs_4_), channel_id=1, source_target_pairs={{0,1},{1,0},{2,3},{3,2},{4,5},{5,4},{6,7},{7,6},{8,9},{9,8},{10,11... | collective-permute-start | bytes 3145736 | tf_op jit(solution)/shard_map/ppermute | solution.py:120
  78.8 30.9 %copy-start.1 = (bf16[256,2048]{1,0:T(8,128)(2,1)}, bf16[256,2048]{1,0:T(8,128)(2,1)S(1)}, u32[]{:S(2)}) copy-start(bf16[256,2048]{1,0:T(8,128)(2,1)S(1)} %collective-permute-done.2.refs_0_.refs_2_) | copy-start | bytes 3145732
  78.8 41.6 %collective-permute-start.3 = (bf16[256,2048]{1,0:T(8,128)(2,1)S(1)}, bf16[256,2048]{1,0:T(8,128)(2,1)S(1)}, u32[]{:S(2)}, u32[]{:S(2)}) collective-permute-start(bf16[256,2048]{1,0:T(8,128)(2,1)S(1)} %collective-permute-done.2.refs_0_.refs_2_), channel_id=1, source_target_pairs={{1,0},{3,2},{5,4},{7,6},{9,8},{11,10},{13,12},{15,14},{17,16},{19,... | collective-permute-start | bytes 3145736 | tf_op jit(solution)/shard_map/ppermute | solution.py:120
  120.4 1.0 copy-start.2

commit v5 on v2

--- a/solution.py
+++ b/solution.py
@@ -89,6 +89,9 @@
     ahead2 = [(i, i + 2) for i in range(n) if i + 2 < n]
     x1 = shifted(own, axis, ahead2)
     y1 = shifted(own, axis, [(i, i + 1) for i in range(0, n, 2)])
+    fenced = [lax.optimization_barrier((a, b)) for a, b in zip(x1, y1)]
+    x1 = tuple(f[0] for f in fenced)
+    y1 = tuple(f[1] for f in fenced)
     x2 = shifted(x1, axis, ahead2)
     y2 = shifted(x1, axis, [(i, i ^ 1) for i in range(n)])
     y3 = shifted(x2, axis, [(i, i - 1) for i in range(1, n, 2)])

time: 116 us -> 123 us (1.060)
  the two profiles are of different devices: /device:TPU:207 before, /device:TPU:256 now
where the time goes in v5:
time: 123 us
  waiting for transfers between devices  79.7 us (65%)
  starting transfers between devices  24.5 us (20%)
  Pallas kernels  15.5 us (13%)
  other arithmetic  2.7 us (2%)
    ppermute x10, waiting for transfers between devices, shifted(): return lax.ppermute(x, axis, pairs)  79.7 us
    ppermute x10, starting transfers between devices, shifted(): return lax.ppermute(x, axis, pairs)  24.5 us
    pallas_call x1, Pallas kernels, attend(): pl.pallas_call(attend_kernel, grid=(KV_HEADS,), in_specs=[pl.BlockSpec(me...  15.5 us
  transfers between devices with their start and end apart: 10, of which 6 were waited for; matrix products, arithmetic and copies ran while one was open for 1% of the time, Pallas kernels for 0%

profile of v5, /device:TPU:256, one launch (start us, length us, event | category | flops | bytes accessed | tf_op | source)
XLA Modules:
  0.0 122.5 jit_solution(4144681590913490610)
XLA Ops:
  0.0 3.4 %collective-permute-start = (bf16[256,1024]{1,0:T(8,128)(2,1)}, bf16[256,1024]{1,0:T(8,128)(2,1)}, u32[]{:S(2)}, u32[]{:S(2)}) collective-permute-start(bf16[256,1024]{1,0:T(8,128)(2,1)} %refs_4_.1), channel_id=1, source_target_pairs={{0,2},{1,3},{2,4},{3,5},{4,6},{5,7},{6,8},{7,9},{8,10},{9,11},{10,... | collective-permute-start | bytes 1572872 | tf_op jit(solution)/shard_map/ppermute | solution.py:81
  3.4 3.5 %collective-permute-start.1 = (bf16[256,1024]{1,0:T(8,128)(2,1)}, bf16[256,1024]{1,0:T(8,128)(2,1)S(1)}, u32[]{:S(2)}, u32[]{:S(2)}) collective-permute-start(bf16[256,1024]{1,0:T(8,128)(2,1)} %refs_4_.1), channel_id=1, source_target_pairs={{0,1},{2,3},{4,5},{6,7},{8,9},{10,11},{12,13},{14,15},{16,17},{18,... | collective-permute-start | bytes 1572872 | tf_op jit(solution)/shard_map/ppermute | solution.py:81
  6.9 3.4 %collective-permute-start.5 = (bf16[256,1024]{1,0:T(8,128)(2,1)}, bf16[256,1024]{1,0:T(8,128)(2,1)}, u32[]{:S(2)}, u32[]{:S(2)}) collective-permute-start(bf16[256,1024]{1,0:T(8,128)(2,1)} %refs_9_.1), channel_id=1, source_target_pairs={{0,2},{1,3},{2,4},{3,5},{4,6},{5,7},{6,8},{7,9},{8,10},{9,11},{10,... | collective-permute-start | bytes 1572872 | tf_op jit(solution)/shard_map/ppermute | solution.py:81
  10.3 1.3 %collective-permute-start.6 = (bf16[256,1024]{1,0:T(8,128)(2,1)}, bf16[256,1024]{1,0:T(8,128)(2,1)S(1)}, u32[]{:S(2)}, u32[]{:S(2)}) collective-permute-start(bf16[256,1024]{1,0:T(8,128)(2,1)} %refs_9_.1), channel_id=1, source_target_pairs={{0,1},{2,3},{4,5},{6,7},{8,9},{10,11},{12,13},{14,15},{16,17},{18,... | collective-permute-start | bytes 1572872 | tf_op jit(solution)/shard_map/ppermute | solution.py:81
  11.7 21.1 %collective-permute-done.refs_2_ = bf16[256,1024]{1,0:T(8,128)(2,1)} collective-permute-done((bf16[256,1024]{1,0:T(8,128)(2,1)}, bf16[256,1024]{1,0:T(8,128)(2,1)}, u32[]{:S(2)}, u32[]{:S(2)}) %collective-permute-start) | collective-permute-done | bytes 524320 | tf_op jit(solution)/shard_map/ppermute | solution.py:81
  32.7 0.0 collective-permute-done.1
  32.7 1.9 %collective-permute-start.2 = (bf16[256,1024]{1,0:T(8,128)(2,1)}, bf16[256,1024]{1,0:T(8,128)(2,1)}, u32[]{:S(2)}, u32[]{:S(2)}) collective-permute-start(bf16[256,1024]{1,0:T(8,128)(2,1)} %collective-permute-done.refs_2_), channel_id=1, source_target_pairs={{0,2},{1,3},{2,4},{3,5},{4,6},{5,7},{6,8},{7,9},{8,10},{9,11},{10,... | collective-permute-start | bytes 1572872 | tf_op jit(solution)/shard_map/ppermute | solution.py:81
  34.7 15.7 %collective-permute-done.5.refs_7_ = bf16[256,1024]{1,0:T(8,128)(2,1)} collective-permute-done((bf16[256,1024]{1,0:T(8,128)(2,1)}, bf16[256,1024]{1,0:T(8,128)(2,1)}, u32[]{:S(2)}, u32[]{:S(2)}) %collective-permute-start.5) | collective-permute-done | bytes 524320 | tf_op jit(solution)/shard_map/ppermute | solution.py:81
  50.3 0.0 collective-permute-done.6
  50.3 1.9 %collective-permute-start.7 = (bf16[256,1024]{1,0:T(8,128)(2,1)}, bf16[256,1024]{1,0:T(8,128)(2,1)}, u32[]{:S(2)}, u32[]{:S(2)}) collective-permute-start(bf16[256,1024]{1,0:T(8,128)(2,1)} %collective-permute-done.5.refs_7_), channel_id=1, source_target_pairs={{0,2},{1,3},{2,4},{3,5},{4,6},{5,7},{6,8},{7,9},{8,10},{9,11},{10,... | collective-permute-start | bytes 1572872 | tf_op jit(solution)/shard_map/ppermute | solution.py:81
  52.3 1.9 %collective-permute-start.3 = (bf16[256,1024]{1,0:T(8,128)(2,1)}, bf16[256,1024]{1,0:T(8,128)(2,1)S(1)}, u32[]{:S(2)}, u32[]{:S(2)}) collective-permute-start(bf16[256,1024]{1,0:T(8,128)(2,1)} %collective-permute-done.refs_2_), channel_id=1, source_target_pairs={{0,1},{1,0},{2,3},{3,2},{4,5},{5,4},{6,7},{7,6},{8,9},{9,8},{10,11... | collective-permute-start | bytes 1572872 | tf_op jit(solution)/shard_map/ppermute | solution.py:81
  54.2 29.2 %collective-permute-done.2.refs_0_ = bf16[256,1024]{1,0:T(8,128)(2,1)} collective-permute-done((bf16[256,1024]{1,0:T(8,128)(2,1)}, bf16[256,1024]{1,0:T(8,128)(2,1)}, u32[]{:S(2)}, u32[]{:S(2)}) %collective-permute-start.2) | collective-permute-done | bytes 524320 | tf_op jit(solution)/shard_map/ppermute | solution.py:81
  83.4 1.3 %collective-permute-start.4 = (bf16[256,1024]{1,0:T(8,128)(2,1)}, bf16[256,1024]{1,0:T(8,128)(2,1)S(1)}, u32[]{:S(2)}, u32[]{:S(2)}) collective-permute-start(bf16[256,1024]{1,0:T(8,128)(2,1)} %collective-permute-done.2.refs_0_), channel_id=1, source_target_pairs={{1,0},{3,2},{5,4},{7,6},{9,8},{11,10},{13,12},{15,14},{17,16},{19,... | collective-permute-start | bytes 1572872 | tf_op jit(solution)/shard_map/ppermute | solution.py:81
  84.7 4.6 %collective-permute-start.8 = (bf16[256,1024]{1,0:T(8,128)(2,1)}, bf16[256,1024]{1,0:T(8,128)(2,1)S(1)}, u32[]{:S(2)}, u32[]{:S(2)}) collective-permute-start(bf16[256,1024]{1,0:T(8,128)(2,1)} %collective-permute-done.5.refs_7_), channel_id=1, source_target_pairs={{0,1},{1,0},{2,3},{3,2},{4,5},{5,4},{6,7},{7,6},{8,9},{9,8},{10,11... | collective-permute-start | bytes 1572872 | tf_op jit(solution)/shard_map/ppermute | solution.py:81
  89.3 0.0 collective-permute-done.7.refs_5_
  89.3 1.3 %collective-permute-start.9 = (bf16[256,1024]{1,0:T(8,128)(2,1)}, bf16[256,1024]{1,0:T(8,128)(2,1)S(1)}, u32[]{:S(2)}, u32[]{:S(2)}) collective-permute-start(bf16[256,1024]{1,0:T(8,128)(2,1)} %collective-permute-done.7.refs_5_), channel_id=1, source_target_pairs={{1,0},{3,2},{5,4},{7,6},{9,8},{11,10},{13,12},{15,14},{17,16},{19,... | collective-permute-start | bytes 1572872 | tf_op jit(solution)/shard_map/ppermute | solution.py:81
  90.6 0.5 compare_convert_fusion.valid_ref
  91.1 0.0 collective-permute-done.3
  91.1 3.5 %collective-permute-done.4 = bf16[256,1024]{1,0:T(8,128)(2,1)S(1)} collective-permute-done((bf16[256,1024]{1,0:T(8,128)(2,1)}, bf16[256,1024]{1,0:T(8,128)(2,1)S(1)}, u32[]{:S(2)}, u32[]{:S(2)}) %collective-permute-start.4) | collective-permute-done | bytes 524320 | tf_op jit(solution)/shard_map/ppermute | solution.py:81
  94.7 1.1 broadcast_select_fusion.2
  95.8 4.5 %collective-permute-done.8 = bf16[256,1024]{1,0:T(8,128)(2,1)S(1)} collective-permute-done((bf16[256,1024]{1,0:T(8,128)(2,1)}, bf16[256,1024]{1,0:T(8,128)(2,1)S(1)}, u32[]{:S(2)}, u32[]{:S(2)}) %collective-permute-start.8) | collective-permute-done | bytes 524320 | tf_op jit(solution)/shard_map/ppermute | solution.py:81
  100.3 5.6 %collective-permute-done.9 = bf16[256,1024]{1,0:T(8,128)(2,1)S(1)} collective-permute-done((bf16[256,1024]{1,0:T(8,128)(2,1)}, bf16[256,1024]{1,0:T(8,128)(2,1)S(1)}, u32[]{:S(2)}, u32[]{:S(2)}) %collective-permute-start.9) | collective-permute-done | bytes 524320 | tf_op jit(solution)/shard_map/ppermute | solution.py:81
  105.9 1.1 broadcast_select_fusion
  107.0 15.5 %shard_map.37 = bf16[256,2048]{1,0:T(8,128)(2,1)} custom-call(s32[5]{0:T(128)} %compare_convert_fusion.valid_ref, bf16[256,2048]{1,0:T(8,128)(2,1)} %q_ref.1, bf16[256,1024]{1,0:T(8,128)(2,1)} %collective-permute-done.2.refs_0_, bf16[256,1024]{1,0:T(8,128)(2,1)} %get-tuple-element.16.refs_1_, bf16[256,1024]{1,0:T(8,128)(2,1)} %collective-permute-done.refs_2_, ...), custom_call_target="tpu_custom_call" | custom-call | flops 2684354560 | bytes 7340032 | tf_op jit(solution)/shard_map/pallas_call | solution.py:67
Async XLA Ops:
  0.0 32.7 %collective-permute-start = (bf16[256,1024]{1,0:T(8,128)(2,1)}, bf16[256,1024]{1,0:T(8,128)(2,1)}, u32[]{:S(2)}, u32[]{:S(2)}) collective-permute-start(bf16[256,1024]{1,0:T(8,128)(2,1)} %refs_4_.1), channel_id=1, source_target_pairs={{0,2},{1,3},{2,4},{3,5},{4,6},{5,7},{6,8},{7,9},{8,10},{9,11},{10,... | collective-permute-start | bytes 1572872 | tf_op jit(solution)/shard_map/ppermute | solution.py:81
  3.4 29.3 %collective-permute-start.1 = (bf16[256,1024]{1,0:T(8,128)(2,1)}, bf16[256,1024]{1,0:T(8,128)(2,1)S(1)}, u32[]{:S(2)}, u32[]{:S(2)}) collective-permute-start(bf16[256,1024]{1,0:T(8,128)(2,1)} %refs_4_.1), channel_id=1, source_target_pairs={{0,1},{2,3},{4,5},{6,7},{8,9},{10,11},{12,13},{14,15},{16,17},{18,... | collective-permute-start | bytes 1572872 | tf_op jit(solution)/shard_map/ppermute | solution.py:81
  6.9 43.4 %collective-permute-start.5 = (bf16[256,1024]{1,0:T(8,128)(2,1)}, bf16[256,1024]{1,0:T(8,128)(2,1)}, u32[]{:S(2)}, u32[]{:S(2)}) collective-permute-start(bf16[256,1024]{1,0:T(8,128)(2,1)} %refs_9_.1), channel_id=1, source_target_pairs={{0,2},{1,3},{2,4},{3,5},{4,6},{5,7},{6,8},{7,9},{8,10},{9,11},{10,... | collective-permute-start | bytes 1572872 | tf_op jit(solution)/shard_map/ppermute | solution.py:81
  10.3 40.0 %collective-permute-start.6 = (bf16[256,1024]{1,0:T(8,128)(2,1)}, bf16[256,1024]{1,0:T(8,128)(2,1)S(1)}, u32[]{:S(2)}, u32[]{:S(2)}) collective-permute-start(bf16[256,1024]{1,0:T(8,128)(2,1)} %refs_9_.1), channel_id=1, source_target_pairs={{0,1},{2,3},{4,5},{6,7},{8,9},{10,11},{12,13},{14,15},{16,17},{18,... | collective-permute-start | bytes 1572872 | tf_op jit(solution)/shard_map/ppermute | solution.py:81
  32.7 50.7 %collective-permute-start.2 = (bf16[256,1024]{1,0:T(8,128)(2,1)}, bf16[256,1024]{1,0:T(8,128)(2,1)}, u32[]{:S(2)}, u32[]{:S(2)}) collective-permute-start(bf16[256,1024]{1,0:T(8,128)(2,1)} %collective-permute-done.refs_2_), channel_id=1, source_target_pairs={{0,2},{1,3},{2,4},{3,5},{4,6},{5,7},{6,8},{7,9},{8,10},{9,11},{10,... | collective-permute-start | bytes 1572872 | tf_op jit(solution)/shard_map/ppermute | solution.py:81
  50.3 39.0 %collective-permute-start.7 = (bf16[256,1024]{1,0:T(8,128)(2,1)}, bf16[256,1024]{1,0:T(8,128)(2,1)}, u32[]{:S(2)}, u32[]{:S(2)}) collective-permute-start(bf16[256,1024]{1,0:T(8,128)(2,1)} %collective-permute-done.5.refs_7_), channel_id=1, source_target_pairs={{0,2},{1,3},{2,4},{3,5},{4,6},{5,7},{6,8},{7,9},{8,10},{9,11},{10,... | collective-permute-start | bytes 1572872 | tf_op jit(solution)/shard_map/ppermute | solution.py:81
  52.3 38.9 %collective-permute-start.3 = (bf16[256,1024]{1,0:T(8,128)(2,1)}, bf16[256,1024]{1,0:T(8,128)(2,1)S(1)}, u32[]{:S(2)}, u32[]{:S(2)}) collective-permute-start(bf16[256,1024]{1,0:T(8,128)(2,1)} %collective-permute-done.refs_2_), channel_id=1, source_target_pairs={{0,1},{1,0},{2,3},{3,2},{4,5},{5,4},{6,7},{7,6},{8,9},{9,8},{10,11... | collective-permute-start | bytes 1572872 | tf_op jit(solution)/shard_map/ppermute | solution.py:81
  83.4 11.3 %collective-permute-start.4 = (bf16[256,1024]{1,0:T(8,128)(2,1)}, bf16[256,1024]{1,0:T(8,128)(2,1)S(1)}, u32[]{:S(2)}, u32[]{:S(2)}) collective-permute-start(bf16[256,1024]{1,0:T(8,128)(2,1)} %collective-permute-done.2.refs_0_), channel_id=1, source_target_pairs={{1,0},{3,2},{5,4},{7,6},{9,8},{11,10},{13,12},{15,14},{17,16},{19,... | collective-permute-start | bytes 1572872 | tf_op jit(solution)/shard_map/ppermute | solution.py:81
  84.7 15.6 %collective-permute-start.8 = (bf16[256,1024]{1,0:T(8,128)(2,1)}, bf16[256,1024]{1,0:T(8,128)(2,1)S(1)}, u32[]{:S(2)}, u32[]{:S(2)}) collective-permute-start(bf16[256,1024]{1,0:T(8,128)(2,1)} %collective-permute-done.5.refs_7_), channel_id=1, source_target_pairs={{0,1},{1,0},{2,3},{3,2},{4,5},{5,4},{6,7},{7,6},{8,9},{9,8},{10,11... | collective-permute-start | bytes 1572872 | tf_op jit(solution)/shard_map/ppermute | solution.py:81
  89.3 16.6 %collective-permute-start.9 = (bf16[256,1024]{1,0:T(8,128)(2,1)}, bf16[256,1024]{1,0:T(8,128)(2,1)S(1)}, u32[]{:S(2)}, u32[]{:S(2)}) collective-permute-start(bf16[256,1024]{1,0:T(8,128)(2,1)} %collective-permute-done.7.refs_5_), channel_id=1, source_target_pairs={{1,0},{3,2},{5,4},{7,6},{9,8},{11,10},{13,12},{15,14},{17,16},{19,... | collective-permute-start | bytes 1572872 | tf_op jit(solution)/shard_map/ppermute | solution.py:81

commit v6 on v4

--- a/solution.py
+++ b/solution.py
@@ -78,16 +78,16 @@
             l_out[...] = jnp.where(here, total, l_out[...])
 
 
-def attend_step(kinds, first, last, valid, queries, kv_blocks, state):
+def attend_step(kinds, first, last, valid, queries, k_blocks, v_blocks, state):
     tok = queries.shape[0]
     nblk = len(kinds)
     k_spec = pl.BlockSpec((tok, HEAD_DIM), lambda h: (0, h))
-    v_spec = pl.BlockSpec((tok, HEAD_DIM), lambda h: (0, KV_HEADS + h))
+    v_spec = k_spec
     q_spec = pl.BlockSpec((tok, GROUP * HEAD_DIM), lambda h: (0, h))
     stat_spec = pl.BlockSpec((tok, HEADS), lambda h: (0, 0))
     in_specs = [pl.BlockSpec(memory_space=pltpu.SMEM), q_spec]
     in_specs += [k_spec] * nblk + [v_spec] * nblk
-    args = [valid, queries, *kv_blocks, *kv_blocks]
+    args = [valid, queries, *k_blocks, *v_blocks]
     if not first:
         in_specs += [stat_spec, stat_spec, q_spec]
         args += list(state)
@@ -102,7 +102,7 @@
             jax.ShapeDtypeStruct(queries.shape, jnp.float32),
         ]
     flops = 4 * HEADS * tok * tok * nblk * HEAD_DIM
-    nbytes = 2 * queries.size * (2 if last else 1) + 2 * nblk * kv_blocks[0].size
+    nbytes = 2 * queries.size * (2 if last else 1) + 4 * nblk * k_blocks[0].size
     nbytes += (0 if first else 4 * queries.size) + (0 if last else 4 * queries.size)
     return pl.pallas_call(
         functools.partial(step_kernel, tuple(kinds), first, last),
@@ -129,21 +129,26 @@
     n = lax.axis_size(axis)
     d = lax.axis_index(axis)
     odd = (d % 2) == 1
-    own = jnp.concatenate([keys, values], axis=1)
+    own = (keys, values)
     ahead2 = [(i, i + 2) for i in range(n) if i + 2 < n]
     x1 = shifted(own, axis, ahead2)
     y1 = shifted(own, axis, [(i, i + 1) for i in range(0, n, 2)])
-    x1, y1 = lax.optimization_barrier((x1, y1))
     x2 = shifted(x1, axis, ahead2)
     y2 = shifted(x1, axis, [(i, i ^ 1) for i in range(n)])
     y3 = shifted(x2, axis, [(i, i - 1) for i in range(1, n, 2)])
 
+    first = [own, x1, y1]
     v1 = flags(d >= 0, d >= 2, odd)
-    state = attend_step((LOWER, WHOLE, WHOLE), True, False, v1, queries, [own, x1, y1], None)
-    v2 = flags(d >= 4, d >= jnp.where(odd, 3, 1))
-    state = attend_step((UPPER, WHOLE), False, False, v2, queries, [x2, y2], state)
-    v3 = flags(jnp.logical_not(odd) & (d >= 3))
-    return attend_step((WHOLE,), False, True, v3, queries, [y3], state)
+    state = attend_step(
+        (LOWER, WHOLE, WHOLE), True, False, v1, queries,
+        [b[0] for b in first], [b[1] for b in first], None,
+    )
+    rest = [x2, y2, y3]
+    v2 = flags(d >= 4, d >= jnp.where(odd, 3, 1), jnp.logical_not(odd) & (d >= 3))
+    return attend_step(
+        (UPPER, WHOLE, WHOLE), False, True, v2, queries,
+        [b[0] for b in rest], [b[1] for b in rest], state,
+    )
 
 
 def solution(mesh):

time: 130 us -> 114 us (0.88)
  the two profiles are of different devices: /device:TPU:504 before, /device:TPU:264 now
where the time goes in v6:
time: 114 us; the launch traced here: 113 us
  starting transfers between devices  68.6 us (60%)
  Pallas kernels  24.6 us (22%)
  waiting for transfers between devices  17.2 us (15%)
  local copies, waits for them, and re-layouts  1.32 us (1%)
  other arithmetic  1.22 us (1%)
    ppermute x10, starting transfers between devices, shifted(): return lax.ppermute(x, axis, pairs)  68.6 us
    pallas_call x2, Pallas kernels, attend_step(): pl.pallas_call(functools.partial(step_kernel, tuple(kinds), first, last),...  24.6 us
    ppermute x10, waiting for transfers between devices, shifted(): return lax.ppermute(x, axis, pairs)  17.2 us
  transfers between devices with their start and end apart: 10, of which 2 were waited for; matrix products, arithmetic and copies ran while one was open for 1% of the time, Pallas kernels for 11%

profile of v6, /device:TPU:264, one launch (start us, length us, event | category | flops | bytes accessed | tf_op | source)
XLA Modules:
  0.0 113.2 jit_solution(701981822842776207)
XLA Ops:
  0.0 3.4 %collective-permute-start = (bf16[256,1024]{1,0:T(8,128)(2,1)}, bf16[256,1024]{1,0:T(8,128)(2,1)}, u32[]{:S(2)}, u32[]{:S(2)}) collective-permute-start(bf16[256,1024]{1,0:T(8,128)(2,1)} %refs_0_.1), channel_id=1, source_target_pairs={{0,2},{1,3},{2,4},{3,5},{4,6},{5,7},{6,8},{7,9},{8,10},{9,11},{10,... | collective-permute-start | bytes 1572872 | tf_op jit(solution)/shard_map/ppermute | solution.py:120
  3.4 3.4 %collective-permute-start.4 = (bf16[256,1024]{1,0:T(8,128)(2,1)}, bf16[256,1024]{1,0:T(8,128)(2,1)}, u32[]{:S(2)}, u32[]{:S(2)}) collective-permute-start(bf16[256,1024]{1,0:T(8,128)(2,1)} %refs_3_.1), channel_id=1, source_target_pairs={{0,2},{1,3},{2,4},{3,5},{4,6},{5,7},{6,8},{7,9},{8,10},{9,11},{10,... | collective-permute-start | bytes 1572872 | tf_op jit(solution)/shard_map/ppermute | solution.py:120
  6.8 1.3 %collective-permute-start.8 = (bf16[256,1024]{1,0:T(8,128)(2,1)}, bf16[256,1024]{1,0:T(8,128)(2,1)S(1)}, u32[]{:S(2)}, u32[]{:S(2)}) collective-permute-start(bf16[256,1024]{1,0:T(8,128)(2,1)} %refs_0_.1), channel_id=1, source_target_pairs={{0,1},{2,3},{4,5},{6,7},{8,9},{10,11},{12,13},{14,15},{16,17},{18,... | collective-permute-start | bytes 1572872 | tf_op jit(solution)/shard_map/ppermute | solution.py:120
  8.1 12.5 %collective-permute-done.refs_1_ = bf16[256,1024]{1,0:T(8,128)(2,1)} collective-permute-done((bf16[256,1024]{1,0:T(8,128)(2,1)}, bf16[256,1024]{1,0:T(8,128)(2,1)}, u32[]{:S(2)}, u32[]{:S(2)}) %collective-permute-start) | collective-permute-done | bytes 524320 | tf_op jit(solution)/shard_map/ppermute | solution.py:120
  20.6 1.9 %collective-permute-start.1 = (bf16[256,1024]{1,0:T(8,128)(2,1)}, bf16[256,1024]{1,0:T(8,128)(2,1)S(1)}, u32[]{:S(2)}, u32[]{:S(2)}) collective-permute-start(bf16[256,1024]{1,0:T(8,128)(2,1)} %collective-permute-done.refs_1_), channel_id=1, source_target_pairs={{0,2},{1,3},{2,4},{3,5},{4,6},{5,7},{6,8},{7,9},{8,10},{9,11},{10,... | collective-permute-start | bytes 1572872 | tf_op jit(solution)/shard_map/ppermute | solution.py:120
  22.5 4.7 %collective-permute-done.4.refs_4_ = bf16[256,1024]{1,0:T(8,128)(2,1)} collective-permute-done((bf16[256,1024]{1,0:T(8,128)(2,1)}, bf16[256,1024]{1,0:T(8,128)(2,1)}, u32[]{:S(2)}, u32[]{:S(2)}) %collective-permute-start.4) | collective-permute-done | bytes 524320 | tf_op jit(solution)/shard_map/ppermute | solution.py:120
  27.2 4.4 %collective-permute-start.5 = (bf16[256,1024]{1,0:T(8,128)(2,1)}, bf16[256,1024]{1,0:T(8,128)(2,1)S(1)}, u32[]{:S(2)}, u32[]{:S(2)}) collective-permute-start(bf16[256,1024]{1,0:T(8,128)(2,1)} %collective-permute-done.4.refs_4_), channel_id=1, source_target_pairs={{0,2},{1,3},{2,4},{3,5},{4,6},{5,7},{6,8},{7,9},{8,10},{9,11},{10,... | collective-permute-start | bytes 1572872 | tf_op jit(solution)/shard_map/ppermute | solution.py:120
  31.6 1.3 %collective-permute-start.9 = (bf16[256,1024]{1,0:T(8,128)(2,1)}, bf16[256,1024]{1,0:T(8,128)(2,1)}, u32[]{:S(2)}, u32[]{:S(2)}) collective-permute-start(bf16[256,1024]{1,0:T(8,128)(2,1)} %refs_3_.1), channel_id=1, source_target_pairs={{0,1},{2,3},{4,5},{6,7},{8,9},{10,11},{12,13},{14,15},{16,17},{18,... | collective-permute-start | bytes 1572872 | tf_op jit(solution)/shard_map/ppermute | solution.py:120
  32.9 26.5 %collective-permute-start.2 = (bf16[256,1024]{1,0:T(8,128)(2,1)}, bf16[256,1024]{1,0:T(8,128)(2,1)S(1)}, u32[]{:S(2)}, u32[]{:S(2)}) collective-permute-start(bf16[256,1024]{1,0:T(8,128)(2,1)} %collective-permute-done.refs_1_), channel_id=1, source_target_pairs={{0,1},{1,0},{2,3},{3,2},{4,5},{5,4},{6,7},{7,6},{8,9},{9,8},{10,11... | collective-permute-start | bytes 1572872 | tf_op jit(solution)/shard_map/ppermute | solution.py:120
  59.5 0.0 collective-permute-done.8.refs_2_
  59.5 0.0 copy-start.6
  59.5 1.9 %collective-permute-start.6 = (bf16[256,1024]{1,0:T(8,128)(2,1)}, bf16[256,1024]{1,0:T(8,128)(2,1)S(1)}, u32[]{:S(2)}, u32[]{:S(2)}) collective-permute-start(bf16[256,1024]{1,0:T(8,128)(2,1)} %collective-permute-done.4.refs_4_), channel_id=1, source_target_pairs={{0,1},{1,0},{2,3},{3,2},{4,5},{5,4},{6,7},{7,6},{8,9},{9,8},{10,11... | collective-permute-start | bytes 1572872 | tf_op jit(solution)/shard_map/ppermute | solution.py:120
  61.4 0.0 collective-permute-done.1.refs_0_
  61.4 0.0 copy-start
  61.4 16.4 %collective-permute-start.3 = (bf16[256,1024]{1,0:T(8,128)(2,1)S(1)}, bf16[256,1024]{1,0:T(8,128)(2,1)S(1)}, u32[]{:S(2)}, u32[]{:S(2)}) collective-permute-start(bf16[256,1024]{1,0:T(8,128)(2,1)S(1)} %collective-permute-done.1.refs_0_), channel_id=1, source_target_pairs={{1,0},{3,2},{5,4},{7,6},{9,8},{11,10},{13,12},{15,14},{17,16},{19,... | collective-permute-start | bytes 1572872 | tf_op jit(solution)/shard_map/ppermute | solution.py:120
  77.8 0.0 collective-permute-done.5.refs_3_
  77.9 0.0 copy-done.6
  77.9 0.0 copy-start.1
  77.9 8.1 %collective-permute-start.7 = (bf16[256,1024]{1,0:T(8,128)(2,1)S(1)}, bf16[256,1024]{1,0:T(8,128)(2,1)S(1)}, u32[]{:S(2)}, u32[]{:S(2)}) collective-permute-start(bf16[256,1024]{1,0:T(8,128)(2,1)S(1)} %collective-permute-done.5.refs_3_), channel_id=1, source_target_pairs={{1,0},{3,2},{5,4},{7,6},{9,8},{11,10},{13,12},{15,14},{17,16},{19,... | collective-permute-start | bytes 1572872 | tf_op jit(solution)/shard_map/ppermute | solution.py:120
  86.0 0.6 add_convert_fusion.1.valid_ref
  86.6 0.6 add_convert_fusion.valid_ref
  87.2 0.0 collective-permute-done.9.refs_5_
  87.2 12.2 %shard_map.37 = (f32[256,16]{1,0:T(8,128)}, f32[256,16]{1,0:T(8,128)}, f32[256,2048]{1,0:T(8,128)}) custom-call(s32[3]{0:T(128)} %add_convert_fusion.1.valid_ref, bf16[256,2048]{1,0:T(8,128)(2,1)} %q_ref.3, bf16[256,1024]{1,0:T(8,128)(2,1)} %refs_0_.1, bf16[256,1024]{1,0:T(8,128)(2,1)} %collective-permute-done.refs_1_, bf16[256,1024]{1,0:T(8,128)(2,1)} %copy-done.6, ...), custom_call_target="tpu_custom_call" | custom-call | flops 1610612736 | bytes 6291456 | tf_op jit(solution)/shard_map/pallas_call | solution.py:107
  99.4 0.0 copy-done
  99.4 0.0 copy-done.1
  99.4 0.0 collective-permute-done.2.refs_1_
  99.4 0.0 copy-start.2
  99.4 0.0 collective-permute-done.6.refs_4_
  99.4 0.0 copy-start.3
  99.4 0.0 collective-permute-done.3.refs_2_
  99.4 0.0 copy-start.4
  99.4 0.0 collective-permute-done.7.refs_5_
  99.4 0.0 copy-start.5
  99.5 0.7 copy-done.2
  100.2 0.2 copy-done.3
  100.4 0.2 copy-done.4
  100.5 0.2 copy-done.5
  100.8 12.5 %shard_map.38 = bf16[256,2048]{1,0:T(8,128)(2,1)} custom-call(s32[3]{0:T(128)} %add_convert_fusion.valid_ref, bf16[256,2048]{1,0:T(8,128)(2,1)} %q_ref.3, bf16[256,1024]{1,0:T(8,128)(2,1)} %copy-done, bf16[256,1024]{1,0:T(8,128)(2,1)} %copy-done.2, bf16[256,1024]{1,0:T(8,128)(2,1)} %copy-done.4, bf16[256,1024]{1,0:T(8,128)(2,1)} %copy-done.1, ...), custom_call_target="tpu_custom_call" | custom-call | flops 1610612736 | bytes 7340032 | tf_op jit(solution)/shard_map/pallas_call | solution.py:107
Async XLA Ops:
  0.0 20.6 %collective-permute-start = (bf16[256,1024]{1,0:T(8,128)(2,1)}, bf16[256,1024]{1,0:T(8,128)(2,1)}, u32[]{:S(2)}, u32[]{:S(2)}) collective-permute-start(bf16[256,1024]{1,0:T(8,128)(2,1)} %refs_0_.1), channel_id=1, source_target_pairs={{0,2},{1,3},{2,4},{3,5},{4,6},{5,7},{6,8},{7,9},{8,10},{9,11},{10,... | collective-permute-start | bytes 1572872 | tf_op jit(solution)/shard_map/ppermute | solution.py:120
  3.4 23.8 %collective-permute-start.4 = (bf16[256,1024]{1,0:T(8,128)(2,1)}, bf16[256,1024]{1,0:T(8,128)(2,1)}, u32[]{:S(2)}, u32[]{:S(2)}) collective-permute-start(bf16[256,1024]{1,0:T(8,128)(2,1)} %refs_3_.1), channel_id=1, source_target_pairs={{0,2},{1,3},{2,4},{3,5},{4,6},{5,7},{6,8},{7,9},{8,10},{9,11},{10,... | collective-permute-start | bytes 1572872 | tf_op jit(solution)/shard_map/ppermute | solution.py:120
  6.8 52.7 %collective-permute-start.8 = (bf16[256,1024]{1,0:T(8,128)(2,1)}, bf16[256,1024]{1,0:T(8,128)(2,1)S(1)}, u32[]{:S(2)}, u32[]{:S(2)}) collective-permute-start(bf16[256,1024]{1,0:T(8,128)(2,1)} %refs_0_.1), channel_id=1, source_target_pairs={{0,1},{2,3},{4,5},{6,7},{8,9},{10,11},{12,13},{14,15},{16,17},{18,... | collective-permute-start | bytes 1572872 | tf_op jit(solution)/shard_map/ppermute | solution.py:120
  20.6 40.8 %collective-permute-start.1 = (bf16[256,1024]{1,0:T(8,128)(2,1)}, bf16[256,1024]{1,0:T(8,128)(2,1)S(1)}, u32[]{:S(2)}, u32[]{:S(2)}) collective-permute-start(bf16[256,1024]{1,0:T(8,128)(2,1)} %collective-permute-done.refs_1_), channel_id=1, source_target_pairs={{0,2},{1,3},{2,4},{3,5},{4,6},{5,7},{6,8},{7,9},{8,10},{9,11},{10,... | collective-permute-start | bytes 1572872 | tf_op jit(solution)/shard_map/ppermute | solution.py:120
  27.2 50.6 %collective-permute-start.5 = (bf16[256,1024]{1,0:T(8,128)(2,1)}, bf16[256,1024]{1,0:T(8,128)(2,1)S(1)}, u32[]{:S(2)}, u32[]{:S(2)}) collective-permute-start(bf16[256,1024]{1,0:T(8,128)(2,1)} %collective-permute-done.4.refs_4_), channel_id=1, source_target_pairs={{0,2},{1,3},{2,4},{3,5},{4,6},{5,7},{6,8},{7,9},{8,10},{9,11},{10,... | collective-permute-start | bytes 1572872 | tf_op jit(solution)/shard_map/ppermute | solution.py:120
  31.6 55.6 %collective-permute-start.9 = (bf16[256,1024]{1,0:T(8,128)(2,1)}, bf16[256,1024]{1,0:T(8,128)(2,1)}, u32[]{:S(2)}, u32[]{:S(2)}) collective-permute-start(bf16[256,1024]{1,0:T(8,128)(2,1)} %refs_3_.1), channel_id=1, source_target_pairs={{0,1},{2,3},{4,5},{6,7},{8,9},{10,11},{12,13},{14,15},{16,17},{18,... | collective-permute-start | bytes 1572872 | tf_op jit(solution)/shard_map/ppermute | solution.py:120
  32.9 66.4 %collective-permute-start.2 = (bf16[256,1024]{1,0:T(8,128)(2,1)}, bf16[256,1024]{1,0:T(8,128)(2,1)S(1)}, u32[]{:S(2)}, u32[]{:S(2)}) collective-permute-start(bf16[256,1024]{1,0:T(8,128)(2,1)} %collective-permute-done.refs_1_), channel_id=1, source_target_pairs={{0,1},{1,0},{2,3},{3,2},{4,5},{5,4},{6,7},{7,6},{8,9},{9,8},{10,11... | collective-permute-start | bytes 1572872 | tf_op jit(solution)/shard_map/ppermute | solution.py:120
  59.5 18.4 %copy-start.6 = (bf16[256,1024]{1,0:T(8,128)(2,1)}, bf16[256,1024]{1,0:T(8,128)(2,1)S(1)}, u32[]{:S(2)}) copy-start(bf16[256,1024]{1,0:T(8,128)(2,1)S(1)} %collective-permute-done.8.refs_2_) | copy-start | bytes 1572868
  59.5 39.9 %collective-permute-start.6 = (bf16[256,1024]{1,0:T(8,128)(2,1)}, bf16[256,1024]{1,0:T(8,128)(2,1)S(1)}, u32[]{:S(2)}, u32[]{:S(2)}) collective-permute-start(bf16[256,1024]{1,0:T(8,128)(2,1)} %collective-permute-done.4.refs_4_), channel_id=1, source_target_pairs={{0,1},{1,0},{2,3},{3,2},{4,5},{5,4},{6,7},{7,6},{8,9},{9,8},{10,11... | collective-permute-start | bytes 1572872 | tf_op jit(solution)/shard_map/ppermute | solution.py:120
  61.4 37.9 %copy-start = (bf16[256,1024]{1,0:T(8,128)(2,1)}, bf16[256,1024]{1,0:T(8,128)(2,1)S(1)}, u32[]{:S(2)}) copy-start(bf16[256,1024]{1,0:T(8,128)(2,1)S(1)} %collective-permute-done.1.refs_0_) | copy-start | bytes 1572868
  61.4 38.0 %collective-permute-start.3 = (bf16[256,1024]{1,0:T(8,128)(2,1)S(1)}, bf16[256,1024]{1,0:T(8,128)(2,1)S(1)}, u32[]{:S(2)}, u32[]{:S(2)}) collective-permute-start(bf16[256,1024]{1,0:T(8,128)(2,1)S(1)} %collective-permute-done.1.refs_0_), channel_id=1, source_target_pairs={{1,0},{3,2},{5,4},{7,6},{9,8},{11,10},{13,12},{15,14},{17,16},{19,... | collective-permute-start | bytes 1572872 | tf_op jit(solution)/shard_map/ppermute | solution.py:120
  77.9 21.5 %copy-start.1 = (bf16[256,1024]{1,0:T(8,128)(2,1)}, bf16[256,1024]{1,0:T(8,128)(2,1)S(1)}, u32[]{:S(2)}) copy-start(bf16[256,1024]{1,0:T(8,128)(2,1)S(1)} %collective-permute-done.5.refs_3_) | copy-start | bytes 1572868
  77.9 21.6 %collective-permute-start.7 = (bf16[256,1024]{1,0:T(8,128)(2,1)S(1)}, bf16[256,1024]{1,0:T(8,128)(2,1)S(1)}, u32[]{:S(2)}, u32[]{:S(2)}) collective-permute-start(bf16[256,1024]{1,0:T(8,128)(2,1)S(1)} %collective-permute-done.5.refs_3_), channel_id=1, source_target_pairs={{1,0},{3,2},{5,4},{7,6},{9,8},{11,10},{13,12},{15,14},{17,16},{19,... | collective-permute-start | bytes 1572872 | tf_op jit(solution)/shard_map/ppermute | solution.py:120
  99.4 0.8 copy-start.2
  99.4 0.9 copy-start.3
  99.4 1.1 copy-start.4
  99.4 1.3 %copy-start.5 = (bf16[256,1024]{1,0:T(8,128)(2,1)}, bf16[256,1024]{1,0:T(8,128)(2,1)S(1)}, u32[]{:S(2)}) copy-start(bf16[256,1024]{1,0:T(8,128)(2,1)S(1)} %collective-permute-done.7.refs_5_) | copy-start | bytes 1572868

commit v7 on v3

--- a/solution.py
+++ b/solution.py
@@ -91,15 +91,21 @@
     n = lax.axis_size(axis)
     block_index = lax.axis_index(axis)
     own = jnp.concatenate([keys, values], axis=1)
+    tok = own.shape[0]
     ahead2 = [(i, i + 2) for i in range(n) if i + 2 < n]
+    pairs = [[i, i + 1] for i in range(0, lax.axis_size("grp"), 2)]
+
+    def pair_gather(x):
+        return lax.all_gather(x, "grp", axis_index_groups=pairs, axis=0, tiled=True)
+
     x1 = shifted(own, axis, ahead2)
-    y1 = shifted(own, axis, [(i, i + 1) for i in range(0, n, 2)])
+    y1 = pair_gather(own)
     x2 = shifted(x1, axis, ahead2)
-    y2 = shifted(x1, axis, [(i, i ^ 1) for i in range(n)])
-    y3 = shifted(x2, axis, [(i, i - 1) for i in range(1, n, 2)])
+    y2 = pair_gather(x1)
+    y3 = pair_gather(x2)
     odd = (block_index % 2) == 1
-    b1 = jnp.where(odd, y1, y2)
-    b3 = jnp.where(odd, y2, y3)
+    b1 = jnp.where(odd, y1[:tok], y2[tok:])
+    b3 = jnp.where(odd, y2[:tok], y3[tok:])
     back_blocks = WINDOW // queries.shape[0]
     nblk = back_blocks + 1
     valid = (block_index + jnp.arange(nblk, dtype=jnp.int32) >= back_blocks).astype(jnp.int32)

time: 122 us -> 197 us (1.61)
  the two profiles are of different devices: /device:TPU:255 before, /device:TPU:1 now
where the time goes in v7:
time: 197 us
  waiting for transfers between devices  148 us (75%)
  Pallas kernels  15.6 us (8%)
  between operations  13.2 us (7%)
  starting transfers between devices  10.4 us (5%)
  local copies, waits for them, and re-layouts  5.23 us (3%)
  other arithmetic  4.29 us (2%)
    all_gather x3, waiting for transfers between devices, pair_gather(): return lax.all_gather(x, 'grp', axis_index_groups=pairs, axis=0, tiled=True)  109 us
    ppermute x2, waiting for transfers between devices, shifted(): return lax.ppermute(x, axis, pairs)  39.3 us
    pallas_call x1, Pallas kernels, attend(): pl.pallas_call(attend_kernel, grid=(KV_HEADS,), in_specs=[pl.BlockSpec(me...  15.6 us
    ppermute x2, starting transfers between devices, shifted(): return lax.ppermute(x, axis, pairs)  10.3 us
    unnamed x7, local copies, waits for them, and re-layouts  4.15 us
  transfers between devices with their start and end apart: 5, of which 4 were waited for; matrix products, arithmetic and copies ran while one was open for 0% of the time, Pallas kernels for 0%

profile of v7, /device:TPU:1, one launch (start us, length us, event | category | flops | bytes accessed | tf_op | source)
XLA Modules:
  0.0 197.1 jit_solution(10847510375915652115)
XLA Ops:
  6.5 0.0 all-gather.8.cloned.1.call-start
  6.5 1.1 constant_dynamic-update-slice_fusion.1
  7.6 1.1 constant_dynamic-update-slice_fusion.refs_4_.refs_9_
  8.7 0.0 copy-start
  8.7 1.0 copy-done
  9.7 0.0 all-gather.8.cloned.1.call-update
  9.7 0.0 all-gather.4.cloned.1.call-start
  9.8 3.9 %collective-permute-start = (bf16[256,2048]{1,0:T(8,128)(2,1)}, bf16[256,2048]{1,0:T(8,128)(2,1)S(1)}, u32[]{:S(2)}, u32[]{:S(2)}) collective-permute-start(bf16[256,2048]{1,0:T(8,128)(2,1)} %copy-done), channel_id=1, source_target_pairs={{0,2},{1,3},{2,4},{3,5},{4,6},{5,7},{6,8},{7,9},{8,10},{9,11},{10,... | collective-permute-start | bytes 3145736 | tf_op jit(solution)/shard_map/ppermute | solution.py:86
  13.7 18.9 %collective-permute-done.refs_2_.refs_7_ = bf16[256,2048]{1,0:T(8,128)(2,1)S(1)} collective-permute-done((bf16[256,2048]{1,0:T(8,128)(2,1)}, bf16[256,2048]{1,0:T(8,128)(2,1)S(1)}, u32[]{:S(2)}, u32[]{:S(2)}) %collective-permute-start) | collective-permute-done | bytes 1048608 | tf_op jit(solution)/shard_map/ppermute | solution.py:86
  32.6 0.0 copy-start.1
  32.6 1.0 copy-done.1
  33.6 0.0 all-gather.4.cloned.1.call-update
  33.7 0.0 all-gather.6.cloned.1.call-start
  33.7 6.4 %collective-permute-start.1 = (bf16[256,2048]{1,0:T(8,128)(2,1)}, bf16[256,2048]{1,0:T(8,128)(2,1)S(1)}, u32[]{:S(2)}, u32[]{:S(2)}) collective-permute-start(bf16[256,2048]{1,0:T(8,128)(2,1)} %copy-done.1), channel_id=1, source_target_pairs={{0,2},{1,3},{2,4},{3,5},{4,6},{5,7},{6,8},{7,9},{8,10},{9,11},{10,... | collective-permute-start | bytes 3145736 | tf_op jit(solution)/shard_map/ppermute | solution.py:86
  40.1 20.4 %collective-permute-done.1.refs_0_.refs_5_ = bf16[256,2048]{1,0:T(8,128)(2,1)S(1)} collective-permute-done((bf16[256,2048]{1,0:T(8,128)(2,1)}, bf16[256,2048]{1,0:T(8,128)(2,1)S(1)}, u32[]{:S(2)}, u32[]{:S(2)}) %collective-permute-start.1) | collective-permute-done | bytes 1048608 | tf_op jit(solution)/shard_map/ppermute | solution.py:86
  60.5 0.0 copy-start.2
  60.5 1.1 copy-done.2
  61.5 0.0 all-gather.6.cloned.1.call-update
  61.6 0.6 compare_convert_fusion.valid_ref
  62.2 0.0 all-gather.8.cloned.1.call-done
  62.2 65.5 %all-gather.4.cloned.1.call-done = bf16[512,2048]{1,0:T(8,128)(2,1)} async-done(((bf16[256,2048]{1,0:T(8,128)(2,1)}), bf16[512,2048]{1,0:T(8,128)(2,1)}) %all-gather.4.cloned.1.call-update) | async-done | bytes 2097168 | tf_op jit(solution)/shard_map/all_gather | solution.py:99
  127.7 43.5 %all-gather.6.cloned.1.call-done = bf16[512,2048]{1,0:T(8,128)(2,1)} async-done(((bf16[256,2048]{1,0:T(8,128)(2,1)}), bf16[512,2048]{1,0:T(8,128)(2,1)}) %all-gather.6.cloned.1.call-update) | async-done | bytes 2097168 | tf_op jit(solution)/shard_map/all_gather | solution.py:99
  171.2 3.7 %slice_select_fusion = (bf16[256,2048]{1,0:T(8,128)(2,1)}, bf16[256,2048]{1,0:T(8,128)(2,1)}) fusion(bf16[512,2048]{1,0:T(8,128)(2,1)} %all-gather.4.cloned.1.call-done, bf16[512,2048]{1,0:T(8,128)(2,1)} %all-gather.8.cloned.1.call-done, pred[]{:T(512)S(6)} %eq.5, bf16[512,2048]{1,0:T(8,128)(2,1)} %all-gather.6.cloned.1.call-done), kind=kLoop, calls=%fused_computation | loop fusion | flops 1048576 | bytes 6291457 | tf_op jit(solution)/shard_map/jit(_where)/select_n | solution.py:107
  174.9 15.6 %shard_map.37 = bf16[256,2048]{1,0:T(8,128)(2,1)} custom-call(s32[5]{0:T(128)} %compare_convert_fusion.valid_ref, bf16[256,2048]{1,0:T(8,128)(2,1)} %q_ref.1, bf16[256,2048]{1,0:T(8,128)(2,1)} %copy-done.2, bf16[256,2048]{1,0:T(8,128)(2,1)} %get-tuple-element.6.refs_1_.refs_6_, bf16[256,2048]{1,0:T(8,128)(2,1)} %copy-done.1, ...), custom_call_target="tpu_custom_call" | custom-call | flops 2684354560 | bytes 7340032 | tf_op jit(solution)/shard_map/pallas_call | solution.py:68
Async XLA Ops:
  6.5 55.6 %all-gather.8.cloned.1.call-start = ((), (), s32[]{:S(2)}) async-start(), calls=%async_computation.2 | async-start | bytes 3145728 | tf_op jit(solution)/shard_map/all_gather | solution.py:99
  8.7 1.0 copy-start
  9.7 118.0 %all-gather.4.cloned.1.call-start = ((), (), s32[]{:S(2)}) async-start(), calls=%async_computation | async-start | bytes 3145728 | tf_op jit(solution)/shard_map/all_gather | solution.py:99
  9.8 22.8 %collective-permute-start = (bf16[256,2048]{1,0:T(8,128)(2,1)}, bf16[256,2048]{1,0:T(8,128)(2,1)S(1)}, u32[]{:S(2)}, u32[]{:S(2)}) collective-permute-start(bf16[256,2048]{1,0:T(8,128)(2,1)} %copy-done), channel_id=1, source_target_pairs={{0,2},{1,3},{2,4},{3,5},{4,6},{5,7},{6,8},{7,9},{8,10},{9,11},{10,... | collective-permute-start | bytes 3145736 | tf_op jit(solution)/shard_map/ppermute | solution.py:86
  32.6 1.0 copy-start.1
  33.7 137.5 %all-gather.6.cloned.1.call-start = ((), (), s32[]{:S(2)}) async-start(), calls=%async_computation.1 | async-start | bytes 3145728 | tf_op jit(solution)/shard_map/all_gather | solution.py:99
  33.7 26.8 %collective-permute-start.1 = (bf16[256,2048]{1,0:T(8,128)(2,1)}, bf16[256,2048]{1,0:T(8,128)(2,1)S(1)}, u32[]{:S(2)}, u32[]{:S(2)}) collective-permute-start(bf16[256,2048]{1,0:T(8,128)(2,1)} %copy-done.1), channel_id=1, source_target_pairs={{0,2},{1,3},{2,4},{3,5},{4,6},{5,7},{6,8},{7,9},{8,10},{9,11},{10,... | collective-permute-start | bytes 3145736 | tf_op jit(solution)/shard_map/ppermute | solution.py:86
  60.5 1.1 copy-start.2
Sparse Core Ops, SparseCore 0:
  9.9 46.2 all-gather.7
  58.3 69.3 all-gather.3
  129.8 41.3 all-gather.5

commit v8 on v2

--- a/solution.py
+++ b/solution.py
@@ -90,7 +90,8 @@
     x1 = shifted(own, axis, ahead2)
     y1 = shifted(own, axis, [(i, i + 1) for i in range(0, n, 2)])
     x2 = shifted(x1, axis, ahead2)
-    y2 = shifted(x1, axis, [(i, i ^ 1) for i in range(n)])
+    x1_fenced = tuple(lax.optimization_barrier((a, b))[0] for a, b in zip(x1, y1))
+    y2 = shifted(x1_fenced, axis, [(i, i ^ 1) for i in range(n)])
     y3 = shifted(x2, axis, [(i, i - 1) for i in range(1, n, 2)])
     odd = (block_index % 2) == 1
     b1 = [jnp.where(odd, a, b) for a, b in zip(y1, y2)]

time: 116 us -> 118 us (1.017)
  the two profiles are of different devices: /device:TPU:207 before, /device:TPU:256 now
where the time goes in v8:
time: 118 us; the launch traced here: 117 us
  waiting for transfers between devices  74.3 us (63%)
  starting transfers between devices  24.5 us (21%)
  Pallas kernels  15.5 us (13%)
  other arithmetic  2.7 us (2%)
    ppermute x10, waiting for transfers between devices, shifted(): return lax.ppermute(x, axis, pairs)  74.3 us
    ppermute x10, starting transfers between devices, shifted(): return lax.ppermute(x, axis, pairs)  24.5 us
    pallas_call x1, Pallas kernels, attend(): pl.pallas_call(attend_kernel, grid=(KV_HEADS,), in_specs=[pl.BlockSpec(me...  15.5 us
  transfers between devices with their start and end apart: 10, of which 6 were waited for; matrix products, arithmetic and copies ran while one was open for 1% of the time, Pallas kernels for 0%

profile of v8, /device:TPU:256, one launch (start us, length us, event | category | flops | bytes accessed | tf_op | source)
XLA Modules:
  0.0 117.2 jit_solution(1047796513966945064)
XLA Ops:
  0.0 3.4 %collective-permute-start = (bf16[256,1024]{1,0:T(8,128)(2,1)}, bf16[256,1024]{1,0:T(8,128)(2,1)}, u32[]{:S(2)}, u32[]{:S(2)}) collective-permute-start(bf16[256,1024]{1,0:T(8,128)(2,1)} %refs_4_.1), channel_id=1, source_target_pairs={{0,2},{1,3},{2,4},{3,5},{4,6},{5,7},{6,8},{7,9},{8,10},{9,11},{10,... | collective-permute-start | bytes 1572872 | tf_op jit(solution)/shard_map/ppermute | solution.py:81
  3.4 3.4 %collective-permute-start.5 = (bf16[256,1024]{1,0:T(8,128)(2,1)}, bf16[256,1024]{1,0:T(8,128)(2,1)}, u32[]{:S(2)}, u32[]{:S(2)}) collective-permute-start(bf16[256,1024]{1,0:T(8,128)(2,1)} %refs_9_.1), channel_id=1, source_target_pairs={{0,2},{1,3},{2,4},{3,5},{4,6},{5,7},{6,8},{7,9},{8,10},{9,11},{10,... | collective-permute-start | bytes 1572872 | tf_op jit(solution)/shard_map/ppermute | solution.py:81
  6.8 3.5 %collective-permute-start.2 = (bf16[256,1024]{1,0:T(8,128)(2,1)}, bf16[256,1024]{1,0:T(8,128)(2,1)S(1)}, u32[]{:S(2)}, u32[]{:S(2)}) collective-permute-start(bf16[256,1024]{1,0:T(8,128)(2,1)} %refs_4_.1), channel_id=1, source_target_pairs={{0,1},{2,3},{4,5},{6,7},{8,9},{10,11},{12,13},{14,15},{16,17},{18,... | collective-permute-start | bytes 1572872 | tf_op jit(solution)/shard_map/ppermute | solution.py:81
  10.3 21.7 %collective-permute-done.refs_2_ = bf16[256,1024]{1,0:T(8,128)(2,1)} collective-permute-done((bf16[256,1024]{1,0:T(8,128)(2,1)}, bf16[256,1024]{1,0:T(8,128)(2,1)}, u32[]{:S(2)}, u32[]{:S(2)}) %collective-permute-start) | collective-permute-done | bytes 524320 | tf_op jit(solution)/shard_map/ppermute | solution.py:81
  32.0 1.9 %collective-permute-start.1 = (bf16[256,1024]{1,0:T(8,128)(2,1)}, bf16[256,1024]{1,0:T(8,128)(2,1)}, u32[]{:S(2)}, u32[]{:S(2)}) collective-permute-start(bf16[256,1024]{1,0:T(8,128)(2,1)} %collective-permute-done.refs_2_), channel_id=1, source_target_pairs={{0,2},{1,3},{2,4},{3,5},{4,6},{5,7},{6,8},{7,9},{8,10},{9,11},{10,... | collective-permute-start | bytes 1572872 | tf_op jit(solution)/shard_map/ppermute | solution.py:81
  34.0 1.3 %collective-permute-start.7 = (bf16[256,1024]{1,0:T(8,128)(2,1)}, bf16[256,1024]{1,0:T(8,128)(2,1)S(1)}, u32[]{:S(2)}, u32[]{:S(2)}) collective-permute-start(bf16[256,1024]{1,0:T(8,128)(2,1)} %refs_9_.1), channel_id=1, source_target_pairs={{0,1},{2,3},{4,5},{6,7},{8,9},{10,11},{12,13},{14,15},{16,17},{18,... | collective-permute-start | bytes 1572872 | tf_op jit(solution)/shard_map/ppermute | solution.py:81
  35.3 17.8 %collective-permute-done.5.refs_7_ = bf16[256,1024]{1,0:T(8,128)(2,1)} collective-permute-done((bf16[256,1024]{1,0:T(8,128)(2,1)}, bf16[256,1024]{1,0:T(8,128)(2,1)}, u32[]{:S(2)}, u32[]{:S(2)}) %collective-permute-start.5) | collective-permute-done | bytes 524320 | tf_op jit(solution)/shard_map/ppermute | solution.py:81
  53.1 1.9 %collective-permute-start.6 = (bf16[256,1024]{1,0:T(8,128)(2,1)}, bf16[256,1024]{1,0:T(8,128)(2,1)}, u32[]{:S(2)}, u32[]{:S(2)}) collective-permute-start(bf16[256,1024]{1,0:T(8,128)(2,1)} %collective-permute-done.5.refs_7_), channel_id=1, source_target_pairs={{0,2},{1,3},{2,4},{3,5},{4,6},{5,7},{6,8},{7,9},{8,10},{9,11},{10,... | collective-permute-start | bytes 1572872 | tf_op jit(solution)/shard_map/ppermute | solution.py:81
  55.0 0.0 collective-permute-done.2
  55.0 1.9 %collective-permute-start.3 = (bf16[256,1024]{1,0:T(8,128)(2,1)}, bf16[256,1024]{1,0:T(8,128)(2,1)S(1)}, u32[]{:S(2)}, u32[]{:S(2)}) collective-permute-start(bf16[256,1024]{1,0:T(8,128)(2,1)} %collective-permute-done.refs_2_), channel_id=1, source_target_pairs={{0,1},{1,0},{2,3},{3,2},{4,5},{5,4},{6,7},{7,6},{8,9},{9,8},{10,11... | collective-permute-start | bytes 1572872 | tf_op jit(solution)/shard_map/ppermute | solution.py:81
  57.0 18.6 %collective-permute-done.1.refs_0_ = bf16[256,1024]{1,0:T(8,128)(2,1)} collective-permute-done((bf16[256,1024]{1,0:T(8,128)(2,1)}, bf16[256,1024]{1,0:T(8,128)(2,1)}, u32[]{:S(2)}, u32[]{:S(2)}) %collective-permute-start.1) | collective-permute-done | bytes 524320 | tf_op jit(solution)/shard_map/ppermute | solution.py:81
  75.6 1.3 %collective-permute-start.4 = (bf16[256,1024]{1,0:T(8,128)(2,1)}, bf16[256,1024]{1,0:T(8,128)(2,1)S(1)}, u32[]{:S(2)}, u32[]{:S(2)}) collective-permute-start(bf16[256,1024]{1,0:T(8,128)(2,1)} %collective-permute-done.1.refs_0_), channel_id=1, source_target_pairs={{1,0},{3,2},{5,4},{7,6},{9,8},{11,10},{13,12},{15,14},{17,16},{19,... | collective-permute-start | bytes 1572872 | tf_op jit(solution)/shard_map/ppermute | solution.py:81
  76.9 0.0 collective-permute-done.7
  76.9 4.6 %collective-permute-start.8 = (bf16[256,1024]{1,0:T(8,128)(2,1)}, bf16[256,1024]{1,0:T(8,128)(2,1)S(1)}, u32[]{:S(2)}, u32[]{:S(2)}) collective-permute-start(bf16[256,1024]{1,0:T(8,128)(2,1)} %collective-permute-done.5.refs_7_), channel_id=1, source_target_pairs={{0,1},{1,0},{2,3},{3,2},{4,5},{5,4},{6,7},{7,6},{8,9},{9,8},{10,11... | collective-permute-start | bytes 1572872 | tf_op jit(solution)/shard_map/ppermute | solution.py:81
  81.5 7.8 %collective-permute-done.6.refs_5_ = bf16[256,1024]{1,0:T(8,128)(2,1)} collective-permute-done((bf16[256,1024]{1,0:T(8,128)(2,1)}, bf16[256,1024]{1,0:T(8,128)(2,1)}, u32[]{:S(2)}, u32[]{:S(2)}) %collective-permute-start.6) | collective-permute-done | bytes 524320 | tf_op jit(solution)/shard_map/ppermute | solution.py:81
  89.3 1.3 %collective-permute-start.9 = (bf16[256,1024]{1,0:T(8,128)(2,1)}, bf16[256,1024]{1,0:T(8,128)(2,1)S(1)}, u32[]{:S(2)}, u32[]{:S(2)}) collective-permute-start(bf16[256,1024]{1,0:T(8,128)(2,1)} %collective-permute-done.6.refs_5_), channel_id=1, source_target_pairs={{1,0},{3,2},{5,4},{7,6},{9,8},{11,10},{13,12},{15,14},{17,16},{19,... | collective-permute-start | bytes 1572872 | tf_op jit(solution)/shard_map/ppermute | solution.py:81
  90.6 0.5 compare_convert_fusion.valid_ref
  91.1 0.0 collective-permute-done.3
  91.1 0.0 collective-permute-done.4
  91.1 1.1 broadcast_select_fusion.2
  92.2 0.3 collective-permute-done.8
  92.5 8.1 %collective-permute-done.9 = bf16[256,1024]{1,0:T(8,128)(2,1)S(1)} collective-permute-done((bf16[256,1024]{1,0:T(8,128)(2,1)}, bf16[256,1024]{1,0:T(8,128)(2,1)S(1)}, u32[]{:S(2)}, u32[]{:S(2)}) %collective-permute-start.9) | collective-permute-done | bytes 524320 | tf_op jit(solution)/shard_map/ppermute | solution.py:81
  100.6 1.1 broadcast_select_fusion
  101.6 15.5 %shard_map.37 = bf16[256,2048]{1,0:T(8,128)(2,1)} custom-call(s32[5]{0:T(128)} %compare_convert_fusion.valid_ref, bf16[256,2048]{1,0:T(8,128)(2,1)} %q_ref.1, bf16[256,1024]{1,0:T(8,128)(2,1)} %collective-permute-done.1.refs_0_, bf16[256,1024]{1,0:T(8,128)(2,1)} %get-tuple-element.12.refs_1_, bf16[256,1024]{1,0:T(8,128)(2,1)} %collective-permute-done.refs_2_, ...), custom_call_target="tpu_custom_call" | custom-call | flops 2684354560 | bytes 7340032 | tf_op jit(solution)/shard_map/pallas_call | solution.py:67
Async XLA Ops:
  0.0 32.0 %collective-permute-start = (bf16[256,1024]{1,0:T(8,128)(2,1)}, bf16[256,1024]{1,0:T(8,128)(2,1)}, u32[]{:S(2)}, u32[]{:S(2)}) collective-permute-start(bf16[256,1024]{1,0:T(8,128)(2,1)} %refs_4_.1), channel_id=1, source_target_pairs={{0,2},{1,3},{2,4},{3,5},{4,6},{5,7},{6,8},{7,9},{8,10},{9,11},{10,... | collective-permute-start | bytes 1572872 | tf_op jit(solution)/shard_map/ppermute | solution.py:81
  3.4 49.7 %collective-permute-start.5 = (bf16[256,1024]{1,0:T(8,128)(2,1)}, bf16[256,1024]{1,0:T(8,128)(2,1)}, u32[]{:S(2)}, u32[]{:S(2)}) collective-permute-start(bf16[256,1024]{1,0:T(8,128)(2,1)} %refs_9_.1), channel_id=1, source_target_pairs={{0,2},{1,3},{2,4},{3,5},{4,6},{5,7},{6,8},{7,9},{8,10},{9,11},{10,... | collective-permute-start | bytes 1572872 | tf_op jit(solution)/shard_map/ppermute | solution.py:81
  6.8 48.2 %collective-permute-start.2 = (bf16[256,1024]{1,0:T(8,128)(2,1)}, bf16[256,1024]{1,0:T(8,128)(2,1)S(1)}, u32[]{:S(2)}, u32[]{:S(2)}) collective-permute-start(bf16[256,1024]{1,0:T(8,128)(2,1)} %refs_4_.1), channel_id=1, source_target_pairs={{0,1},{2,3},{4,5},{6,7},{8,9},{10,11},{12,13},{14,15},{16,17},{18,... | collective-permute-start | bytes 1572872 | tf_op jit(solution)/shard_map/ppermute | solution.py:81
  32.0 43.5 %collective-permute-start.1 = (bf16[256,1024]{1,0:T(8,128)(2,1)}, bf16[256,1024]{1,0:T(8,128)(2,1)}, u32[]{:S(2)}, u32[]{:S(2)}) collective-permute-start(bf16[256,1024]{1,0:T(8,128)(2,1)} %collective-permute-done.refs_2_), channel_id=1, source_target_pairs={{0,2},{1,3},{2,4},{3,5},{4,6},{5,7},{6,8},{7,9},{8,10},{9,11},{10,... | collective-permute-start | bytes 1572872 | tf_op jit(solution)/shard_map/ppermute | solution.py:81
  34.0 42.9 %collective-permute-start.7 = (bf16[256,1024]{1,0:T(8,128)(2,1)}, bf16[256,1024]{1,0:T(8,128)(2,1)S(1)}, u32[]{:S(2)}, u32[]{:S(2)}) collective-permute-start(bf16[256,1024]{1,0:T(8,128)(2,1)} %refs_9_.1), channel_id=1, source_target_pairs={{0,1},{2,3},{4,5},{6,7},{8,9},{10,11},{12,13},{14,15},{16,17},{18,... | collective-permute-start | bytes 1572872 | tf_op jit(solution)/shard_map/ppermute | solution.py:81
  53.1 36.2 %collective-permute-start.6 = (bf16[256,1024]{1,0:T(8,128)(2,1)}, bf16[256,1024]{1,0:T(8,128)(2,1)}, u32[]{:S(2)}, u32[]{:S(2)}) collective-permute-start(bf16[256,1024]{1,0:T(8,128)(2,1)} %collective-permute-done.5.refs_7_), channel_id=1, source_target_pairs={{0,2},{1,3},{2,4},{3,5},{4,6},{5,7},{6,8},{7,9},{8,10},{9,11},{10,... | collective-permute-start | bytes 1572872 | tf_op jit(solution)/shard_map/ppermute | solution.py:81
  55.0 36.1 %collective-permute-start.3 = (bf16[256,1024]{1,0:T(8,128)(2,1)}, bf16[256,1024]{1,0:T(8,128)(2,1)S(1)}, u32[]{:S(2)}, u32[]{:S(2)}) collective-permute-start(bf16[256,1024]{1,0:T(8,128)(2,1)} %collective-permute-done.refs_2_), channel_id=1, source_target_pairs={{0,1},{1,0},{2,3},{3,2},{4,5},{5,4},{6,7},{7,6},{8,9},{9,8},{10,11... | collective-permute-start | bytes 1572872 | tf_op jit(solution)/shard_map/ppermute | solution.py:81
  75.6 15.5 %collective-permute-start.4 = (bf16[256,1024]{1,0:T(8,128)(2,1)}, bf16[256,1024]{1,0:T(8,128)(2,1)S(1)}, u32[]{:S(2)}, u32[]{:S(2)}) collective-permute-start(bf16[256,1024]{1,0:T(8,128)(2,1)} %collective-permute-done.1.refs_0_), channel_id=1, source_target_pairs={{1,0},{3,2},{5,4},{7,6},{9,8},{11,10},{13,12},{15,14},{17,16},{19,... | collective-permute-start | bytes 1572872 | tf_op jit(solution)/shard_map/ppermute | solution.py:81
  76.9 15.6 %collective-permute-start.8 = (bf16[256,1024]{1,0:T(8,128)(2,1)}, bf16[256,1024]{1,0:T(8,128)(2,1)S(1)}, u32[]{:S(2)}, u32[]{:S(2)}) collective-permute-start(bf16[256,1024]{1,0:T(8,128)(2,1)} %collective-permute-done.5.refs_7_), channel_id=1, source_target_pairs={{0,1},{1,0},{2,3},{3,2},{4,5},{5,4},{6,7},{7,6},{8,9},{9,8},{10,11... | collective-permute-start | bytes 1572872 | tf_op jit(solution)/shard_map/ppermute | solution.py:81
  89.3 11.3 %collective-permute-start.9 = (bf16[256,1024]{1,0:T(8,128)(2,1)}, bf16[256,1024]{1,0:T(8,128)(2,1)S(1)}, u32[]{:S(2)}, u32[]{:S(2)}) collective-permute-start(bf16[256,1024]{1,0:T(8,128)(2,1)} %collective-permute-done.6.refs_5_), channel_id=1, source_target_pairs={{1,0},{3,2},{5,4},{7,6},{9,8},{11,10},{13,12},{15,14},{17,16},{19,... | collective-permute-start | bytes 1572872 | tf_op jit(solution)/shard_map/ppermute | solution.py:81

commit v9 on v2

--- a/solution.py
+++ b/solution.py
@@ -86,20 +86,28 @@
     n = lax.axis_size(axis)
     block_index = lax.axis_index(axis)
     own = (keys, values)
+    plane = 2 * lax.axis_size("grp")
+
+    def crossing(t):
+        return t % plane < 2
+
     ahead2 = [(i, i + 2) for i in range(n) if i + 2 < n]
     x1 = shifted(own, axis, ahead2)
     y1 = shifted(own, axis, [(i, i + 1) for i in range(0, n, 2)])
-    x2 = shifted(x1, axis, ahead2)
+    far = shifted(own, axis, [(i, i + 4) for i in range(n) if i + 4 < n and crossing(i + 4)])
+    x2 = shifted(x1, axis, [(i, i + 2) for i in range(n) if i + 2 < n and not crossing(i + 2)])
+    first_two = (block_index % plane) < 2
+    b4 = [jnp.where(first_two, a, b) for a, b in zip(far, x2)]
     y2 = shifted(x1, axis, [(i, i ^ 1) for i in range(n)])
-    y3 = shifted(x2, axis, [(i, i - 1) for i in range(1, n, 2)])
+    y3 = shifted(b4, axis, [(i, i - 1) for i in range(1, n, 2)])
     odd = (block_index % 2) == 1
     b1 = [jnp.where(odd, a, b) for a, b in zip(y1, y2)]
     b3 = [jnp.where(odd, a, b) for a, b in zip(y2, y3)]
     back_blocks = WINDOW // queries.shape[0]
     nblk = back_blocks + 1
     valid = (block_index + jnp.arange(nblk, dtype=jnp.int32) >= back_blocks).astype(jnp.int32)
-    k_blocks = [x2[0], b3[0], x1[0], b1[0], keys]
-    v_blocks = [x2[1], b3[1], x1[1], b1[1], values]
+    k_blocks = [b4[0], b3[0], x1[0], b1[0], keys]
+    v_blocks = [b4[1], b3[1], x1[1], b1[1], values]
     return attend(valid, queries, k_blocks, v_blocks)
 
 

time: 116 us -> 109 us (0.940)
  the two profiles are of different devices: /device:TPU:207 before, /device:TPU:484 now
where the time goes in v9:
time: 109 us
  waiting for transfers between devices  53.3 us (49%)
  starting transfers between devices  34.7 us (32%)
  Pallas kernels  15.5 us (14%)
  other arithmetic  5.04 us (5%)
    ppermute x12, waiting for transfers between devices, shifted(): return lax.ppermute(x, axis, pairs)  53.3 us
    ppermute x12, starting transfers between devices, shifted(): return lax.ppermute(x, axis, pairs)  34.7 us
    pallas_call x1, Pallas kernels, attend(): pl.pallas_call(attend_kernel, grid=(KV_HEADS,), in_specs=[pl.BlockSpec(me...  15.5 us
    select_n x2, other arithmetic, body(): b1 = [jnp.where(odd, a, b) for a, b in zip(y1, y2)]  4.4 us
  transfers between devices with their start and end apart: 12, of which 9 were waited for; matrix products, arithmetic and copies ran while one was open for 3% of the time, Pallas kernels for 0%

profile of v9, /device:TPU:484, one launch (start us, length us, event | category | flops | bytes accessed | tf_op | source)
XLA Modules:
  0.0 108.8 jit_solution(12097514944506914506)
XLA Ops:
  0.0 3.1 %collective-permute-start.1 = (bf16[256,1024]{1,0:T(8,128)(2,1)}, bf16[256,1024]{1,0:T(8,128)(2,1)}, u32[]{:S(2)}, u32[]{:S(2)}) collective-permute-start(bf16[256,1024]{1,0:T(8,128)(2,1)} %refs_4_.1), channel_id=1, source_target_pairs={{0,2},{1,3},{2,4},{3,5},{4,6},{5,7},{6,8},{7,9},{8,10},{9,11},{10,... | collective-permute-start | bytes 1572872 | tf_op jit(solution)/shard_map/ppermute | solution.py:81
  3.1 1.9 %collective-permute-start.7 = (bf16[256,1024]{1,0:T(8,128)(2,1)}, bf16[256,1024]{1,0:T(8,128)(2,1)}, u32[]{:S(2)}, u32[]{:S(2)}) collective-permute-start(bf16[256,1024]{1,0:T(8,128)(2,1)} %refs_9_.1), channel_id=1, source_target_pairs={{0,2},{1,3},{2,4},{3,5},{4,6},{5,7},{6,8},{7,9},{8,10},{9,11},{10,... | collective-permute-start | bytes 1572872 | tf_op jit(solution)/shard_map/ppermute | solution.py:81
  5.0 0.7 collective-permute-start
  5.7 13.0 %collective-permute-done.1.refs_2_ = bf16[256,1024]{1,0:T(8,128)(2,1)} collective-permute-done((bf16[256,1024]{1,0:T(8,128)(2,1)}, bf16[256,1024]{1,0:T(8,128)(2,1)}, u32[]{:S(2)}, u32[]{:S(2)}) %collective-permute-start.1) | collective-permute-done | bytes 524320 | tf_op jit(solution)/shard_map/ppermute | solution.py:81
  18.7 10.1 %collective-permute-start.2 = (bf16[256,1024]{1,0:T(8,128)(2,1)}, bf16[256,1024]{1,0:T(8,128)(2,1)S(1)}, u32[]{:S(2)}, u32[]{:S(2)}) collective-permute-start(bf16[256,1024]{1,0:T(8,128)(2,1)} %collective-permute-done.1.refs_2_), channel_id=1, source_target_pairs={{0,2},{1,3},{2,4},{3,5},{4,6},{5,7},{6,8},{7,9},{8,10},{9,11},{10,... | collective-permute-start | bytes 1572872 | tf_op jit(solution)/shard_map/ppermute | solution.py:81
  28.9 0.7 collective-permute-start.6
  29.6 8.6 %collective-permute-done.7.refs_7_ = bf16[256,1024]{1,0:T(8,128)(2,1)} collective-permute-done((bf16[256,1024]{1,0:T(8,128)(2,1)}, bf16[256,1024]{1,0:T(8,128)(2,1)}, u32[]{:S(2)}, u32[]{:S(2)}) %collective-permute-start.7) | collective-permute-done | bytes 524320 | tf_op jit(solution)/shard_map/ppermute | solution.py:81
  38.2 4.4 %collective-permute-start.8 = (bf16[256,1024]{1,0:T(8,128)(2,1)}, bf16[256,1024]{1,0:T(8,128)(2,1)S(1)}, u32[]{:S(2)}, u32[]{:S(2)}) collective-permute-start(bf16[256,1024]{1,0:T(8,128)(2,1)} %collective-permute-done.7.refs_7_), channel_id=1, source_target_pairs={{0,2},{1,3},{2,4},{3,5},{4,6},{5,7},{6,8},{7,9},{8,10},{9,11},{10,... | collective-permute-start | bytes 1572872 | tf_op jit(solution)/shard_map/ppermute | solution.py:81
  42.6 1.3 %collective-permute-start.5 = (bf16[256,1024]{1,0:T(8,128)(2,1)}, bf16[256,1024]{1,0:T(8,128)(2,1)S(1)}, u32[]{:S(2)}, u32[]{:S(2)}) collective-permute-start(bf16[256,1024]{1,0:T(8,128)(2,1)} %refs_4_.1), channel_id=1, source_target_pairs={{0,1},{2,3},{4,5},{6,7},{8,9},{10,11},{12,13},{14,15},{16,17},{18,... | collective-permute-start | bytes 1572872 | tf_op jit(solution)/shard_map/ppermute | solution.py:81
  43.9 0.0 collective-permute-done
  43.9 1.9 %collective-permute-start.3 = (bf16[256,1024]{1,0:T(8,128)(2,1)}, bf16[256,1024]{1,0:T(8,128)(2,1)}, u32[]{:S(2)}, u32[]{:S(2)}) collective-permute-start(bf16[256,1024]{1,0:T(8,128)(2,1)} %collective-permute-done.1.refs_2_), channel_id=1, source_target_pairs={{0,1},{1,0},{2,3},{3,2},{4,5},{5,4},{6,7},{7,6},{8,9},{9,8},{10,11... | collective-permute-start | bytes 1572872 | tf_op jit(solution)/shard_map/ppermute | solution.py:81
  45.9 3.6 %collective-permute-done.2 = bf16[256,1024]{1,0:T(8,128)(2,1)S(1)} collective-permute-done((bf16[256,1024]{1,0:T(8,128)(2,1)}, bf16[256,1024]{1,0:T(8,128)(2,1)S(1)}, u32[]{:S(2)}, u32[]{:S(2)}) %collective-permute-start.2) | collective-permute-done | bytes 524320 | tf_op jit(solution)/shard_map/ppermute | solution.py:81
  49.4 0.1 broadcast_select_fusion.5.refs_0_
  49.5 0.0 copy-start
  49.5 1.3 %collective-permute-start.4 = (bf16[256,1024]{1,0:T(8,128)(2,1)S(1)}, bf16[256,1024]{1,0:T(8,128)(2,1)}, u32[]{:S(2)}, u32[]{:S(2)}) collective-permute-start(bf16[256,1024]{1,0:T(8,128)(2,1)S(1)} %broadcast_select_fusion.5.refs_0_), channel_id=1, source_target_pairs={{1,0},{3,2},{5,4},{7,6},{9,8},{11,10},{13,12},{15,14},{17,16},{19,... | collective-permute-start | bytes 1572872 | tf_op jit(solution)/shard_map/ppermute | solution.py:81
  50.8 0.0 collective-permute-done.6
  50.8 5.4 %collective-permute-start.11 = (bf16[256,1024]{1,0:T(8,128)(2,1)}, bf16[256,1024]{1,0:T(8,128)(2,1)S(1)}, u32[]{:S(2)}, u32[]{:S(2)}) collective-permute-start(bf16[256,1024]{1,0:T(8,128)(2,1)} %refs_9_.1), channel_id=1, source_target_pairs={{0,1},{2,3},{4,5},{6,7},{8,9},{10,11},{12,13},{14,15},{16,17},{18,... | collective-permute-start | bytes 1572872 | tf_op jit(solution)/shard_map/ppermute | solution.py:81
  56.2 3.4 %collective-permute-done.8 = bf16[256,1024]{1,0:T(8,128)(2,1)S(1)} collective-permute-done((bf16[256,1024]{1,0:T(8,128)(2,1)}, bf16[256,1024]{1,0:T(8,128)(2,1)S(1)}, u32[]{:S(2)}, u32[]{:S(2)}) %collective-permute-start.8) | collective-permute-done | bytes 524320 | tf_op jit(solution)/shard_map/ppermute | solution.py:81
  59.5 2.6 %collective-permute-start.9 = (bf16[256,1024]{1,0:T(8,128)(2,1)}, bf16[256,1024]{1,0:T(8,128)(2,1)}, u32[]{:S(2)}, u32[]{:S(2)}) collective-permute-start(bf16[256,1024]{1,0:T(8,128)(2,1)} %collective-permute-done.7.refs_7_), channel_id=1, source_target_pairs={{0,1},{1,0},{2,3},{3,2},{4,5},{5,4},{6,7},{7,6},{8,9},{9,8},{10,11... | collective-permute-start | bytes 1572872 | tf_op jit(solution)/shard_map/ppermute | solution.py:81
  62.1 0.1 broadcast_select_fusion.4.refs_5_
  62.2 0.0 copy-done
  62.2 0.0 copy-start.1
  62.2 0.0 collective-permute-done.5
  62.2 1.3 %collective-permute-start.10 = (bf16[256,1024]{1,0:T(8,128)(2,1)S(1)}, bf16[256,1024]{1,0:T(8,128)(2,1)S(1)}, u32[]{:S(2)}, u32[]{:S(2)}) collective-permute-start(bf16[256,1024]{1,0:T(8,128)(2,1)S(1)} %broadcast_select_fusion.4.refs_5_), channel_id=1, source_target_pairs={{1,0},{3,2},{5,4},{7,6},{9,8},{11,10},{13,12},{15,14},{17,16},{19,... | collective-permute-start | bytes 1572872 | tf_op jit(solution)/shard_map/ppermute | solution.py:81
  63.5 0.5 compare_convert_fusion.valid_ref
  64.0 3.7 %collective-permute-done.3 = bf16[256,1024]{1,0:T(8,128)(2,1)} collective-permute-done((bf16[256,1024]{1,0:T(8,128)(2,1)}, bf16[256,1024]{1,0:T(8,128)(2,1)}, u32[]{:S(2)}, u32[]{:S(2)}) %collective-permute-start.3) | collective-permute-done | bytes 524320 | tf_op jit(solution)/shard_map/ppermute | solution.py:81
  67.7 4.5 %collective-permute-done.4 = bf16[256,1024]{1,0:T(8,128)(2,1)} collective-permute-done((bf16[256,1024]{1,0:T(8,128)(2,1)S(1)}, bf16[256,1024]{1,0:T(8,128)(2,1)}, u32[]{:S(2)}, u32[]{:S(2)}) %collective-permute-start.4) | collective-permute-done | bytes 524320 | tf_op jit(solution)/shard_map/ppermute | solution.py:81
  72.2 2.3 %broadcast_select_fusion.2 = (bf16[256,1024]{1,0:T(8,128)(2,1)}, bf16[256,1024]{1,0:T(8,128)(2,1)}) fusion(bf16[256,1024]{1,0:T(8,128)(2,1)S(1)} %collective-permute-done.5, bf16[256,1024]{1,0:T(8,128)(2,1)} %collective-permute-done.3, pred[]{:T(512)S(6)} %eq.6, bf16[256,1024]{1,0:T(8,128)(2,1)} %collective-permute-done.4), kind=kLoop, calls=%fused_computation.2 | loop fusion | flops 524288 | bytes 2621441 | tf_op jit(solution)/shard_map/jit(_where)/select_n | solution.py:104
  74.4 0.0 copy-done.1
  74.4 4.5 %collective-permute-done.11 = bf16[256,1024]{1,0:T(8,128)(2,1)S(1)} collective-permute-done((bf16[256,1024]{1,0:T(8,128)(2,1)}, bf16[256,1024]{1,0:T(8,128)(2,1)S(1)}, u32[]{:S(2)}, u32[]{:S(2)}) %collective-permute-start.11) | collective-permute-done | bytes 524320 | tf_op jit(solution)/shard_map/ppermute | solution.py:81
  79.0 8.1 %collective-permute-done.9 = bf16[256,1024]{1,0:T(8,128)(2,1)} collective-permute-done((bf16[256,1024]{1,0:T(8,128)(2,1)}, bf16[256,1024]{1,0:T(8,128)(2,1)}, u32[]{:S(2)}, u32[]{:S(2)}) %collective-permute-start.9) | collective-permute-done | bytes 524320 | tf_op jit(solution)/shard_map/ppermute | solution.py:81
  87.1 4.1 %collective-permute-done.10 = bf16[256,1024]{1,0:T(8,128)(2,1)S(1)} collective-permute-done((bf16[256,1024]{1,0:T(8,128)(2,1)S(1)}, bf16[256,1024]{1,0:T(8,128)(2,1)S(1)}, u32[]{:S(2)}, u32[]{:S(2)}) %collective-permute-start.10) | collective-permute-done | bytes 524320 | tf_op jit(solution)/shard_map/ppermute | solution.py:81
  91.1 2.1 %broadcast_select_fusion = (bf16[256,1024]{1,0:T(8,128)(2,1)}, bf16[256,1024]{1,0:T(8,128)(2,1)}) fusion(bf16[256,1024]{1,0:T(8,128)(2,1)S(1)} %collective-permute-done.11, bf16[256,1024]{1,0:T(8,128)(2,1)} %collective-permute-done.9, pred[]{:T(512)S(6)} %eq.6, bf16[256,1024]{1,0:T(8,128)(2,1)S(1)} %collective-permute-done.10), kind=kLoop, calls=%fused_computation | loop fusion | flops 524288 | bytes 2621441 | tf_op jit(solution)/shard_map/jit(_where)/select_n | solution.py:104
  93.3 15.5 %shard_map.37 = bf16[256,2048]{1,0:T(8,128)(2,1)} custom-call(s32[5]{0:T(128)} %compare_convert_fusion.valid_ref, bf16[256,2048]{1,0:T(8,128)(2,1)} %q_ref.1, bf16[256,1024]{1,0:T(8,128)(2,1)} %copy-done, bf16[256,1024]{1,0:T(8,128)(2,1)} %get-tuple-element.8.refs_1_, bf16[256,1024]{1,0:T(8,128)(2,1)} %collective-permute-done.1.refs_2_, ...), custom_call_target="tpu_custom_call" | custom-call | flops 2684354560 | bytes 7340032 | tf_op jit(solution)/shard_map/pallas_call | solution.py:67
Async XLA Ops:
  0.0 18.7 %collective-permute-start.1 = (bf16[256,1024]{1,0:T(8,128)(2,1)}, bf16[256,1024]{1,0:T(8,128)(2,1)}, u32[]{:S(2)}, u32[]{:S(2)}) collective-permute-start(bf16[256,1024]{1,0:T(8,128)(2,1)} %refs_4_.1), channel_id=1, source_target_pairs={{0,2},{1,3},{2,4},{3,5},{4,6},{5,7},{6,8},{7,9},{8,10},{9,11},{10,... | collective-permute-start | bytes 1572872 | tf_op jit(solution)/shard_map/ppermute | solution.py:81
  3.1 35.1 %collective-permute-start.7 = (bf16[256,1024]{1,0:T(8,128)(2,1)}, bf16[256,1024]{1,0:T(8,128)(2,1)}, u32[]{:S(2)}, u32[]{:S(2)}) collective-permute-start(bf16[256,1024]{1,0:T(8,128)(2,1)} %refs_9_.1), channel_id=1, source_target_pairs={{0,2},{1,3},{2,4},{3,5},{4,6},{5,7},{6,8},{7,9},{8,10},{9,11},{10,... | collective-permute-start | bytes 1572872 | tf_op jit(solution)/shard_map/ppermute | solution.py:81
  5.0 38.9 %collective-permute-start = (bf16[256,1024]{1,0:T(8,128)(2,1)}, bf16[256,1024]{1,0:T(8,128)(2,1)S(1)}, u32[]{:S(2)}, u32[]{:S(2)}) collective-permute-start(bf16[256,1024]{1,0:T(8,128)(2,1)} %refs_4_.1), channel_id=1, source_target_pairs={{12,16},{13,17},{28,32},{29,33},{44,48},{45,49},{60,64},{61,65},{7... | collective-permute-start | bytes 1572872 | tf_op jit(solution)/shard_map/ppermute | solution.py:81
  18.7 30.7 %collective-permute-start.2 = (bf16[256,1024]{1,0:T(8,128)(2,1)}, bf16[256,1024]{1,0:T(8,128)(2,1)S(1)}, u32[]{:S(2)}, u32[]{:S(2)}) collective-permute-start(bf16[256,1024]{1,0:T(8,128)(2,1)} %collective-permute-done.1.refs_2_), channel_id=1, source_target_pairs={{0,2},{1,3},{2,4},{3,5},{4,6},{5,7},{6,8},{7,9},{8,10},{9,11},{10,... | collective-permute-start | bytes 1572872 | tf_op jit(solution)/shard_map/ppermute | solution.py:81
  28.9 21.9 %collective-permute-start.6 = (bf16[256,1024]{1,0:T(8,128)(2,1)}, bf16[256,1024]{1,0:T(8,128)(2,1)S(1)}, u32[]{:S(2)}, u32[]{:S(2)}) collective-permute-start(bf16[256,1024]{1,0:T(8,128)(2,1)} %refs_9_.1), channel_id=1, source_target_pairs={{12,16},{13,17},{28,32},{29,33},{44,48},{45,49},{60,64},{61,65},{7... | collective-permute-start | bytes 1572872 | tf_op jit(solution)/shard_map/ppermute | solution.py:81
  38.2 21.3 %collective-permute-start.8 = (bf16[256,1024]{1,0:T(8,128)(2,1)}, bf16[256,1024]{1,0:T(8,128)(2,1)S(1)}, u32[]{:S(2)}, u32[]{:S(2)}) collective-permute-start(bf16[256,1024]{1,0:T(8,128)(2,1)} %collective-permute-done.7.refs_7_), channel_id=1, source_target_pairs={{0,2},{1,3},{2,4},{3,5},{4,6},{5,7},{6,8},{7,9},{8,10},{9,11},{10,... | collective-permute-start | bytes 1572872 | tf_op jit(solution)/shard_map/ppermute | solution.py:81
  42.6 19.6 %collective-permute-start.5 = (bf16[256,1024]{1,0:T(8,128)(2,1)}, bf16[256,1024]{1,0:T(8,128)(2,1)S(1)}, u32[]{:S(2)}, u32[]{:S(2)}) collective-permute-start(bf16[256,1024]{1,0:T(8,128)(2,1)} %refs_4_.1), channel_id=1, source_target_pairs={{0,1},{2,3},{4,5},{6,7},{8,9},{10,11},{12,13},{14,15},{16,17},{18,... | collective-permute-start | bytes 1572872 | tf_op jit(solution)/shard_map/ppermute | solution.py:81
  43.9 23.8 %collective-permute-start.3 = (bf16[256,1024]{1,0:T(8,128)(2,1)}, bf16[256,1024]{1,0:T(8,128)(2,1)}, u32[]{:S(2)}, u32[]{:S(2)}) collective-permute-start(bf16[256,1024]{1,0:T(8,128)(2,1)} %collective-permute-done.1.refs_2_), channel_id=1, source_target_pairs={{0,1},{1,0},{2,3},{3,2},{4,5},{5,4},{6,7},{7,6},{8,9},{9,8},{10,11... | collective-permute-start | bytes 1572872 | tf_op jit(solution)/shard_map/ppermute | solution.py:81
  49.5 12.7 %copy-start = (bf16[256,1024]{1,0:T(8,128)(2,1)}, bf16[256,1024]{1,0:T(8,128)(2,1)S(1)}, u32[]{:S(2)}) copy-start(bf16[256,1024]{1,0:T(8,128)(2,1)S(1)} %broadcast_select_fusion.5.refs_0_) | copy-start | bytes 1572868
  49.5 22.7 %collective-permute-start.4 = (bf16[256,1024]{1,0:T(8,128)(2,1)S(1)}, bf16[256,1024]{1,0:T(8,128)(2,1)}, u32[]{:S(2)}, u32[]{:S(2)}) collective-permute-start(bf16[256,1024]{1,0:T(8,128)(2,1)S(1)} %broadcast_select_fusion.5.refs_0_), channel_id=1, source_target_pairs={{1,0},{3,2},{5,4},{7,6},{9,8},{11,10},{13,12},{15,14},{17,16},{19,... | collective-permute-start | bytes 1572872 | tf_op jit(solution)/shard_map/ppermute | solution.py:81
  50.8 28.2 %collective-permute-start.11 = (bf16[256,1024]{1,0:T(8,128)(2,1)}, bf16[256,1024]{1,0:T(8,128)(2,1)S(1)}, u32[]{:S(2)}, u32[]{:S(2)}) collective-permute-start(bf16[256,1024]{1,0:T(8,128)(2,1)} %refs_9_.1), channel_id=1, source_target_pairs={{0,1},{2,3},{4,5},{6,7},{8,9},{10,11},{12,13},{14,15},{16,17},{18,... | collective-permute-start | bytes 1572872 | tf_op jit(solution)/shard_map/ppermute | solution.py:81
  59.5 27.5 %collective-permute-start.9 = (bf16[256,1024]{1,0:T(8,128)(2,1)}, bf16[256,1024]{1,0:T(8,128)(2,1)}, u32[]{:S(2)}, u32[]{:S(2)}) collective-permute-start(bf16[256,1024]{1,0:T(8,128)(2,1)} %collective-permute-done.7.refs_7_), channel_id=1, source_target_pairs={{0,1},{1,0},{2,3},{3,2},{4,5},{5,4},{6,7},{7,6},{8,9},{9,8},{10,11... | collective-permute-start | bytes 1572872 | tf_op jit(solution)/shard_map/ppermute | solution.py:81
  62.2 12.3 %copy-start.1 = (bf16[256,1024]{1,0:T(8,128)(2,1)}, bf16[256,1024]{1,0:T(8,128)(2,1)S(1)}, u32[]{:S(2)}) copy-start(bf16[256,1024]{1,0:T(8,128)(2,1)S(1)} %broadcast_select_fusion.4.refs_5_) | copy-start | bytes 1572868
  62.2 28.9 %collective-permute-start.10 = (bf16[256,1024]{1,0:T(8,128)(2,1)S(1)}, bf16[256,1024]{1,0:T(8,128)(2,1)S(1)}, u32[]{:S(2)}, u32[]{:S(2)}) collective-permute-start(bf16[256,1024]{1,0:T(8,128)(2,1)S(1)} %broadcast_select_fusion.4.refs_5_), channel_id=1, source_target_pairs={{1,0},{3,2},{5,4},{7,6},{9,8},{11,10},{13,12},{15,14},{17,16},{19,... | collective-permute-start | bytes 1572872 | tf_op jit(solution)/shard_map/ppermute | solution.py:81

commit v10 on v9

--- a/solution.py
+++ b/solution.py
@@ -1,3 +1,5 @@
+import functools
+
 import jax
 import jax.numpy as jnp
 from jax import lax
@@ -18,19 +20,29 @@
     return lax.ppermute(x, axis, pairs)
 
 
-def attend_kernel(valid_ref, q_ref, *refs):
-    nblk = (len(refs) - 1) // 2
-    k_refs, v_refs, o_ref = refs[:nblk], refs[nblk:2 * nblk], refs[-1]
+def attend_kernel(slots, valid_ref, q_ref, *refs):
+    nref = (len(refs) - 1) // 2
+    k_refs, v_refs, o_ref = refs[:nref], refs[nref:2 * nref], refs[-1]
+    nblk = len(slots)
+    odd = valid_ref[nblk] > 0
+
+    def load(which, slot):
+        if isinstance(slot, tuple):
+            return jnp.where(odd, which[slot[0]][...], which[slot[1]][...])
+        return which[slot][...]
+
     tok = q_ref.shape[0]
     row = lax.broadcasted_iota(jnp.int32, (tok, tok), 0)
     col = lax.broadcasted_iota(jnp.int32, (tok, tok), 1)
     group = HEADS // KV_HEADS
+    keys = [load(k_refs, s) for s in slots]
+    vals = [load(v_refs, s) for s in slots]
     for a in range(group):
         qa = q_ref[:, a * HEAD_DIM:(a + 1) * HEAD_DIM]
         scores = []
         for j in range(nblk):
             s = lax.dot_general(
-                qa, k_refs[j][...], (((1,), (1,)), ((), ())),
+                qa, keys[j], (((1,), (1,)), ((), ())),
                 preferred_element_type=jnp.float32,
             ) * HEAD_DIM ** (-0.5)
             if j == 0:
@@ -51,30 +63,31 @@
         out = None
         for j in range(nblk):
             w = (expos[j] * inv).astype(jnp.bfloat16)
-            part = jnp.dot(w, v_refs[j][...], preferred_element_type=jnp.float32)
+            part = jnp.dot(w, vals[j], preferred_element_type=jnp.float32)
             out = part if out is None else out + part
         o_ref[:, a * HEAD_DIM:(a + 1) * HEAD_DIM] = out.astype(o_ref.dtype)
 
 
-def attend(valid, queries, k_blocks, v_blocks):
+def attend(slots, valid, queries, k_arrays, v_arrays):
     tok = queries.shape[0]
     group = HEADS // KV_HEADS
-    nblk = len(k_blocks)
+    nblk = len(slots)
+    nref = len(k_arrays)
     kv_spec = pl.BlockSpec((tok, HEAD_DIM), lambda h: (0, h))
     q_spec = pl.BlockSpec((tok, group * HEAD_DIM), lambda h: (0, h))
     flops = 4 * HEADS * tok * tok * nblk * HEAD_DIM
-    nbytes = 2 * (2 * queries.size + 2 * nblk * k_blocks[0].size)
+    nbytes = 2 * (2 * queries.size + 2 * nref * k_arrays[0].size)
     return pl.pallas_call(
-        attend_kernel,
+        functools.partial(attend_kernel, tuple(slots)),
         grid=(KV_HEADS,),
         in_specs=[pl.BlockSpec(memory_space=pltpu.SMEM), q_spec]
-        + [kv_spec] * (2 * nblk),
+        + [kv_spec] * (2 * nref),
         out_specs=q_spec,
         out_shape=jax.ShapeDtypeStruct(queries.shape, queries.dtype),
         cost_estimate=pl.CostEstimate(
             flops=flops, transcendentals=HEADS * tok * tok * nblk, bytes_accessed=nbytes
         ),
-    )(valid, queries, *k_blocks, *v_blocks)
+    )(valid, queries, *k_arrays, *v_arrays)
 
 
 def shifted(x, axis, pairs):
@@ -101,14 +114,14 @@
     y2 = shifted(x1, axis, [(i, i ^ 1) for i in range(n)])
     y3 = shifted(b4, axis, [(i, i - 1) for i in range(1, n, 2)])
     odd = (block_index % 2) == 1
-    b1 = [jnp.where(odd, a, b) for a, b in zip(y1, y2)]
-    b3 = [jnp.where(odd, a, b) for a, b in zip(y2, y3)]
     back_blocks = WINDOW // queries.shape[0]
     nblk = back_blocks + 1
     valid = (block_index + jnp.arange(nblk, dtype=jnp.int32) >= back_blocks).astype(jnp.int32)
-    k_blocks = [b4[0], b3[0], x1[0], b1[0], keys]
-    v_blocks = [b4[1], b3[1], x1[1], b1[1], values]
-    return attend(valid, queries, k_blocks, v_blocks)
+    valid = jnp.concatenate([valid, odd.astype(jnp.int32).reshape(1)])
+    slots = (0, (2, 3), 4, (1, 2), 5)
+    k_arrays = [b4[0], y1[0], y2[0], y3[0], x1[0], keys]
+    v_arrays = [b4[1], y1[1], y2[1], y3[1], x1[1], values]
+    return attend(slots, valid, queries, k_arrays, v_arrays)
 
 
 def solution(mesh):

time: 109 us -> 115 us (1.055)
  the two profiles are of different devices: /device:TPU:484 before, /device:TPU:246 now
where the time goes in v10:
time: 115 us; the launch traced here: 114 us
  waiting for transfers between devices  64.1 us (56%)
  starting transfers between devices  32.8 us (29%)
  Pallas kernels  15.7 us (14%)
    ppermute x12, waiting for transfers between devices, shifted(): return lax.ppermute(x, axis, pairs)  64.1 us
    ppermute x12, starting transfers between devices, shifted(): return lax.ppermute(x, axis, pairs)  32.8 us
    pallas_call x1, Pallas kernels, attend(): pl.pallas_call(functools.partial(attend_kernel, tuple(slots)), grid=(KV_H...  15.7 us
  transfers between devices with their start and end apart: 12, of which 9 were waited for; matrix products, arithmetic and copies ran while one was open for 1% of the time, Pallas kernels for 0%

profile of v10, /device:TPU:246, one launch (start us, length us, event | category | flops | bytes accessed | tf_op | source)
XLA Modules:
  0.0 114.3 jit_solution(2328899146322637498)
XLA Ops:
  0.0 1.9 %collective-permute-start.1 = (bf16[256,1024]{1,0:T(8,128)(2,1)}, bf16[256,1024]{1,0:T(8,128)(2,1)S(1)}, u32[]{:S(2)}, u32[]{:S(2)}) collective-permute-start(bf16[256,1024]{1,0:T(8,128)(2,1)} %refs_5_.1), channel_id=1, source_target_pairs={{0,2},{1,3},{2,4},{3,5},{4,6},{5,7},{6,8},{7,9},{8,10},{9,11},{10,... | collective-permute-start | bytes 1572872 | tf_op jit(solution)/shard_map/ppermute | solution.py:94
  1.9 3.0 %collective-permute-start.7 = (bf16[256,1024]{1,0:T(8,128)(2,1)}, bf16[256,1024]{1,0:T(8,128)(2,1)}, u32[]{:S(2)}, u32[]{:S(2)}) collective-permute-start(bf16[256,1024]{1,0:T(8,128)(2,1)} %refs_11_.1), channel_id=1, source_target_pairs={{0,2},{1,3},{2,4},{3,5},{4,6},{5,7},{6,8},{7,9},{8,10},{9,11},{10,... | collective-permute-start | bytes 1572872 | tf_op jit(solution)/shard_map/ppermute | solution.py:94
  5.0 0.7 collective-permute-start
  5.7 20.2 %collective-permute-done.1.refs_4_ = bf16[256,1024]{1,0:T(8,128)(2,1)S(1)} collective-permute-done((bf16[256,1024]{1,0:T(8,128)(2,1)}, bf16[256,1024]{1,0:T(8,128)(2,1)S(1)}, u32[]{:S(2)}, u32[]{:S(2)}) %collective-permute-start.1) | collective-permute-done | bytes 524320 | tf_op jit(solution)/shard_map/ppermute | solution.py:94
  25.8 0.0 copy-start.2
  25.8 10.6 %collective-permute-start.2 = (bf16[256,1024]{1,0:T(8,128)(2,1)S(1)}, bf16[256,1024]{1,0:T(8,128)(2,1)S(1)}, u32[]{:S(2)}, u32[]{:S(2)}) collective-permute-start(bf16[256,1024]{1,0:T(8,128)(2,1)S(1)} %collective-permute-done.1.refs_4_), channel_id=1, source_target_pairs={{0,2},{1,3},{2,4},{3,5},{4,6},{5,7},{6,8},{7,9},{8,10},{9,11},{10,... | collective-permute-start | bytes 1572872 | tf_op jit(solution)/shard_map/ppermute | solution.py:94
  36.5 0.7 collective-permute-start.6
  37.2 2.3 %collective-permute-done.7.refs_10_ = bf16[256,1024]{1,0:T(8,128)(2,1)} collective-permute-done((bf16[256,1024]{1,0:T(8,128)(2,1)}, bf16[256,1024]{1,0:T(8,128)(2,1)}, u32[]{:S(2)}, u32[]{:S(2)}) %collective-permute-start.7) | collective-permute-done | bytes 524320 | tf_op jit(solution)/shard_map/ppermute | solution.py:94
  39.5 2.5 %collective-permute-start.8 = (bf16[256,1024]{1,0:T(8,128)(2,1)}, bf16[256,1024]{1,0:T(8,128)(2,1)S(1)}, u32[]{:S(2)}, u32[]{:S(2)}) collective-permute-start(bf16[256,1024]{1,0:T(8,128)(2,1)} %collective-permute-done.7.refs_10_), channel_id=1, source_target_pairs={{0,2},{1,3},{2,4},{3,5},{4,6},{5,7},{6,8},{7,9},{8,10},{9,11},{10,... | collective-permute-start | bytes 1572872 | tf_op jit(solution)/shard_map/ppermute | solution.py:94
  42.0 2.8 %collective-permute-start.3 = (bf16[256,1024]{1,0:T(8,128)(2,1)}, bf16[256,1024]{1,0:T(8,128)(2,1)}, u32[]{:S(2)}, u32[]{:S(2)}) collective-permute-start(bf16[256,1024]{1,0:T(8,128)(2,1)} %refs_5_.1), channel_id=1, source_target_pairs={{0,1},{2,3},{4,5},{6,7},{8,9},{10,11},{12,13},{14,15},{16,17},{18,... | collective-permute-start | bytes 1572872 | tf_op jit(solution)/shard_map/ppermute | solution.py:94
  44.8 0.0 collective-permute-done
  44.8 2.1 %collective-permute-start.9 = (bf16[256,1024]{1,0:T(8,128)(2,1)}, bf16[256,1024]{1,0:T(8,128)(2,1)}, u32[]{:S(2)}, u32[]{:S(2)}) collective-permute-start(bf16[256,1024]{1,0:T(8,128)(2,1)} %refs_11_.1), channel_id=1, source_target_pairs={{0,1},{2,3},{4,5},{6,7},{8,9},{10,11},{12,13},{14,15},{16,17},{18,... | collective-permute-start | bytes 1572872 | tf_op jit(solution)/shard_map/ppermute | solution.py:94
  46.9 3.7 %collective-permute-done.2 = bf16[256,1024]{1,0:T(8,128)(2,1)S(1)} collective-permute-done((bf16[256,1024]{1,0:T(8,128)(2,1)S(1)}, bf16[256,1024]{1,0:T(8,128)(2,1)S(1)}, u32[]{:S(2)}, u32[]{:S(2)}) %collective-permute-start.2) | collective-permute-done | bytes 524320 | tf_op jit(solution)/shard_map/ppermute | solution.py:94
  50.6 2.6 %collective-permute-start.4 = (bf16[256,1024]{1,0:T(8,128)(2,1)S(1)}, bf16[256,1024]{1,0:T(8,128)(2,1)}, u32[]{:S(2)}, u32[]{:S(2)}) collective-permute-start(bf16[256,1024]{1,0:T(8,128)(2,1)S(1)} %collective-permute-done.1.refs_4_), channel_id=1, source_target_pairs={{0,1},{1,0},{2,3},{3,2},{4,5},{5,4},{6,7},{7,6},{8,9},{9,8},{10,11... | collective-permute-start | bytes 1572872 | tf_op jit(solution)/shard_map/ppermute | solution.py:94
  53.2 0.1 broadcast_select_fusion.1.refs_0_
  53.2 0.0 copy-done.2
  53.3 0.0 copy-start
  53.3 0.0 collective-permute-done.6
  53.3 3.3 %collective-permute-start.10 = (bf16[256,1024]{1,0:T(8,128)(2,1)}, bf16[256,1024]{1,0:T(8,128)(2,1)S(1)}, u32[]{:S(2)}, u32[]{:S(2)}) collective-permute-start(bf16[256,1024]{1,0:T(8,128)(2,1)} %collective-permute-done.7.refs_10_), channel_id=1, source_target_pairs={{0,1},{1,0},{2,3},{3,2},{4,5},{5,4},{6,7},{7,6},{8,9},{9,8},{10,11... | collective-permute-start | bytes 1572872 | tf_op jit(solution)/shard_map/ppermute | solution.py:94
  56.5 4.2 %collective-permute-done.8 = bf16[256,1024]{1,0:T(8,128)(2,1)S(1)} collective-permute-done((bf16[256,1024]{1,0:T(8,128)(2,1)}, bf16[256,1024]{1,0:T(8,128)(2,1)S(1)}, u32[]{:S(2)}, u32[]{:S(2)}) %collective-permute-start.8) | collective-permute-done | bytes 524320 | tf_op jit(solution)/shard_map/ppermute | solution.py:94
  60.7 1.3 %collective-permute-start.5 = (bf16[256,1024]{1,0:T(8,128)(2,1)S(1)}, bf16[256,1024]{1,0:T(8,128)(2,1)}, u32[]{:S(2)}, u32[]{:S(2)}) collective-permute-start(bf16[256,1024]{1,0:T(8,128)(2,1)S(1)} %broadcast_select_fusion.1.refs_0_), channel_id=1, source_target_pairs={{1,0},{3,2},{5,4},{7,6},{9,8},{11,10},{13,12},{15,14},{17,16},{19,... | collective-permute-start | bytes 1572872 | tf_op jit(solution)/shard_map/ppermute | solution.py:94
  62.0 0.1 broadcast_select_fusion.refs_6_
  62.1 0.0 copy-done
  62.1 0.0 copy-start.1
  62.1 0.0 collective-permute-done.3.refs_1_
  62.1 1.3 %collective-permute-start.11 = (bf16[256,1024]{1,0:T(8,128)(2,1)S(1)}, bf16[256,1024]{1,0:T(8,128)(2,1)S(1)}, u32[]{:S(2)}, u32[]{:S(2)}) collective-permute-start(bf16[256,1024]{1,0:T(8,128)(2,1)S(1)} %broadcast_select_fusion.refs_6_), channel_id=1, source_target_pairs={{1,0},{3,2},{5,4},{7,6},{9,8},{11,10},{13,12},{15,14},{17,16},{19,... | collective-permute-start | bytes 1572872 | tf_op jit(solution)/shard_map/ppermute | solution.py:94
  63.4 0.7 add_convert_fusion.valid_ref
  64.1 3.8 %collective-permute-done.9.refs_7_ = bf16[256,1024]{1,0:T(8,128)(2,1)} collective-permute-done((bf16[256,1024]{1,0:T(8,128)(2,1)}, bf16[256,1024]{1,0:T(8,128)(2,1)}, u32[]{:S(2)}, u32[]{:S(2)}) %collective-permute-start.9) | collective-permute-done | bytes 524320 | tf_op jit(solution)/shard_map/ppermute | solution.py:94
  67.8 11.1 %collective-permute-done.4.refs_2_ = bf16[256,1024]{1,0:T(8,128)(2,1)} collective-permute-done((bf16[256,1024]{1,0:T(8,128)(2,1)S(1)}, bf16[256,1024]{1,0:T(8,128)(2,1)}, u32[]{:S(2)}, u32[]{:S(2)}) %collective-permute-start.4) | collective-permute-done | bytes 524320 | tf_op jit(solution)/shard_map/ppermute | solution.py:94
  79.0 6.6 %collective-permute-done.10.refs_8_ = bf16[256,1024]{1,0:T(8,128)(2,1)S(1)} collective-permute-done((bf16[256,1024]{1,0:T(8,128)(2,1)}, bf16[256,1024]{1,0:T(8,128)(2,1)S(1)}, u32[]{:S(2)}, u32[]{:S(2)}) %collective-permute-start.10) | collective-permute-done | bytes 524320 | tf_op jit(solution)/shard_map/ppermute | solution.py:94
  85.5 0.0 copy-start.3
  85.5 4.3 %collective-permute-done.5.refs_3_ = bf16[256,1024]{1,0:T(8,128)(2,1)} collective-permute-done((bf16[256,1024]{1,0:T(8,128)(2,1)S(1)}, bf16[256,1024]{1,0:T(8,128)(2,1)}, u32[]{:S(2)}, u32[]{:S(2)}) %collective-permute-start.5) | collective-permute-done | bytes 524320 | tf_op jit(solution)/shard_map/ppermute | solution.py:94
  89.8 8.0 %collective-permute-done.11.refs_9_ = bf16[256,1024]{1,0:T(8,128)(2,1)S(1)} collective-permute-done((bf16[256,1024]{1,0:T(8,128)(2,1)S(1)}, bf16[256,1024]{1,0:T(8,128)(2,1)S(1)}, u32[]{:S(2)}, u32[]{:S(2)}) %collective-permute-start.11) | collective-permute-done | bytes 524320 | tf_op jit(solution)/shard_map/ppermute | solution.py:94
  97.9 0.0 copy-done.1
  97.9 0.0 copy-done.3
  97.9 0.0 copy-start.4
  97.9 0.8 copy-done.4
  98.7 15.7 %shard_map.37 = bf16[256,2048]{1,0:T(8,128)(2,1)} custom-call(s32[6]{0:T(128)} %add_convert_fusion.valid_ref, bf16[256,2048]{1,0:T(8,128)(2,1)} %q_ref.1, bf16[256,1024]{1,0:T(8,128)(2,1)} %copy-done, bf16[256,1024]{1,0:T(8,128)(2,1)} %collective-permute-done.3.refs_1_, bf16[256,1024]{1,0:T(8,128)(2,1)} %collective-permute-done.4.refs_2_, ...), custom_call_target="tpu_custom_call" | custom-call | flops 2684354560 | bytes 8388608 | tf_op jit(solution)/shard_map/pallas_call | solution.py:80
  (1 shorter events, 0.0 us)
Async XLA Ops:
  0.0 25.8 %collective-permute-start.1 = (bf16[256,1024]{1,0:T(8,128)(2,1)}, bf16[256,1024]{1,0:T(8,128)(2,1)S(1)}, u32[]{:S(2)}, u32[]{:S(2)}) collective-permute-start(bf16[256,1024]{1,0:T(8,128)(2,1)} %refs_5_.1), channel_id=1, source_target_pairs={{0,2},{1,3},{2,4},{3,5},{4,6},{5,7},{6,8},{7,9},{8,10},{9,11},{10,... | collective-permute-start | bytes 1572872 | tf_op jit(solution)/shard_map/ppermute | solution.py:94
  1.9 37.5 %collective-permute-start.7 = (bf16[256,1024]{1,0:T(8,128)(2,1)}, bf16[256,1024]{1,0:T(8,128)(2,1)}, u32[]{:S(2)}, u32[]{:S(2)}) collective-permute-start(bf16[256,1024]{1,0:T(8,128)(2,1)} %refs_11_.1), channel_id=1, source_target_pairs={{0,2},{1,3},{2,4},{3,5},{4,6},{5,7},{6,8},{7,9},{8,10},{9,11},{10,... | collective-permute-start | bytes 1572872 | tf_op jit(solution)/shard_map/ppermute | solution.py:94
  5.0 39.8 %collective-permute-start = (bf16[256,1024]{1,0:T(8,128)(2,1)}, bf16[256,1024]{1,0:T(8,128)(2,1)S(1)}, u32[]{:S(2)}, u32[]{:S(2)}) collective-permute-start(bf16[256,1024]{1,0:T(8,128)(2,1)} %refs_5_.1), channel_id=1, source_target_pairs={{12,16},{13,17},{28,32},{29,33},{44,48},{45,49},{60,64},{61,65},{7... | collective-permute-start | bytes 1572872 | tf_op jit(solution)/shard_map/ppermute | solution.py:94
  25.8 27.4 %copy-start.2 = (bf16[256,1024]{1,0:T(8,128)(2,1)}, bf16[256,1024]{1,0:T(8,128)(2,1)S(1)}, u32[]{:S(2)}) copy-start(bf16[256,1024]{1,0:T(8,128)(2,1)S(1)} %collective-permute-done.1.refs_4_) | copy-start | bytes 1572868
  25.8 24.8 %collective-permute-start.2 = (bf16[256,1024]{1,0:T(8,128)(2,1)S(1)}, bf16[256,1024]{1,0:T(8,128)(2,1)S(1)}, u32[]{:S(2)}, u32[]{:S(2)}) collective-permute-start(bf16[256,1024]{1,0:T(8,128)(2,1)S(1)} %collective-permute-done.1.refs_4_), channel_id=1, source_target_pairs={{0,2},{1,3},{2,4},{3,5},{4,6},{5,7},{6,8},{7,9},{8,10},{9,11},{10,... | collective-permute-start | bytes 1572872 | tf_op jit(solution)/shard_map/ppermute | solution.py:94
  36.5 16.8 %collective-permute-start.6 = (bf16[256,1024]{1,0:T(8,128)(2,1)}, bf16[256,1024]{1,0:T(8,128)(2,1)S(1)}, u32[]{:S(2)}, u32[]{:S(2)}) collective-permute-start(bf16[256,1024]{1,0:T(8,128)(2,1)} %refs_11_.1), channel_id=1, source_target_pairs={{12,16},{13,17},{28,32},{29,33},{44,48},{45,49},{60,64},{61,65},{7... | collective-permute-start | bytes 1572872 | tf_op jit(solution)/shard_map/ppermute | solution.py:94
  39.5 21.2 %collective-permute-start.8 = (bf16[256,1024]{1,0:T(8,128)(2,1)}, bf16[256,1024]{1,0:T(8,128)(2,1)S(1)}, u32[]{:S(2)}, u32[]{:S(2)}) collective-permute-start(bf16[256,1024]{1,0:T(8,128)(2,1)} %collective-permute-done.7.refs_10_), channel_id=1, source_target_pairs={{0,2},{1,3},{2,4},{3,5},{4,6},{5,7},{6,8},{7,9},{8,10},{9,11},{10,... | collective-permute-start | bytes 1572872 | tf_op jit(solution)/shard_map/ppermute | solution.py:94
  42.0 20.1 %collective-permute-start.3 = (bf16[256,1024]{1,0:T(8,128)(2,1)}, bf16[256,1024]{1,0:T(8,128)(2,1)}, u32[]{:S(2)}, u32[]{:S(2)}) collective-permute-start(bf16[256,1024]{1,0:T(8,128)(2,1)} %refs_5_.1), channel_id=1, source_target_pairs={{0,1},{2,3},{4,5},{6,7},{8,9},{10,11},{12,13},{14,15},{16,17},{18,... | collective-permute-start | bytes 1572872 | tf_op jit(solution)/shard_map/ppermute | solution.py:94
  44.8 23.0 %collective-permute-start.9 = (bf16[256,1024]{1,0:T(8,128)(2,1)}, bf16[256,1024]{1,0:T(8,128)(2,1)}, u32[]{:S(2)}, u32[]{:S(2)}) collective-permute-start(bf16[256,1024]{1,0:T(8,128)(2,1)} %refs_11_.1), channel_id=1, source_target_pairs={{0,1},{2,3},{4,5},{6,7},{8,9},{10,11},{12,13},{14,15},{16,17},{18,... | collective-permute-start | bytes 1572872 | tf_op jit(solution)/shard_map/ppermute | solution.py:94
  50.6 28.4 %collective-permute-start.4 = (bf16[256,1024]{1,0:T(8,128)(2,1)S(1)}, bf16[256,1024]{1,0:T(8,128)(2,1)}, u32[]{:S(2)}, u32[]{:S(2)}) collective-permute-start(bf16[256,1024]{1,0:T(8,128)(2,1)S(1)} %collective-permute-done.1.refs_4_), channel_id=1, source_target_pairs={{0,1},{1,0},{2,3},{3,2},{4,5},{5,4},{6,7},{7,6},{8,9},{9,8},{10,11... | collective-permute-start | bytes 1572872 | tf_op jit(solution)/shard_map/ppermute | solution.py:94
  53.3 8.8 %copy-start = (bf16[256,1024]{1,0:T(8,128)(2,1)}, bf16[256,1024]{1,0:T(8,128)(2,1)S(1)}, u32[]{:S(2)}) copy-start(bf16[256,1024]{1,0:T(8,128)(2,1)S(1)} %broadcast_select_fusion.1.refs_0_) | copy-start | bytes 1572868
  53.3 32.3 %collective-permute-start.10 = (bf16[256,1024]{1,0:T(8,128)(2,1)}, bf16[256,1024]{1,0:T(8,128)(2,1)S(1)}, u32[]{:S(2)}, u32[]{:S(2)}) collective-permute-start(bf16[256,1024]{1,0:T(8,128)(2,1)} %collective-permute-done.7.refs_10_), channel_id=1, source_target_pairs={{0,1},{1,0},{2,3},{3,2},{4,5},{5,4},{6,7},{7,6},{8,9},{9,8},{10,11... | collective-permute-start | bytes 1572872 | tf_op jit(solution)/shard_map/ppermute | solution.py:94
  60.7 29.1 %collective-permute-start.5 = (bf16[256,1024]{1,0:T(8,128)(2,1)S(1)}, bf16[256,1024]{1,0:T(8,128)(2,1)}, u32[]{:S(2)}, u32[]{:S(2)}) collective-permute-start(bf16[256,1024]{1,0:T(8,128)(2,1)S(1)} %broadcast_select_fusion.1.refs_0_), channel_id=1, source_target_pairs={{1,0},{3,2},{5,4},{7,6},{9,8},{11,10},{13,12},{15,14},{17,16},{19,... | collective-permute-start | bytes 1572872 | tf_op jit(solution)/shard_map/ppermute | solution.py:94
  62.1 35.8 %copy-start.1 = (bf16[256,1024]{1,0:T(8,128)(2,1)}, bf16[256,1024]{1,0:T(8,128)(2,1)S(1)}, u32[]{:S(2)}) copy-start(bf16[256,1024]{1,0:T(8,128)(2,1)S(1)} %broadcast_select_fusion.refs_6_) | copy-start | bytes 1572868
  62.1 35.8 %collective-permute-start.11 = (bf16[256,1024]{1,0:T(8,128)(2,1)S(1)}, bf16[256,1024]{1,0:T(8,128)(2,1)S(1)}, u32[]{:S(2)}, u32[]{:S(2)}) collective-permute-start(bf16[256,1024]{1,0:T(8,128)(2,1)S(1)} %broadcast_select_fusion.refs_6_), channel_id=1, source_target_pairs={{1,0},{3,2},{5,4},{7,6},{9,8},{11,10},{13,12},{15,14},{17,16},{19,... | collective-permute-start | bytes 1572872 | tf_op jit(solution)/shard_map/ppermute | solution.py:94
  85.5 12.3 %copy-start.3 = (bf16[256,1024]{1,0:T(8,128)(2,1)}, bf16[256,1024]{1,0:T(8,128)(2,1)S(1)}, u32[]{:S(2)}) copy-start(bf16[256,1024]{1,0:T(8,128)(2,1)S(1)} %collective-permute-done.10.refs_8_) | copy-start | bytes 1572868
  97.9 0.8 copy-start.4

commit v11 on v9

--- a/solution.py
+++ b/solution.py
@@ -92,11 +92,13 @@
         return t % plane < 2
 
     ahead2 = [(i, i + 2) for i in range(n) if i + 2 < n]
-    x1 = shifted(own, axis, ahead2)
+    x1_near = shifted(own, axis, [(i, i + 2) for i in range(n) if i + 2 < n and not crossing(i + 2)])
+    x1_far = shifted(own, axis, [(i, i + 2) for i in range(n) if i + 2 < n and crossing(i + 2)])
     y1 = shifted(own, axis, [(i, i + 1) for i in range(0, n, 2)])
+    first_two = (block_index % plane) < 2
+    x1 = [jnp.where(first_two, a, b) for a, b in zip(x1_far, x1_near)]
     far = shifted(own, axis, [(i, i + 4) for i in range(n) if i + 4 < n and crossing(i + 4)])
     x2 = shifted(x1, axis, [(i, i + 2) for i in range(n) if i + 2 < n and not crossing(i + 2)])
-    first_two = (block_index % plane) < 2
     b4 = [jnp.where(first_two, a, b) for a, b in zip(far, x2)]
     y2 = shifted(x1, axis, [(i, i ^ 1) for i in range(n)])
     y3 = shifted(b4, axis, [(i, i - 1) for i in range(1, n, 2)])

time: 109 us -> 111 us (1.018)
  the two profiles are of different devices: /device:TPU:484 before, /device:TPU:242 now
where the time goes in v11:
time: 111 us
  waiting for transfers between devices  48.8 us (44%)
  starting transfers between devices  41.2 us (37%)
  Pallas kernels  15.5 us (14%)
  other arithmetic  5.16 us (5%)
    ppermute x14, waiting for transfers between devices, shifted(): return lax.ppermute(x, axis, pairs)  48.8 us
    ppermute x14, starting transfers between devices, shifted(): return lax.ppermute(x, axis, pairs)  41.2 us
    pallas_call x1, Pallas kernels, attend(): pl.pallas_call(attend_kernel, grid=(KV_HEADS,), in_specs=[pl.BlockSpec(me...  15.5 us
    select_n x2, other arithmetic, body(): b1 = [jnp.where(odd, a, b) for a, b in zip(y1, y2)]  4.39 us
  transfers between devices with their start and end apart: 14, of which 8 were waited for; matrix products, arithmetic and copies ran while one was open for 3% of the time, Pallas kernels for 0%

profile of v11, /device:TPU:242, one launch (start us, length us, event | category | flops | bytes accessed | tf_op | source)
XLA Modules:
  0.0 111.0 jit_solution(6903148460398517343)
XLA Ops:
  0.0 3.4 %collective-permute-start.2 = (bf16[256,1024]{1,0:T(8,128)(2,1)}, bf16[256,1024]{1,0:T(8,128)(2,1)S(1)}, u32[]{:S(2)}, u32[]{:S(2)}) collective-permute-start(bf16[256,1024]{1,0:T(8,128)(2,1)} %refs_4_.1), channel_id=1, source_target_pairs={{0,2},{1,3},{2,4},{3,5},{4,6},{5,7},{6,8},{7,9},{8,10},{9,11},{10,... | collective-permute-start | bytes 1572872 | tf_op jit(solution)/shard_map/ppermute | solution.py:81
  3.4 0.7 collective-permute-start.1
  4.1 3.1 %collective-permute-start.9 = (bf16[256,1024]{1,0:T(8,128)(2,1)}, bf16[256,1024]{1,0:T(8,128)(2,1)S(1)}, u32[]{:S(2)}, u32[]{:S(2)}) collective-permute-start(bf16[256,1024]{1,0:T(8,128)(2,1)} %refs_9_.1), channel_id=1, source_target_pairs={{0,2},{1,3},{2,4},{3,5},{4,6},{5,7},{6,8},{7,9},{8,10},{9,11},{10,... | collective-permute-start | bytes 1572872 | tf_op jit(solution)/shard_map/ppermute | solution.py:81
  7.2 0.7 collective-permute-start.8
  7.9 0.7 collective-permute-start
  8.6 8.3 %collective-permute-done.2 = bf16[256,1024]{1,0:T(8,128)(2,1)S(1)} collective-permute-done((bf16[256,1024]{1,0:T(8,128)(2,1)}, bf16[256,1024]{1,0:T(8,128)(2,1)S(1)}, u32[]{:S(2)}, u32[]{:S(2)}) %collective-permute-start.2) | collective-permute-done | bytes 524320 | tf_op jit(solution)/shard_map/ppermute | solution.py:81
  16.9 0.0 collective-permute-done.1
  16.9 0.1 broadcast_select_fusion.7.refs_2_
  17.0 0.0 copy-start
  17.0 0.0 copy-start.4
  17.0 4.6 %collective-permute-start.3 = (bf16[256,1024]{1,0:T(8,128)(2,1)S(1)}, bf16[256,1024]{1,0:T(8,128)(2,1)S(1)}, u32[]{:S(2)}, u32[]{:S(2)}) collective-permute-start(bf16[256,1024]{1,0:T(8,128)(2,1)S(1)} %broadcast_select_fusion.7.refs_2_), channel_id=1, source_target_pairs={{0,2},{1,3},{2,4},{3,5},{4,6},{5,7},{6,8},{7,9},{8,10},{9,11},{10,... | collective-permute-start | bytes 1572872 | tf_op jit(solution)/shard_map/ppermute | solution.py:81
  21.6 0.7 collective-permute-start.7
  22.3 5.8 %collective-permute-done.9 = bf16[256,1024]{1,0:T(8,128)(2,1)S(1)} collective-permute-done((bf16[256,1024]{1,0:T(8,128)(2,1)}, bf16[256,1024]{1,0:T(8,128)(2,1)S(1)}, u32[]{:S(2)}, u32[]{:S(2)}) %collective-permute-start.9) | collective-permute-done | bytes 524320 | tf_op jit(solution)/shard_map/ppermute | solution.py:81
  28.1 0.0 collective-permute-done.8
  28.1 0.1 broadcast_select_fusion.5.refs_7_
  28.2 0.0 copy-start.1
  28.2 13.5 %collective-permute-start.10 = (bf16[256,1024]{1,0:T(8,128)(2,1)S(1)}, bf16[256,1024]{1,0:T(8,128)(2,1)S(1)}, u32[]{:S(2)}, u32[]{:S(2)}) collective-permute-start(bf16[256,1024]{1,0:T(8,128)(2,1)S(1)} %broadcast_select_fusion.5.refs_7_), channel_id=1, source_target_pairs={{0,2},{1,3},{2,4},{3,5},{4,6},{5,7},{6,8},{7,9},{8,10},{9,11},{10,... | collective-permute-start | bytes 1572872 | tf_op jit(solution)/shard_map/ppermute | solution.py:81
  41.7 0.0 copy-done.4
  41.7 1.3 %collective-permute-start.6 = (bf16[256,1024]{1,0:T(8,128)(2,1)S(1)}, bf16[256,1024]{1,0:T(8,128)(2,1)S(1)}, u32[]{:S(2)}, u32[]{:S(2)}) collective-permute-start(bf16[256,1024]{1,0:T(8,128)(2,1)S(1)} %copy-done.4), channel_id=1, source_target_pairs={{0,1},{2,3},{4,5},{6,7},{8,9},{10,11},{12,13},{14,15},{16,17},{18,... | collective-permute-start | bytes 1572872 | tf_op jit(solution)/shard_map/ppermute | solution.py:81
  43.0 0.0 collective-permute-done
  43.0 0.0 copy-done
  43.0 1.9 %collective-permute-start.4 = (bf16[256,1024]{1,0:T(8,128)(2,1)S(1)}, bf16[256,1024]{1,0:T(8,128)(2,1)S(1)}, u32[]{:S(2)}, u32[]{:S(2)}) collective-permute-start(bf16[256,1024]{1,0:T(8,128)(2,1)S(1)} %broadcast_select_fusion.7.refs_2_), channel_id=1, source_target_pairs={{0,1},{1,0},{2,3},{3,2},{4,5},{5,4},{6,7},{7,6},{8,9},{9,8},{10,11... | collective-permute-start | bytes 1572872 | tf_op jit(solution)/shard_map/ppermute | solution.py:81
  45.0 0.0 collective-permute-done.3
  45.0 0.1 broadcast_select_fusion.6.refs_0_
  45.0 0.0 copy-start.2
  45.0 1.3 %collective-permute-start.5 = (bf16[256,1024]{1,0:T(8,128)(2,1)S(1)}, bf16[256,1024]{1,0:T(8,128)(2,1)}, u32[]{:S(2)}, u32[]{:S(2)}) collective-permute-start(bf16[256,1024]{1,0:T(8,128)(2,1)S(1)} %broadcast_select_fusion.6.refs_0_), channel_id=1, source_target_pairs={{1,0},{3,2},{5,4},{7,6},{9,8},{11,10},{13,12},{15,14},{17,16},{19,... | collective-permute-start | bytes 1572872 | tf_op jit(solution)/shard_map/ppermute | solution.py:81
  46.3 0.0 collective-permute-done.7
  46.3 6.1 %collective-permute-start.13 = (bf16[256,1024]{1,0:T(8,128)(2,1)}, bf16[256,1024]{1,0:T(8,128)(2,1)}, u32[]{:S(2)}, u32[]{:S(2)}) collective-permute-start(bf16[256,1024]{1,0:T(8,128)(2,1)} %refs_9_.1), channel_id=1, source_target_pairs={{0,1},{2,3},{4,5},{6,7},{8,9},{10,11},{12,13},{14,15},{16,17},{18,... | collective-permute-start | bytes 1572872 | tf_op jit(solution)/shard_map/ppermute | solution.py:81
  52.5 0.0 collective-permute-done.10
  52.5 0.0 copy-done.1
  52.5 1.9 %collective-permute-start.11 = (bf16[256,1024]{1,0:T(8,128)(2,1)S(1)}, bf16[256,1024]{1,0:T(8,128)(2,1)}, u32[]{:S(2)}, u32[]{:S(2)}) collective-permute-start(bf16[256,1024]{1,0:T(8,128)(2,1)S(1)} %broadcast_select_fusion.5.refs_7_), channel_id=1, source_target_pairs={{0,1},{1,0},{2,3},{3,2},{4,5},{5,4},{6,7},{7,6},{8,9},{9,8},{10,11... | collective-permute-start | bytes 1572872 | tf_op jit(solution)/shard_map/ppermute | solution.py:81
  54.4 0.1 broadcast_select_fusion.4.refs_5_
  54.5 0.0 copy-done.2
  54.5 0.0 copy-start.3
  54.5 0.8 collective-permute-done.6
  55.3 1.3 %collective-permute-start.12 = (bf16[256,1024]{1,0:T(8,128)(2,1)S(1)}, bf16[256,1024]{1,0:T(8,128)(2,1)}, u32[]{:S(2)}, u32[]{:S(2)}) collective-permute-start(bf16[256,1024]{1,0:T(8,128)(2,1)S(1)} %broadcast_select_fusion.4.refs_5_), channel_id=1, source_target_pairs={{1,0},{3,2},{5,4},{7,6},{9,8},{11,10},{13,12},{15,14},{17,16},{19,... | collective-permute-start | bytes 1572872 | tf_op jit(solution)/shard_map/ppermute | solution.py:81
  56.6 0.5 compare_convert_fusion.valid_ref
  57.1 9.4 %collective-permute-done.4 = bf16[256,1024]{1,0:T(8,128)(2,1)S(1)} collective-permute-done((bf16[256,1024]{1,0:T(8,128)(2,1)S(1)}, bf16[256,1024]{1,0:T(8,128)(2,1)S(1)}, u32[]{:S(2)}, u32[]{:S(2)}) %collective-permute-start.4) | collective-permute-done | bytes 524320 | tf_op jit(solution)/shard_map/ppermute | solution.py:81
  66.5 4.6 %collective-permute-done.5 = bf16[256,1024]{1,0:T(8,128)(2,1)} collective-permute-done((bf16[256,1024]{1,0:T(8,128)(2,1)S(1)}, bf16[256,1024]{1,0:T(8,128)(2,1)}, u32[]{:S(2)}, u32[]{:S(2)}) %collective-permute-start.5) | collective-permute-done | bytes 524320 | tf_op jit(solution)/shard_map/ppermute | solution.py:81
  71.1 2.1 %broadcast_select_fusion.2 = (bf16[256,1024]{1,0:T(8,128)(2,1)}, bf16[256,1024]{1,0:T(8,128)(2,1)}) fusion(bf16[256,1024]{1,0:T(8,128)(2,1)S(1)} %collective-permute-done.6, bf16[256,1024]{1,0:T(8,128)(2,1)S(1)} %collective-permute-done.4, pred[]{:T(512)S(6)} %eq.6, bf16[256,1024]{1,0:T(8,128)(2,1)} %collective-permute-done.5), kind=kLoop, calls=%fused_computation.2 | loop fusion | flops 524288 | bytes 2621441 | tf_op jit(solution)/shard_map/jit(_where)/select_n | solution.py:106
  73.2 0.0 copy-done.3
  73.2 4.7 %collective-permute-done.13 = bf16[256,1024]{1,0:T(8,128)(2,1)} collective-permute-done((bf16[256,1024]{1,0:T(8,128)(2,1)}, bf16[256,1024]{1,0:T(8,128)(2,1)}, u32[]{:S(2)}, u32[]{:S(2)}) %collective-permute-start.13) | collective-permute-done | bytes 524320 | tf_op jit(solution)/shard_map/ppermute | solution.py:81
  77.8 11.0 %collective-permute-done.11 = bf16[256,1024]{1,0:T(8,128)(2,1)} collective-permute-done((bf16[256,1024]{1,0:T(8,128)(2,1)S(1)}, bf16[256,1024]{1,0:T(8,128)(2,1)}, u32[]{:S(2)}, u32[]{:S(2)}) %collective-permute-start.11) | collective-permute-done | bytes 524320 | tf_op jit(solution)/shard_map/ppermute | solution.py:81
  88.9 4.3 %collective-permute-done.12 = bf16[256,1024]{1,0:T(8,128)(2,1)} collective-permute-done((bf16[256,1024]{1,0:T(8,128)(2,1)S(1)}, bf16[256,1024]{1,0:T(8,128)(2,1)}, u32[]{:S(2)}, u32[]{:S(2)}) %collective-permute-start.12) | collective-permute-done | bytes 524320 | tf_op jit(solution)/shard_map/ppermute | solution.py:81
  93.1 2.3 %broadcast_select_fusion = (bf16[256,1024]{1,0:T(8,128)(2,1)}, bf16[256,1024]{1,0:T(8,128)(2,1)}) fusion(bf16[256,1024]{1,0:T(8,128)(2,1)} %collective-permute-done.13, bf16[256,1024]{1,0:T(8,128)(2,1)} %collective-permute-done.11, pred[]{:T(512)S(6)} %eq.6, bf16[256,1024]{1,0:T(8,128)(2,1)} %collective-permute-done.12), kind=kLoop, calls=%fused_computation | loop fusion | flops 524288 | bytes 2621441 | tf_op jit(solution)/shard_map/jit(_where)/select_n | solution.py:106
  95.4 15.5 %shard_map.37 = bf16[256,2048]{1,0:T(8,128)(2,1)} custom-call(s32[5]{0:T(128)} %compare_convert_fusion.valid_ref, bf16[256,2048]{1,0:T(8,128)(2,1)} %q_ref.1, bf16[256,1024]{1,0:T(8,128)(2,1)} %copy-done.2, bf16[256,1024]{1,0:T(8,128)(2,1)} %get-tuple-element.8.refs_1_, bf16[256,1024]{1,0:T(8,128)(2,1)} %copy-done, ...), custom_call_target="tpu_custom_call" | custom-call | flops 2684354560 | bytes 7340032 | tf_op jit(solution)/shard_map/pallas_call | solution.py:67
Async XLA Ops:
  0.0 16.9 %collective-permute-start.2 = (bf16[256,1024]{1,0:T(8,128)(2,1)}, bf16[256,1024]{1,0:T(8,128)(2,1)S(1)}, u32[]{:S(2)}, u32[]{:S(2)}) collective-permute-start(bf16[256,1024]{1,0:T(8,128)(2,1)} %refs_4_.1), channel_id=1, source_target_pairs={{0,2},{1,3},{2,4},{3,5},{4,6},{5,7},{6,8},{7,9},{8,10},{9,11},{10,... | collective-permute-start | bytes 1572872 | tf_op jit(solution)/shard_map/ppermute | solution.py:81
  3.4 13.5 %collective-permute-start.1 = (bf16[256,1024]{1,0:T(8,128)(2,1)}, bf16[256,1024]{1,0:T(8,128)(2,1)S(1)}, u32[]{:S(2)}, u32[]{:S(2)}) collective-permute-start(bf16[256,1024]{1,0:T(8,128)(2,1)} %refs_4_.1), channel_id=1, source_target_pairs={{14,16},{15,17},{30,32},{31,33},{46,48},{47,49},{62,64},{63,65},{7... | collective-permute-start | bytes 1572872 | tf_op jit(solution)/shard_map/ppermute | solution.py:81
  4.1 24.0 %collective-permute-start.9 = (bf16[256,1024]{1,0:T(8,128)(2,1)}, bf16[256,1024]{1,0:T(8,128)(2,1)S(1)}, u32[]{:S(2)}, u32[]{:S(2)}) collective-permute-start(bf16[256,1024]{1,0:T(8,128)(2,1)} %refs_9_.1), channel_id=1, source_target_pairs={{0,2},{1,3},{2,4},{3,5},{4,6},{5,7},{6,8},{7,9},{8,10},{9,11},{10,... | collective-permute-start | bytes 1572872 | tf_op jit(solution)/shard_map/ppermute | solution.py:81
  7.2 20.9 %collective-permute-start.8 = (bf16[256,1024]{1,0:T(8,128)(2,1)}, bf16[256,1024]{1,0:T(8,128)(2,1)S(1)}, u32[]{:S(2)}, u32[]{:S(2)}) collective-permute-start(bf16[256,1024]{1,0:T(8,128)(2,1)} %refs_9_.1), channel_id=1, source_target_pairs={{14,16},{15,17},{30,32},{31,33},{46,48},{47,49},{62,64},{63,65},{7... | collective-permute-start | bytes 1572872 | tf_op jit(solution)/shard_map/ppermute | solution.py:81
  7.9 35.1 %collective-permute-start = (bf16[256,1024]{1,0:T(8,128)(2,1)}, bf16[256,1024]{1,0:T(8,128)(2,1)S(1)}, u32[]{:S(2)}, u32[]{:S(2)}) collective-permute-start(bf16[256,1024]{1,0:T(8,128)(2,1)} %refs_4_.1), channel_id=1, source_target_pairs={{12,16},{13,17},{28,32},{29,33},{44,48},{45,49},{60,64},{61,65},{7... | collective-permute-start | bytes 1572872 | tf_op jit(solution)/shard_map/ppermute | solution.py:81
  17.0 26.1 %copy-start = (bf16[256,1024]{1,0:T(8,128)(2,1)}, bf16[256,1024]{1,0:T(8,128)(2,1)S(1)}, u32[]{:S(2)}) copy-start(bf16[256,1024]{1,0:T(8,128)(2,1)S(1)} %broadcast_select_fusion.7.refs_2_) | copy-start | bytes 1572868
  17.0 24.7 %copy-start.4 = (bf16[256,1024]{1,0:T(8,128)(2,1)S(1)}, bf16[256,1024]{1,0:T(8,128)(2,1)}, u32[]{:S(2)}) copy-start(bf16[256,1024]{1,0:T(8,128)(2,1)} %refs_4_.1) | copy-start | bytes 1572868
  17.0 28.0 %collective-permute-start.3 = (bf16[256,1024]{1,0:T(8,128)(2,1)S(1)}, bf16[256,1024]{1,0:T(8,128)(2,1)S(1)}, u32[]{:S(2)}, u32[]{:S(2)}) collective-permute-start(bf16[256,1024]{1,0:T(8,128)(2,1)S(1)} %broadcast_select_fusion.7.refs_2_), channel_id=1, source_target_pairs={{0,2},{1,3},{2,4},{3,5},{4,6},{5,7},{6,8},{7,9},{8,10},{9,11},{10,... | collective-permute-start | bytes 1572872 | tf_op jit(solution)/shard_map/ppermute | solution.py:81
  21.6 24.7 %collective-permute-start.7 = (bf16[256,1024]{1,0:T(8,128)(2,1)}, bf16[256,1024]{1,0:T(8,128)(2,1)S(1)}, u32[]{:S(2)}, u32[]{:S(2)}) collective-permute-start(bf16[256,1024]{1,0:T(8,128)(2,1)} %refs_9_.1), channel_id=1, source_target_pairs={{12,16},{13,17},{28,32},{29,33},{44,48},{45,49},{60,64},{61,65},{7... | collective-permute-start | bytes 1572872 | tf_op jit(solution)/shard_map/ppermute | solution.py:81
  28.2 24.3 %copy-start.1 = (bf16[256,1024]{1,0:T(8,128)(2,1)}, bf16[256,1024]{1,0:T(8,128)(2,1)S(1)}, u32[]{:S(2)}) copy-start(bf16[256,1024]{1,0:T(8,128)(2,1)S(1)} %broadcast_select_fusion.5.refs_7_) | copy-start | bytes 1572868
  28.2 24.3 %collective-permute-start.10 = (bf16[256,1024]{1,0:T(8,128)(2,1)S(1)}, bf16[256,1024]{1,0:T(8,128)(2,1)S(1)}, u32[]{:S(2)}, u32[]{:S(2)}) collective-permute-start(bf16[256,1024]{1,0:T(8,128)(2,1)S(1)} %broadcast_select_fusion.5.refs_7_), channel_id=1, source_target_pairs={{0,2},{1,3},{2,4},{3,5},{4,6},{5,7},{6,8},{7,9},{8,10},{9,11},{10,... | collective-permute-start | bytes 1572872 | tf_op jit(solution)/shard_map/ppermute | solution.py:81
  41.7 13.6 %collective-permute-start.6 = (bf16[256,1024]{1,0:T(8,128)(2,1)S(1)}, bf16[256,1024]{1,0:T(8,128)(2,1)S(1)}, u32[]{:S(2)}, u32[]{:S(2)}) collective-permute-start(bf16[256,1024]{1,0:T(8,128)(2,1)S(1)} %copy-done.4), channel_id=1, source_target_pairs={{0,1},{2,3},{4,5},{6,7},{8,9},{10,11},{12,13},{14,15},{16,17},{18,... | collective-permute-start | bytes 1572872 | tf_op jit(solution)/shard_map/ppermute | solution.py:81
  43.0 23.5 %collective-permute-start.4 = (bf16[256,1024]{1,0:T(8,128)(2,1)S(1)}, bf16[256,1024]{1,0:T(8,128)(2,1)S(1)}, u32[]{:S(2)}, u32[]{:S(2)}) collective-permute-start(bf16[256,1024]{1,0:T(8,128)(2,1)S(1)} %broadcast_select_fusion.7.refs_2_), channel_id=1, source_target_pairs={{0,1},{1,0},{2,3},{3,2},{4,5},{5,4},{6,7},{7,6},{8,9},{9,8},{10,11... | collective-permute-start | bytes 1572872 | tf_op jit(solution)/shard_map/ppermute | solution.py:81
  45.0 9.4 %copy-start.2 = (bf16[256,1024]{1,0:T(8,128)(2,1)}, bf16[256,1024]{1,0:T(8,128)(2,1)S(1)}, u32[]{:S(2)}) copy-start(bf16[256,1024]{1,0:T(8,128)(2,1)S(1)} %broadcast_select_fusion.6.refs_0_) | copy-start | bytes 1572868
  45.0 26.0 %collective-permute-start.5 = (bf16[256,1024]{1,0:T(8,128)(2,1)S(1)}, bf16[256,1024]{1,0:T(8,128)(2,1)}, u32[]{:S(2)}, u32[]{:S(2)}) collective-permute-start(bf16[256,1024]{1,0:T(8,128)(2,1)S(1)} %broadcast_select_fusion.6.refs_0_), channel_id=1, source_target_pairs={{1,0},{3,2},{5,4},{7,6},{9,8},{11,10},{13,12},{15,14},{17,16},{19,... | collective-permute-start | bytes 1572872 | tf_op jit(solution)/shard_map/ppermute | solution.py:81
  46.3 31.5 %collective-permute-start.13 = (bf16[256,1024]{1,0:T(8,128)(2,1)}, bf16[256,1024]{1,0:T(8,128)(2,1)}, u32[]{:S(2)}, u32[]{:S(2)}) collective-permute-start(bf16[256,1024]{1,0:T(8,128)(2,1)} %refs_9_.1), channel_id=1, source_target_pairs={{0,1},{2,3},{4,5},{6,7},{8,9},{10,11},{12,13},{14,15},{16,17},{18,... | collective-permute-start | bytes 1572872 | tf_op jit(solution)/shard_map/ppermute | solution.py:81
  52.5 36.4 %collective-permute-start.11 = (bf16[256,1024]{1,0:T(8,128)(2,1)S(1)}, bf16[256,1024]{1,0:T(8,128)(2,1)}, u32[]{:S(2)}, u32[]{:S(2)}) collective-permute-start(bf16[256,1024]{1,0:T(8,128)(2,1)S(1)} %broadcast_select_fusion.5.refs_7_), channel_id=1, source_target_pairs={{0,1},{1,0},{2,3},{3,2},{4,5},{5,4},{6,7},{7,6},{8,9},{9,8},{10,11... | collective-permute-start | bytes 1572872 | tf_op jit(solution)/shard_map/ppermute | solution.py:81
  54.5 18.7 %copy-start.3 = (bf16[256,1024]{1,0:T(8,128)(2,1)}, bf16[256,1024]{1,0:T(8,128)(2,1)S(1)}, u32[]{:S(2)}) copy-start(bf16[256,1024]{1,0:T(8,128)(2,1)S(1)} %broadcast_select_fusion.4.refs_5_) | copy-start | bytes 1572868
  55.3 37.9 %collective-permute-start.12 = (bf16[256,1024]{1,0:T(8,128)(2,1)S(1)}, bf16[256,1024]{1,0:T(8,128)(2,1)}, u32[]{:S(2)}, u32[]{:S(2)}) collective-permute-start(bf16[256,1024]{1,0:T(8,128)(2,1)S(1)} %broadcast_select_fusion.4.refs_5_), channel_id=1, source_target_pairs={{1,0},{3,2},{5,4},{7,6},{9,8},{11,10},{13,12},{15,14},{17,16},{19,... | collective-permute-start | bytes 1572872 | tf_op jit(solution)/shard_map/ppermute | solution.py:81

commit v12 on v9

--- a/solution.py
+++ b/solution.py
@@ -87,17 +87,18 @@
     block_index = lax.axis_index(axis)
     own = (keys, values)
     plane = 2 * lax.axis_size("grp")
+    back = WINDOW // queries.shape[0]
 
     def crossing(t):
-        return t % plane < 2
+        return t % plane < back
 
     ahead2 = [(i, i + 2) for i in range(n) if i + 2 < n]
     x1 = shifted(own, axis, ahead2)
     y1 = shifted(own, axis, [(i, i + 1) for i in range(0, n, 2)])
     far = shifted(own, axis, [(i, i + 4) for i in range(n) if i + 4 < n and crossing(i + 4)])
     x2 = shifted(x1, axis, [(i, i + 2) for i in range(n) if i + 2 < n and not crossing(i + 2)])
-    first_two = (block_index % plane) < 2
-    b4 = [jnp.where(first_two, a, b) for a, b in zip(far, x2)]
+    first_few = (block_index % plane) < back
+    b4 = [jnp.where(first_few, a, b) for a, b in zip(far, x2)]
     y2 = shifted(x1, axis, [(i, i ^ 1) for i in range(n)])
     y3 = shifted(b4, axis, [(i, i - 1) for i in range(1, n, 2)])
     odd = (block_index % 2) == 1

time: 109 us -> 116 us (1.064)
  the two profiles are of different devices: /device:TPU:484 before, /device:TPU:206 now
where the time goes in v12:
time: 116 us; the launch traced here: 115 us
  waiting for transfers between devices  65.8 us (57%)
  starting transfers between devices  28.6 us (25%)
  Pallas kernels  15.5 us (13%)
  other arithmetic  4.88 us (4%)
    ppermute x12, waiting for transfers between devices, shifted(): return lax.ppermute(x, axis, pairs)  65.8 us
    ppermute x12, starting transfers between devices, shifted(): return lax.ppermute(x, axis, pairs)  28.6 us
    pallas_call x1, Pallas kernels, attend(): pl.pallas_call(attend_kernel, grid=(KV_HEADS,), in_specs=[pl.BlockSpec(me...  15.5 us
    select_n x2, other arithmetic, body(): b1 = [jnp.where(odd, a, b) for a, b in zip(y1, y2)]  4.25 us
  transfers between devices with their start and end apart: 12, of which 8 were waited for; matrix products, arithmetic and copies ran while one was open for 2% of the time, Pallas kernels for 0%

profile of v12, /device:TPU:206, one launch (start us, length us, event | category | flops | bytes accessed | tf_op | source)
XLA Modules:
  0.0 115.1 jit_solution(11765243504400503155)
XLA Ops:
  0.0 1.9 %collective-permute-start.1 = (bf16[256,1024]{1,0:T(8,128)(2,1)}, bf16[256,1024]{1,0:T(8,128)(2,1)}, u32[]{:S(2)}, u32[]{:S(2)}) collective-permute-start(bf16[256,1024]{1,0:T(8,128)(2,1)} %refs_4_.1), channel_id=1, source_target_pairs={{0,2},{1,3},{2,4},{3,5},{4,6},{5,7},{6,8},{7,9},{8,10},{9,11},{10,... | collective-permute-start | bytes 1572872 | tf_op jit(solution)/shard_map/ppermute | solution.py:81
  1.9 3.0 %collective-permute-start.7 = (bf16[256,1024]{1,0:T(8,128)(2,1)}, bf16[256,1024]{1,0:T(8,128)(2,1)}, u32[]{:S(2)}, u32[]{:S(2)}) collective-permute-start(bf16[256,1024]{1,0:T(8,128)(2,1)} %refs_9_.1), channel_id=1, source_target_pairs={{0,2},{1,3},{2,4},{3,5},{4,6},{5,7},{6,8},{7,9},{8,10},{9,11},{10,... | collective-permute-start | bytes 1572872 | tf_op jit(solution)/shard_map/ppermute | solution.py:81
  5.0 0.7 collective-permute-start
  5.7 12.1 %collective-permute-done.1.refs_2_ = bf16[256,1024]{1,0:T(8,128)(2,1)} collective-permute-done((bf16[256,1024]{1,0:T(8,128)(2,1)}, bf16[256,1024]{1,0:T(8,128)(2,1)}, u32[]{:S(2)}, u32[]{:S(2)}) %collective-permute-start.1) | collective-permute-done | bytes 524320 | tf_op jit(solution)/shard_map/ppermute | solution.py:81
  17.8 1.9 %collective-permute-start.2 = (bf16[256,1024]{1,0:T(8,128)(2,1)}, bf16[256,1024]{1,0:T(8,128)(2,1)S(1)}, u32[]{:S(2)}, u32[]{:S(2)}) collective-permute-start(bf16[256,1024]{1,0:T(8,128)(2,1)} %collective-permute-done.1.refs_2_), channel_id=1, source_target_pairs={{2,4},{3,5},{4,6},{5,7},{6,8},{7,9},{8,10},{9,11},{10,12},{11,13},... | collective-permute-start | bytes 1572872 | tf_op jit(solution)/shard_map/ppermute | solution.py:81
  19.7 0.7 collective-permute-start.6
  20.4 13.5 %collective-permute-done.7.refs_7_ = bf16[256,1024]{1,0:T(8,128)(2,1)} collective-permute-done((bf16[256,1024]{1,0:T(8,128)(2,1)}, bf16[256,1024]{1,0:T(8,128)(2,1)}, u32[]{:S(2)}, u32[]{:S(2)}) %collective-permute-start.7) | collective-permute-done | bytes 524320 | tf_op jit(solution)/shard_map/ppermute | solution.py:81
  33.9 1.9 %collective-permute-start.8 = (bf16[256,1024]{1,0:T(8,128)(2,1)}, bf16[256,1024]{1,0:T(8,128)(2,1)S(1)}, u32[]{:S(2)}, u32[]{:S(2)}) collective-permute-start(bf16[256,1024]{1,0:T(8,128)(2,1)} %collective-permute-done.7.refs_7_), channel_id=1, source_target_pairs={{2,4},{3,5},{4,6},{5,7},{6,8},{7,9},{8,10},{9,11},{10,12},{11,13},... | collective-permute-start | bytes 1572872 | tf_op jit(solution)/shard_map/ppermute | solution.py:81
  35.8 1.3 %collective-permute-start.5 = (bf16[256,1024]{1,0:T(8,128)(2,1)}, bf16[256,1024]{1,0:T(8,128)(2,1)S(1)}, u32[]{:S(2)}, u32[]{:S(2)}) collective-permute-start(bf16[256,1024]{1,0:T(8,128)(2,1)} %refs_4_.1), channel_id=1, source_target_pairs={{0,1},{2,3},{4,5},{6,7},{8,9},{10,11},{12,13},{14,15},{16,17},{18,... | collective-permute-start | bytes 1572872 | tf_op jit(solution)/shard_map/ppermute | solution.py:81
  37.1 0.0 collective-permute-done
  37.1 8.6 %collective-permute-start.3 = (bf16[256,1024]{1,0:T(8,128)(2,1)}, bf16[256,1024]{1,0:T(8,128)(2,1)}, u32[]{:S(2)}, u32[]{:S(2)}) collective-permute-start(bf16[256,1024]{1,0:T(8,128)(2,1)} %collective-permute-done.1.refs_2_), channel_id=1, source_target_pairs={{0,1},{1,0},{2,3},{3,2},{4,5},{5,4},{6,7},{7,6},{8,9},{9,8},{10,11... | collective-permute-start | bytes 1572872 | tf_op jit(solution)/shard_map/ppermute | solution.py:81
  45.8 4.8 %collective-permute-done.2 = bf16[256,1024]{1,0:T(8,128)(2,1)S(1)} collective-permute-done((bf16[256,1024]{1,0:T(8,128)(2,1)}, bf16[256,1024]{1,0:T(8,128)(2,1)S(1)}, u32[]{:S(2)}, u32[]{:S(2)}) %collective-permute-start.2) | collective-permute-done | bytes 524320 | tf_op jit(solution)/shard_map/ppermute | solution.py:81
  50.6 0.1 broadcast_select_fusion.5.refs_0_
  50.7 0.0 copy-start
  50.7 3.2 %collective-permute-start.4 = (bf16[256,1024]{1,0:T(8,128)(2,1)S(1)}, bf16[256,1024]{1,0:T(8,128)(2,1)}, u32[]{:S(2)}, u32[]{:S(2)}) collective-permute-start(bf16[256,1024]{1,0:T(8,128)(2,1)S(1)} %broadcast_select_fusion.5.refs_0_), channel_id=1, source_target_pairs={{1,0},{3,2},{5,4},{7,6},{9,8},{11,10},{13,12},{15,14},{17,16},{19,... | collective-permute-start | bytes 1572872 | tf_op jit(solution)/shard_map/ppermute | solution.py:81
  53.8 0.0 collective-permute-done.6
  53.8 1.3 %collective-permute-start.11 = (bf16[256,1024]{1,0:T(8,128)(2,1)}, bf16[256,1024]{1,0:T(8,128)(2,1)S(1)}, u32[]{:S(2)}, u32[]{:S(2)}) collective-permute-start(bf16[256,1024]{1,0:T(8,128)(2,1)} %refs_9_.1), channel_id=1, source_target_pairs={{0,1},{2,3},{4,5},{6,7},{8,9},{10,11},{12,13},{14,15},{16,17},{18,... | collective-permute-start | bytes 1572872 | tf_op jit(solution)/shard_map/ppermute | solution.py:81
  55.1 5.6 %collective-permute-done.8 = bf16[256,1024]{1,0:T(8,128)(2,1)S(1)} collective-permute-done((bf16[256,1024]{1,0:T(8,128)(2,1)}, bf16[256,1024]{1,0:T(8,128)(2,1)S(1)}, u32[]{:S(2)}, u32[]{:S(2)}) %collective-permute-start.8) | collective-permute-done | bytes 524320 | tf_op jit(solution)/shard_map/ppermute | solution.py:81
  60.7 2.3 %collective-permute-start.9 = (bf16[256,1024]{1,0:T(8,128)(2,1)}, bf16[256,1024]{1,0:T(8,128)(2,1)}, u32[]{:S(2)}, u32[]{:S(2)}) collective-permute-start(bf16[256,1024]{1,0:T(8,128)(2,1)} %collective-permute-done.7.refs_7_), channel_id=1, source_target_pairs={{0,1},{1,0},{2,3},{3,2},{4,5},{5,4},{6,7},{7,6},{8,9},{9,8},{10,11... | collective-permute-start | bytes 1572872 | tf_op jit(solution)/shard_map/ppermute | solution.py:81
  63.1 0.1 broadcast_select_fusion.4.refs_5_
  63.1 0.0 copy-done
  63.1 0.0 copy-start.1
  63.1 1.8 %collective-permute-done.5 = bf16[256,1024]{1,0:T(8,128)(2,1)S(1)} collective-permute-done((bf16[256,1024]{1,0:T(8,128)(2,1)}, bf16[256,1024]{1,0:T(8,128)(2,1)S(1)}, u32[]{:S(2)}, u32[]{:S(2)}) %collective-permute-start.5) | collective-permute-done | bytes 524320 | tf_op jit(solution)/shard_map/ppermute | solution.py:81
  64.9 1.8 %collective-permute-start.10 = (bf16[256,1024]{1,0:T(8,128)(2,1)S(1)}, bf16[256,1024]{1,0:T(8,128)(2,1)S(1)}, u32[]{:S(2)}, u32[]{:S(2)}) collective-permute-start(bf16[256,1024]{1,0:T(8,128)(2,1)S(1)} %broadcast_select_fusion.4.refs_5_), channel_id=1, source_target_pairs={{1,0},{3,2},{5,4},{7,6},{9,8},{11,10},{13,12},{15,14},{17,16},{19,... | collective-permute-start | bytes 1572872 | tf_op jit(solution)/shard_map/ppermute | solution.py:81
  66.7 0.5 compare_convert_fusion.valid_ref
  67.2 9.0 %collective-permute-done.3 = bf16[256,1024]{1,0:T(8,128)(2,1)} collective-permute-done((bf16[256,1024]{1,0:T(8,128)(2,1)}, bf16[256,1024]{1,0:T(8,128)(2,1)}, u32[]{:S(2)}, u32[]{:S(2)}) %collective-permute-start.3) | collective-permute-done | bytes 524320 | tf_op jit(solution)/shard_map/ppermute | solution.py:81
  76.2 0.0 collective-permute-done.4
  76.2 2.1 %broadcast_select_fusion.2 = (bf16[256,1024]{1,0:T(8,128)(2,1)}, bf16[256,1024]{1,0:T(8,128)(2,1)}) fusion(bf16[256,1024]{1,0:T(8,128)(2,1)S(1)} %collective-permute-done.5, bf16[256,1024]{1,0:T(8,128)(2,1)} %collective-permute-done.3, pred[]{:T(512)S(6)} %eq.6, bf16[256,1024]{1,0:T(8,128)(2,1)} %collective-permute-done.4), kind=kLoop, calls=%fused_computation.2 | loop fusion | flops 524288 | bytes 2621441 | tf_op jit(solution)/shard_map/jit(_where)/select_n | solution.py:105
  78.4 0.0 copy-done.1
  78.4 9.0 %collective-permute-done.11 = bf16[256,1024]{1,0:T(8,128)(2,1)S(1)} collective-permute-done((bf16[256,1024]{1,0:T(8,128)(2,1)}, bf16[256,1024]{1,0:T(8,128)(2,1)S(1)}, u32[]{:S(2)}, u32[]{:S(2)}) %collective-permute-start.11) | collective-permute-done | bytes 524320 | tf_op jit(solution)/shard_map/ppermute | solution.py:81
  87.4 10.0 %collective-permute-done.9 = bf16[256,1024]{1,0:T(8,128)(2,1)} collective-permute-done((bf16[256,1024]{1,0:T(8,128)(2,1)}, bf16[256,1024]{1,0:T(8,128)(2,1)}, u32[]{:S(2)}, u32[]{:S(2)}) %collective-permute-start.9) | collective-permute-done | bytes 524320 | tf_op jit(solution)/shard_map/ppermute | solution.py:81
  97.4 0.0 collective-permute-done.10
  97.4 2.1 %broadcast_select_fusion = (bf16[256,1024]{1,0:T(8,128)(2,1)}, bf16[256,1024]{1,0:T(8,128)(2,1)}) fusion(bf16[256,1024]{1,0:T(8,128)(2,1)S(1)} %collective-permute-done.11, bf16[256,1024]{1,0:T(8,128)(2,1)} %collective-permute-done.9, pred[]{:T(512)S(6)} %eq.6, bf16[256,1024]{1,0:T(8,128)(2,1)S(1)} %collective-permute-done.10), kind=kLoop, calls=%fused_computation | loop fusion | flops 524288 | bytes 2621441 | tf_op jit(solution)/shard_map/jit(_where)/select_n | solution.py:105
  99.5 15.5 %shard_map.37 = bf16[256,2048]{1,0:T(8,128)(2,1)} custom-call(s32[5]{0:T(128)} %compare_convert_fusion.valid_ref, bf16[256,2048]{1,0:T(8,128)(2,1)} %q_ref.1, bf16[256,1024]{1,0:T(8,128)(2,1)} %copy-done, bf16[256,1024]{1,0:T(8,128)(2,1)} %get-tuple-element.8.refs_1_, bf16[256,1024]{1,0:T(8,128)(2,1)} %collective-permute-done.1.refs_2_, ...), custom_call_target="tpu_custom_call" | custom-call | flops 2684354560 | bytes 7340032 | tf_op jit(solution)/shard_map/pallas_call | solution.py:67
Async XLA Ops:
  0.0 17.8 %collective-permute-start.1 = (bf16[256,1024]{1,0:T(8,128)(2,1)}, bf16[256,1024]{1,0:T(8,128)(2,1)}, u32[]{:S(2)}, u32[]{:S(2)}) collective-permute-start(bf16[256,1024]{1,0:T(8,128)(2,1)} %refs_4_.1), channel_id=1, source_target_pairs={{0,2},{1,3},{2,4},{3,5},{4,6},{5,7},{6,8},{7,9},{8,10},{9,11},{10,... | collective-permute-start | bytes 1572872 | tf_op jit(solution)/shard_map/ppermute | solution.py:81
  1.9 31.9 %collective-permute-start.7 = (bf16[256,1024]{1,0:T(8,128)(2,1)}, bf16[256,1024]{1,0:T(8,128)(2,1)}, u32[]{:S(2)}, u32[]{:S(2)}) collective-permute-start(bf16[256,1024]{1,0:T(8,128)(2,1)} %refs_9_.1), channel_id=1, source_target_pairs={{0,2},{1,3},{2,4},{3,5},{4,6},{5,7},{6,8},{7,9},{8,10},{9,11},{10,... | collective-permute-start | bytes 1572872 | tf_op jit(solution)/shard_map/ppermute | solution.py:81
  5.0 32.1 %collective-permute-start = (bf16[256,1024]{1,0:T(8,128)(2,1)}, bf16[256,1024]{1,0:T(8,128)(2,1)S(1)}, u32[]{:S(2)}, u32[]{:S(2)}) collective-permute-start(bf16[256,1024]{1,0:T(8,128)(2,1)} %refs_4_.1), channel_id=1, source_target_pairs={{12,16},{13,17},{14,18},{15,19},{28,32},{29,33},{30,34},{31,35},{4... | collective-permute-start | bytes 1572872 | tf_op jit(solution)/shard_map/ppermute | solution.py:81
  17.8 32.8 %collective-permute-start.2 = (bf16[256,1024]{1,0:T(8,128)(2,1)}, bf16[256,1024]{1,0:T(8,128)(2,1)S(1)}, u32[]{:S(2)}, u32[]{:S(2)}) collective-permute-start(bf16[256,1024]{1,0:T(8,128)(2,1)} %collective-permute-done.1.refs_2_), channel_id=1, source_target_pairs={{2,4},{3,5},{4,6},{5,7},{6,8},{7,9},{8,10},{9,11},{10,12},{11,13},... | collective-permute-start | bytes 1572872 | tf_op jit(solution)/shard_map/ppermute | solution.py:81
  19.7 34.1 %collective-permute-start.6 = (bf16[256,1024]{1,0:T(8,128)(2,1)}, bf16[256,1024]{1,0:T(8,128)(2,1)S(1)}, u32[]{:S(2)}, u32[]{:S(2)}) collective-permute-start(bf16[256,1024]{1,0:T(8,128)(2,1)} %refs_9_.1), channel_id=1, source_target_pairs={{12,16},{13,17},{14,18},{15,19},{28,32},{29,33},{30,34},{31,35},{4... | collective-permute-start | bytes 1572872 | tf_op jit(solution)/shard_map/ppermute | solution.py:81
  33.9 26.8 %collective-permute-start.8 = (bf16[256,1024]{1,0:T(8,128)(2,1)}, bf16[256,1024]{1,0:T(8,128)(2,1)S(1)}, u32[]{:S(2)}, u32[]{:S(2)}) collective-permute-start(bf16[256,1024]{1,0:T(8,128)(2,1)} %collective-permute-done.7.refs_7_), channel_id=1, source_target_pairs={{2,4},{3,5},{4,6},{5,7},{6,8},{7,9},{8,10},{9,11},{10,12},{11,13},... | collective-permute-start | bytes 1572872 | tf_op jit(solution)/shard_map/ppermute | solution.py:81
  35.8 29.1 %collective-permute-start.5 = (bf16[256,1024]{1,0:T(8,128)(2,1)}, bf16[256,1024]{1,0:T(8,128)(2,1)S(1)}, u32[]{:S(2)}, u32[]{:S(2)}) collective-permute-start(bf16[256,1024]{1,0:T(8,128)(2,1)} %refs_4_.1), channel_id=1, source_target_pairs={{0,1},{2,3},{4,5},{6,7},{8,9},{10,11},{12,13},{14,15},{16,17},{18,... | collective-permute-start | bytes 1572872 | tf_op jit(solution)/shard_map/ppermute | solution.py:81
  37.1 39.1 %collective-permute-start.3 = (bf16[256,1024]{1,0:T(8,128)(2,1)}, bf16[256,1024]{1,0:T(8,128)(2,1)}, u32[]{:S(2)}, u32[]{:S(2)}) collective-permute-start(bf16[256,1024]{1,0:T(8,128)(2,1)} %collective-permute-done.1.refs_2_), channel_id=1, source_target_pairs={{0,1},{1,0},{2,3},{3,2},{4,5},{5,4},{6,7},{7,6},{8,9},{9,8},{10,11... | collective-permute-start | bytes 1572872 | tf_op jit(solution)/shard_map/ppermute | solution.py:81
  50.7 12.5 %copy-start = (bf16[256,1024]{1,0:T(8,128)(2,1)}, bf16[256,1024]{1,0:T(8,128)(2,1)S(1)}, u32[]{:S(2)}) copy-start(bf16[256,1024]{1,0:T(8,128)(2,1)S(1)} %broadcast_select_fusion.5.refs_0_) | copy-start | bytes 1572868
  50.7 25.6 %collective-permute-start.4 = (bf16[256,1024]{1,0:T(8,128)(2,1)S(1)}, bf16[256,1024]{1,0:T(8,128)(2,1)}, u32[]{:S(2)}, u32[]{:S(2)}) collective-permute-start(bf16[256,1024]{1,0:T(8,128)(2,1)S(1)} %broadcast_select_fusion.5.refs_0_), channel_id=1, source_target_pairs={{1,0},{3,2},{5,4},{7,6},{9,8},{11,10},{13,12},{15,14},{17,16},{19,... | collective-permute-start | bytes 1572872 | tf_op jit(solution)/shard_map/ppermute | solution.py:81
  53.8 33.5 %collective-permute-start.11 = (bf16[256,1024]{1,0:T(8,128)(2,1)}, bf16[256,1024]{1,0:T(8,128)(2,1)S(1)}, u32[]{:S(2)}, u32[]{:S(2)}) collective-permute-start(bf16[256,1024]{1,0:T(8,128)(2,1)} %refs_9_.1), channel_id=1, source_target_pairs={{0,1},{2,3},{4,5},{6,7},{8,9},{10,11},{12,13},{14,15},{16,17},{18,... | collective-permute-start | bytes 1572872 | tf_op jit(solution)/shard_map/ppermute | solution.py:81
  60.7 36.7 %collective-permute-start.9 = (bf16[256,1024]{1,0:T(8,128)(2,1)}, bf16[256,1024]{1,0:T(8,128)(2,1)}, u32[]{:S(2)}, u32[]{:S(2)}) collective-permute-start(bf16[256,1024]{1,0:T(8,128)(2,1)} %collective-permute-done.7.refs_7_), channel_id=1, source_target_pairs={{0,1},{1,0},{2,3},{3,2},{4,5},{5,4},{6,7},{7,6},{8,9},{9,8},{10,11... | collective-permute-start | bytes 1572872 | tf_op jit(solution)/shard_map/ppermute | solution.py:81
  63.1 15.2 %copy-start.1 = (bf16[256,1024]{1,0:T(8,128)(2,1)}, bf16[256,1024]{1,0:T(8,128)(2,1)S(1)}, u32[]{:S(2)}) copy-start(bf16[256,1024]{1,0:T(8,128)(2,1)S(1)} %broadcast_select_fusion.4.refs_5_) | copy-start | bytes 1572868
  64.9 32.5 %collective-permute-start.10 = (bf16[256,1024]{1,0:T(8,128)(2,1)S(1)}, bf16[256,1024]{1,0:T(8,128)(2,1)S(1)}, u32[]{:S(2)}, u32[]{:S(2)}) collective-permute-start(bf16[256,1024]{1,0:T(8,128)(2,1)S(1)} %broadcast_select_fusion.4.refs_5_), channel_id=1, source_target_pairs={{1,0},{3,2},{5,4},{7,6},{9,8},{11,10},{13,12},{15,14},{17,16},{19,... | collective-permute-start | bytes 1572872 | tf_op jit(solution)/shard_map/ppermute | solution.py:81

commit v13 on v9

--- a/solution.py
+++ b/solution.py
@@ -22,38 +22,51 @@
     nblk = (len(refs) - 1) // 2
     k_refs, v_refs, o_ref = refs[:nblk], refs[nblk:2 * nblk], refs[-1]
     tok = q_ref.shape[0]
-    row = lax.broadcasted_iota(jnp.int32, (tok, tok), 0)
-    col = lax.broadcasted_iota(jnp.int32, (tok, tok), 1)
+    half = tok // 2
     group = HEADS // KV_HEADS
-    for a in range(group):
-        qa = q_ref[:, a * HEAD_DIM:(a + 1) * HEAD_DIM]
-        scores = []
+    for r in range(2):
+        rows = slice(r * half, (r + 1) * half)
+        spans = []
         for j in range(nblk):
-            s = lax.dot_general(
-                qa, k_refs[j][...], (((1,), (1,)), ((), ())),
-                preferred_element_type=jnp.float32,
-            ) * HEAD_DIM ** (-0.5)
-            if j == 0:
-                s = jnp.where((col > row) & (valid_ref[0] > 0), s, NEG)
-            elif j == nblk - 1:
-                s = jnp.where(col <= row, s, NEG)
+            if j == 0 and r == 1:
+                spans.append(slice(half, tok))
+            elif j == nblk - 1 and r == 0:
+                spans.append(slice(0, half))
             else:
-                s = jnp.where(valid_ref[j] > 0, s, NEG)
-            scores.append(s)
-        largest = scores[0].max(axis=1, keepdims=True)
-        for s in scores[1:]:
-            largest = jnp.maximum(largest, s.max(axis=1, keepdims=True))
-        expos = [jnp.exp(s - largest) for s in scores]
-        total = expos[0].sum(axis=1, keepdims=True)
-        for e in expos[1:]:
-            total = total + e.sum(axis=1, keepdims=True)
-        inv = 1.0 / total
-        out = None
-        for j in range(nblk):
-            w = (expos[j] * inv).astype(jnp.bfloat16)
-            part = jnp.dot(w, v_refs[j][...], preferred_element_type=jnp.float32)
-            out = part if out is None else out + part
-        o_ref[:, a * HEAD_DIM:(a + 1) * HEAD_DIM] = out.astype(o_ref.dtype)
+                spans.append(slice(0, tok))
+        for a in range(group):
+            qa = q_ref[rows, a * HEAD_DIM:(a + 1) * HEAD_DIM]
+            scores = []
+            for j in range(nblk):
+                cs = spans[j]
+                width = cs.stop - cs.start
+                s = lax.dot_general(
+                    qa, k_refs[j][cs, :], (((1,), (1,)), ((), ())),
+                    preferred_element_type=jnp.float32,
+                ) * HEAD_DIM ** (-0.5)
+                row = lax.broadcasted_iota(jnp.int32, (half, width), 0) + r * half
+                col = lax.broadcasted_iota(jnp.int32, (half, width), 1) + cs.start
+                if j == 0:
+                    s = jnp.where((col > row) & (valid_ref[0] > 0), s, NEG)
+                elif j == nblk - 1:
+                    s = jnp.where(col <= row, s, NEG)
+                else:
+                    s = jnp.where(valid_ref[j] > 0, s, NEG)
+                scores.append(s)
+            largest = scores[0].max(axis=1, keepdims=True)
+            for s in scores[1:]:
+                largest = jnp.maximum(largest, s.max(axis=1, keepdims=True))
+            expos = [jnp.exp(s - largest) for s in scores]
+            total = expos[0].sum(axis=1, keepdims=True)
+            for e in expos[1:]:
+                total = total + e.sum(axis=1, keepdims=True)
+            inv = 1.0 / total
+            out = None
+            for j in range(nblk):
+                w = (expos[j] * inv).astype(jnp.bfloat16)
+                part = jnp.dot(w, v_refs[j][spans[j], :], preferred_element_type=jnp.float32)
+                out = part if out is None else out + part
+            o_ref[rows, a * HEAD_DIM:(a + 1) * HEAD_DIM] = out.astype(o_ref.dtype)
 
 
 def attend(valid, queries, k_blocks, v_blocks):

time: 109 us -> 114 us (1.046)
  the two profiles are of different devices: /device:TPU:484 before, /device:TPU:452 now
where the time goes in v13:
time: 114 us; the launch traced here: 113 us
  waiting for transfers between devices  57.7 us (51%)
  starting transfers between devices  30.3 us (27%)
  Pallas kernels  20.1 us (18%)
  other arithmetic  5.04 us (4%)
    ppermute x12, waiting for transfers between devices, shifted(): return lax.ppermute(x, axis, pairs)  57.7 us
    ppermute x12, starting transfers between devices, shifted(): return lax.ppermute(x, axis, pairs)  30.3 us
    pallas_call x1, Pallas kernels, attend(): pl.pallas_call(attend_kernel, grid=(KV_HEADS,), in_specs=[pl.BlockSpec(me...  20.1 us
    select_n x2, other arithmetic, body(): b1 = [jnp.where(odd, a, b) for a, b in zip(y1, y2)]  4.4 us
  transfers between devices with their start and end apart: 12, of which 9 were waited for; matrix products, arithmetic and copies ran while one was open for 3% of the time, Pallas kernels for 0%

profile of v13, /device:TPU:452, one launch (start us, length us, event | category | flops | bytes accessed | tf_op | source)
XLA Modules:
  0.0 113.4 jit_solution(12537982484447890646)
XLA Ops:
  0.0 3.1 %collective-permute-start.1 = (bf16[256,1024]{1,0:T(8,128)(2,1)}, bf16[256,1024]{1,0:T(8,128)(2,1)}, u32[]{:S(2)}, u32[]{:S(2)}) collective-permute-start(bf16[256,1024]{1,0:T(8,128)(2,1)} %refs_4_.1), channel_id=1, source_target_pairs={{0,2},{1,3},{2,4},{3,5},{4,6},{5,7},{6,8},{7,9},{8,10},{9,11},{10,... | collective-permute-start | bytes 1572872 | tf_op jit(solution)/shard_map/ppermute | solution.py:94
  3.1 1.9 %collective-permute-start.7 = (bf16[256,1024]{1,0:T(8,128)(2,1)}, bf16[256,1024]{1,0:T(8,128)(2,1)}, u32[]{:S(2)}, u32[]{:S(2)}) collective-permute-start(bf16[256,1024]{1,0:T(8,128)(2,1)} %refs_9_.1), channel_id=1, source_target_pairs={{0,2},{1,3},{2,4},{3,5},{4,6},{5,7},{6,8},{7,9},{8,10},{9,11},{10,... | collective-permute-start | bytes 1572872 | tf_op jit(solution)/shard_map/ppermute | solution.py:94
  5.0 0.7 collective-permute-start
  5.7 11.7 %collective-permute-done.1.refs_2_ = bf16[256,1024]{1,0:T(8,128)(2,1)} collective-permute-done((bf16[256,1024]{1,0:T(8,128)(2,1)}, bf16[256,1024]{1,0:T(8,128)(2,1)}, u32[]{:S(2)}, u32[]{:S(2)}) %collective-permute-start.1) | collective-permute-done | bytes 524320 | tf_op jit(solution)/shard_map/ppermute | solution.py:94
  17.4 4.9 %collective-permute-start.2 = (bf16[256,1024]{1,0:T(8,128)(2,1)}, bf16[256,1024]{1,0:T(8,128)(2,1)S(1)}, u32[]{:S(2)}, u32[]{:S(2)}) collective-permute-start(bf16[256,1024]{1,0:T(8,128)(2,1)} %collective-permute-done.1.refs_2_), channel_id=1, source_target_pairs={{0,2},{1,3},{2,4},{3,5},{4,6},{5,7},{6,8},{7,9},{8,10},{9,11},{10,... | collective-permute-start | bytes 1572872 | tf_op jit(solution)/shard_map/ppermute | solution.py:94
  22.3 0.7 collective-permute-start.6
  23.0 15.2 %collective-permute-done.7.refs_7_ = bf16[256,1024]{1,0:T(8,128)(2,1)} collective-permute-done((bf16[256,1024]{1,0:T(8,128)(2,1)}, bf16[256,1024]{1,0:T(8,128)(2,1)}, u32[]{:S(2)}, u32[]{:S(2)}) %collective-permute-start.7) | collective-permute-done | bytes 524320 | tf_op jit(solution)/shard_map/ppermute | solution.py:94
  38.2 4.4 %collective-permute-start.8 = (bf16[256,1024]{1,0:T(8,128)(2,1)}, bf16[256,1024]{1,0:T(8,128)(2,1)S(1)}, u32[]{:S(2)}, u32[]{:S(2)}) collective-permute-start(bf16[256,1024]{1,0:T(8,128)(2,1)} %collective-permute-done.7.refs_7_), channel_id=1, source_target_pairs={{0,2},{1,3},{2,4},{3,5},{4,6},{5,7},{6,8},{7,9},{8,10},{9,11},{10,... | collective-permute-start | bytes 1572872 | tf_op jit(solution)/shard_map/ppermute | solution.py:94
  42.6 1.3 %collective-permute-start.5 = (bf16[256,1024]{1,0:T(8,128)(2,1)}, bf16[256,1024]{1,0:T(8,128)(2,1)S(1)}, u32[]{:S(2)}, u32[]{:S(2)}) collective-permute-start(bf16[256,1024]{1,0:T(8,128)(2,1)} %refs_4_.1), channel_id=1, source_target_pairs={{0,1},{2,3},{4,5},{6,7},{8,9},{10,11},{12,13},{14,15},{16,17},{18,... | collective-permute-start | bytes 1572872 | tf_op jit(solution)/shard_map/ppermute | solution.py:94
  43.9 0.0 collective-permute-done
  43.9 1.9 %collective-permute-start.3 = (bf16[256,1024]{1,0:T(8,128)(2,1)}, bf16[256,1024]{1,0:T(8,128)(2,1)}, u32[]{:S(2)}, u32[]{:S(2)}) collective-permute-start(bf16[256,1024]{1,0:T(8,128)(2,1)} %collective-permute-done.1.refs_2_), channel_id=1, source_target_pairs={{0,1},{1,0},{2,3},{3,2},{4,5},{5,4},{6,7},{7,6},{8,9},{9,8},{10,11... | collective-permute-start | bytes 1572872 | tf_op jit(solution)/shard_map/ppermute | solution.py:94
  45.9 3.6 %collective-permute-done.2 = bf16[256,1024]{1,0:T(8,128)(2,1)S(1)} collective-permute-done((bf16[256,1024]{1,0:T(8,128)(2,1)}, bf16[256,1024]{1,0:T(8,128)(2,1)S(1)}, u32[]{:S(2)}, u32[]{:S(2)}) %collective-permute-start.2) | collective-permute-done | bytes 524320 | tf_op jit(solution)/shard_map/ppermute | solution.py:94
  49.4 0.1 broadcast_select_fusion.5.refs_0_
  49.5 0.0 copy-start
  49.5 1.3 %collective-permute-start.4 = (bf16[256,1024]{1,0:T(8,128)(2,1)S(1)}, bf16[256,1024]{1,0:T(8,128)(2,1)}, u32[]{:S(2)}, u32[]{:S(2)}) collective-permute-start(bf16[256,1024]{1,0:T(8,128)(2,1)S(1)} %broadcast_select_fusion.5.refs_0_), channel_id=1, source_target_pairs={{1,0},{3,2},{5,4},{7,6},{9,8},{11,10},{13,12},{15,14},{17,16},{19,... | collective-permute-start | bytes 1572872 | tf_op jit(solution)/shard_map/ppermute | solution.py:94
  50.8 0.0 collective-permute-done.6
  50.8 5.4 %collective-permute-start.11 = (bf16[256,1024]{1,0:T(8,128)(2,1)}, bf16[256,1024]{1,0:T(8,128)(2,1)S(1)}, u32[]{:S(2)}, u32[]{:S(2)}) collective-permute-start(bf16[256,1024]{1,0:T(8,128)(2,1)} %refs_9_.1), channel_id=1, source_target_pairs={{0,1},{2,3},{4,5},{6,7},{8,9},{10,11},{12,13},{14,15},{16,17},{18,... | collective-permute-start | bytes 1572872 | tf_op jit(solution)/shard_map/ppermute | solution.py:94
  56.2 3.4 %collective-permute-done.8 = bf16[256,1024]{1,0:T(8,128)(2,1)S(1)} collective-permute-done((bf16[256,1024]{1,0:T(8,128)(2,1)}, bf16[256,1024]{1,0:T(8,128)(2,1)S(1)}, u32[]{:S(2)}, u32[]{:S(2)}) %collective-permute-start.8) | collective-permute-done | bytes 524320 | tf_op jit(solution)/shard_map/ppermute | solution.py:94
  59.5 3.5 %collective-permute-start.9 = (bf16[256,1024]{1,0:T(8,128)(2,1)}, bf16[256,1024]{1,0:T(8,128)(2,1)}, u32[]{:S(2)}, u32[]{:S(2)}) collective-permute-start(bf16[256,1024]{1,0:T(8,128)(2,1)} %collective-permute-done.7.refs_7_), channel_id=1, source_target_pairs={{0,1},{1,0},{2,3},{3,2},{4,5},{5,4},{6,7},{7,6},{8,9},{9,8},{10,11... | collective-permute-start | bytes 1572872 | tf_op jit(solution)/shard_map/ppermute | solution.py:94
  63.0 0.1 broadcast_select_fusion.4.refs_5_
  63.1 0.0 copy-done
  63.1 0.0 copy-start.1
  63.1 0.0 collective-permute-done.5
  63.1 1.3 %collective-permute-start.10 = (bf16[256,1024]{1,0:T(8,128)(2,1)S(1)}, bf16[256,1024]{1,0:T(8,128)(2,1)S(1)}, u32[]{:S(2)}, u32[]{:S(2)}) collective-permute-start(bf16[256,1024]{1,0:T(8,128)(2,1)S(1)} %broadcast_select_fusion.4.refs_5_), channel_id=1, source_target_pairs={{1,0},{3,2},{5,4},{7,6},{9,8},{11,10},{13,12},{15,14},{17,16},{19,... | collective-permute-start | bytes 1572872 | tf_op jit(solution)/shard_map/ppermute | solution.py:94
  64.4 0.5 compare_convert_fusion.valid_ref
  64.9 2.8 %collective-permute-done.3 = bf16[256,1024]{1,0:T(8,128)(2,1)} collective-permute-done((bf16[256,1024]{1,0:T(8,128)(2,1)}, bf16[256,1024]{1,0:T(8,128)(2,1)}, u32[]{:S(2)}, u32[]{:S(2)}) %collective-permute-start.3) | collective-permute-done | bytes 524320 | tf_op jit(solution)/shard_map/ppermute | solution.py:94
  67.7 4.5 %collective-permute-done.4 = bf16[256,1024]{1,0:T(8,128)(2,1)} collective-permute-done((bf16[256,1024]{1,0:T(8,128)(2,1)S(1)}, bf16[256,1024]{1,0:T(8,128)(2,1)}, u32[]{:S(2)}, u32[]{:S(2)}) %collective-permute-start.4) | collective-permute-done | bytes 524320 | tf_op jit(solution)/shard_map/ppermute | solution.py:94
  72.2 2.3 %broadcast_select_fusion.2 = (bf16[256,1024]{1,0:T(8,128)(2,1)}, bf16[256,1024]{1,0:T(8,128)(2,1)}) fusion(bf16[256,1024]{1,0:T(8,128)(2,1)S(1)} %collective-permute-done.5, bf16[256,1024]{1,0:T(8,128)(2,1)} %collective-permute-done.3, pred[]{:T(512)S(6)} %eq.6, bf16[256,1024]{1,0:T(8,128)(2,1)} %collective-permute-done.4), kind=kLoop, calls=%fused_computation.2 | loop fusion | flops 524288 | bytes 2621441 | tf_op jit(solution)/shard_map/jit(_where)/select_n | solution.py:117
  74.4 0.0 copy-done.1
  74.4 4.5 %collective-permute-done.11 = bf16[256,1024]{1,0:T(8,128)(2,1)S(1)} collective-permute-done((bf16[256,1024]{1,0:T(8,128)(2,1)}, bf16[256,1024]{1,0:T(8,128)(2,1)S(1)}, u32[]{:S(2)}, u32[]{:S(2)}) %collective-permute-start.11) | collective-permute-done | bytes 524320 | tf_op jit(solution)/shard_map/ppermute | solution.py:94
  79.0 8.1 %collective-permute-done.9 = bf16[256,1024]{1,0:T(8,128)(2,1)} collective-permute-done((bf16[256,1024]{1,0:T(8,128)(2,1)}, bf16[256,1024]{1,0:T(8,128)(2,1)}, u32[]{:S(2)}, u32[]{:S(2)}) %collective-permute-start.9) | collective-permute-done | bytes 524320 | tf_op jit(solution)/shard_map/ppermute | solution.py:94
  87.1 4.1 %collective-permute-done.10 = bf16[256,1024]{1,0:T(8,128)(2,1)S(1)} collective-permute-done((bf16[256,1024]{1,0:T(8,128)(2,1)S(1)}, bf16[256,1024]{1,0:T(8,128)(2,1)S(1)}, u32[]{:S(2)}, u32[]{:S(2)}) %collective-permute-start.10) | collective-permute-done | bytes 524320 | tf_op jit(solution)/shard_map/ppermute | solution.py:94
  91.1 2.1 %broadcast_select_fusion = (bf16[256,1024]{1,0:T(8,128)(2,1)}, bf16[256,1024]{1,0:T(8,128)(2,1)}) fusion(bf16[256,1024]{1,0:T(8,128)(2,1)S(1)} %collective-permute-done.11, bf16[256,1024]{1,0:T(8,128)(2,1)} %collective-permute-done.9, pred[]{:T(512)S(6)} %eq.6, bf16[256,1024]{1,0:T(8,128)(2,1)S(1)} %collective-permute-done.10), kind=kLoop, calls=%fused_computation | loop fusion | flops 524288 | bytes 2621441 | tf_op jit(solution)/shard_map/jit(_where)/select_n | solution.py:117
  93.3 20.1 %shard_map.37 = bf16[256,2048]{1,0:T(8,128)(2,1)} custom-call(s32[5]{0:T(128)} %compare_convert_fusion.valid_ref, bf16[256,2048]{1,0:T(8,128)(2,1)} %q_ref.1, bf16[256,1024]{1,0:T(8,128)(2,1)} %copy-done, bf16[256,1024]{1,0:T(8,128)(2,1)} %get-tuple-element.8.refs_1_, bf16[256,1024]{1,0:T(8,128)(2,1)} %collective-permute-done.1.refs_2_, ...), custom_call_target="tpu_custom_call" | custom-call | flops 2684354560 | bytes 7340032 | tf_op jit(solution)/shard_map/pallas_call | solution.py:80
Async XLA Ops:
  0.0 17.4 %collective-permute-start.1 = (bf16[256,1024]{1,0:T(8,128)(2,1)}, bf16[256,1024]{1,0:T(8,128)(2,1)}, u32[]{:S(2)}, u32[]{:S(2)}) collective-permute-start(bf16[256,1024]{1,0:T(8,128)(2,1)} %refs_4_.1), channel_id=1, source_target_pairs={{0,2},{1,3},{2,4},{3,5},{4,6},{5,7},{6,8},{7,9},{8,10},{9,11},{10,... | collective-permute-start | bytes 1572872 | tf_op jit(solution)/shard_map/ppermute | solution.py:94
  3.1 35.1 %collective-permute-start.7 = (bf16[256,1024]{1,0:T(8,128)(2,1)}, bf16[256,1024]{1,0:T(8,128)(2,1)}, u32[]{:S(2)}, u32[]{:S(2)}) collective-permute-start(bf16[256,1024]{1,0:T(8,128)(2,1)} %refs_9_.1), channel_id=1, source_target_pairs={{0,2},{1,3},{2,4},{3,5},{4,6},{5,7},{6,8},{7,9},{8,10},{9,11},{10,... | collective-permute-start | bytes 1572872 | tf_op jit(solution)/shard_map/ppermute | solution.py:94
  5.0 38.9 %collective-permute-start = (bf16[256,1024]{1,0:T(8,128)(2,1)}, bf16[256,1024]{1,0:T(8,128)(2,1)S(1)}, u32[]{:S(2)}, u32[]{:S(2)}) collective-permute-start(bf16[256,1024]{1,0:T(8,128)(2,1)} %refs_4_.1), channel_id=1, source_target_pairs={{12,16},{13,17},{28,32},{29,33},{44,48},{45,49},{60,64},{61,65},{7... | collective-permute-start | bytes 1572872 | tf_op jit(solution)/shard_map/ppermute | solution.py:94
  17.4 32.0 %collective-permute-start.2 = (bf16[256,1024]{1,0:T(8,128)(2,1)}, bf16[256,1024]{1,0:T(8,128)(2,1)S(1)}, u32[]{:S(2)}, u32[]{:S(2)}) collective-permute-start(bf16[256,1024]{1,0:T(8,128)(2,1)} %collective-permute-done.1.refs_2_), channel_id=1, source_target_pairs={{0,2},{1,3},{2,4},{3,5},{4,6},{5,7},{6,8},{7,9},{8,10},{9,11},{10,... | collective-permute-start | bytes 1572872 | tf_op jit(solution)/shard_map/ppermute | solution.py:94
  22.3 28.5 %collective-permute-start.6 = (bf16[256,1024]{1,0:T(8,128)(2,1)}, bf16[256,1024]{1,0:T(8,128)(2,1)S(1)}, u32[]{:S(2)}, u32[]{:S(2)}) collective-permute-start(bf16[256,1024]{1,0:T(8,128)(2,1)} %refs_9_.1), channel_id=1, source_target_pairs={{12,16},{13,17},{28,32},{29,33},{44,48},{45,49},{60,64},{61,65},{7... | collective-permute-start | bytes 1572872 | tf_op jit(solution)/shard_map/ppermute | solution.py:94
  38.2 21.3 %collective-permute-start.8 = (bf16[256,1024]{1,0:T(8,128)(2,1)}, bf16[256,1024]{1,0:T(8,128)(2,1)S(1)}, u32[]{:S(2)}, u32[]{:S(2)}) collective-permute-start(bf16[256,1024]{1,0:T(8,128)(2,1)} %collective-permute-done.7.refs_7_), channel_id=1, source_target_pairs={{0,2},{1,3},{2,4},{3,5},{4,6},{5,7},{6,8},{7,9},{8,10},{9,11},{10,... | collective-permute-start | bytes 1572872 | tf_op jit(solution)/shard_map/ppermute | solution.py:94
  42.6 20.5 %collective-permute-start.5 = (bf16[256,1024]{1,0:T(8,128)(2,1)}, bf16[256,1024]{1,0:T(8,128)(2,1)S(1)}, u32[]{:S(2)}, u32[]{:S(2)}) collective-permute-start(bf16[256,1024]{1,0:T(8,128)(2,1)} %refs_4_.1), channel_id=1, source_target_pairs={{0,1},{2,3},{4,5},{6,7},{8,9},{10,11},{12,13},{14,15},{16,17},{18,... | collective-permute-start | bytes 1572872 | tf_op jit(solution)/shard_map/ppermute | solution.py:94
  43.9 23.8 %collective-permute-start.3 = (bf16[256,1024]{1,0:T(8,128)(2,1)}, bf16[256,1024]{1,0:T(8,128)(2,1)}, u32[]{:S(2)}, u32[]{:S(2)}) collective-permute-start(bf16[256,1024]{1,0:T(8,128)(2,1)} %collective-permute-done.1.refs_2_), channel_id=1, source_target_pairs={{0,1},{1,0},{2,3},{3,2},{4,5},{5,4},{6,7},{7,6},{8,9},{9,8},{10,11... | collective-permute-start | bytes 1572872 | tf_op jit(solution)/shard_map/ppermute | solution.py:94
  49.5 13.6 %copy-start = (bf16[256,1024]{1,0:T(8,128)(2,1)}, bf16[256,1024]{1,0:T(8,128)(2,1)S(1)}, u32[]{:S(2)}) copy-start(bf16[256,1024]{1,0:T(8,128)(2,1)S(1)} %broadcast_select_fusion.5.refs_0_) | copy-start | bytes 1572868
  49.5 22.7 %collective-permute-start.4 = (bf16[256,1024]{1,0:T(8,128)(2,1)S(1)}, bf16[256,1024]{1,0:T(8,128)(2,1)}, u32[]{:S(2)}, u32[]{:S(2)}) collective-permute-start(bf16[256,1024]{1,0:T(8,128)(2,1)S(1)} %broadcast_select_fusion.5.refs_0_), channel_id=1, source_target_pairs={{1,0},{3,2},{5,4},{7,6},{9,8},{11,10},{13,12},{15,14},{17,16},{19,... | collective-permute-start | bytes 1572872 | tf_op jit(solution)/shard_map/ppermute | solution.py:94
  50.8 28.2 %collective-permute-start.11 = (bf16[256,1024]{1,0:T(8,128)(2,1)}, bf16[256,1024]{1,0:T(8,128)(2,1)S(1)}, u32[]{:S(2)}, u32[]{:S(2)}) collective-permute-start(bf16[256,1024]{1,0:T(8,128)(2,1)} %refs_9_.1), channel_id=1, source_target_pairs={{0,1},{2,3},{4,5},{6,7},{8,9},{10,11},{12,13},{14,15},{16,17},{18,... | collective-permute-start | bytes 1572872 | tf_op jit(solution)/shard_map/ppermute | solution.py:94
  59.5 27.5 %collective-permute-start.9 = (bf16[256,1024]{1,0:T(8,128)(2,1)}, bf16[256,1024]{1,0:T(8,128)(2,1)}, u32[]{:S(2)}, u32[]{:S(2)}) collective-permute-start(bf16[256,1024]{1,0:T(8,128)(2,1)} %collective-permute-done.7.refs_7_), channel_id=1, source_target_pairs={{0,1},{1,0},{2,3},{3,2},{4,5},{5,4},{6,7},{7,6},{8,9},{9,8},{10,11... | collective-permute-start | bytes 1572872 | tf_op jit(solution)/shard_map/ppermute | solution.py:94
  63.1 11.4 %copy-start.1 = (bf16[256,1024]{1,0:T(8,128)(2,1)}, bf16[256,1024]{1,0:T(8,128)(2,1)S(1)}, u32[]{:S(2)}) copy-start(bf16[256,1024]{1,0:T(8,128)(2,1)S(1)} %broadcast_select_fusion.4.refs_5_) | copy-start | bytes 1572868
  63.1 28.0 %collective-permute-start.10 = (bf16[256,1024]{1,0:T(8,128)(2,1)S(1)}, bf16[256,1024]{1,0:T(8,128)(2,1)S(1)}, u32[]{:S(2)}, u32[]{:S(2)}) collective-permute-start(bf16[256,1024]{1,0:T(8,128)(2,1)S(1)} %broadcast_select_fusion.4.refs_5_), channel_id=1, source_target_pairs={{1,0},{3,2},{5,4},{7,6},{9,8},{11,10},{13,12},{15,14},{17,16},{19,... | collective-permute-start | bytes 1572872 | tf_op jit(solution)/shard_map/ppermute | solution.py:94

commit v14 on v9

--- a/solution.py
+++ b/solution.py
@@ -22,38 +22,40 @@
     nblk = (len(refs) - 1) // 2
     k_refs, v_refs, o_ref = refs[:nblk], refs[nblk:2 * nblk], refs[-1]
     tok = q_ref.shape[0]
-    row = lax.broadcasted_iota(jnp.int32, (tok, tok), 0)
-    col = lax.broadcasted_iota(jnp.int32, (tok, tok), 1)
     group = HEADS // KV_HEADS
+    q = jnp.concatenate(
+        [q_ref[:, a * HEAD_DIM:(a + 1) * HEAD_DIM] for a in range(group)], axis=0
+    )
+    row = lax.broadcasted_iota(jnp.int32, (group * tok, tok), 0) % tok
+    col = lax.broadcasted_iota(jnp.int32, (group * tok, tok), 1)
+    scores = []
+    for j in range(nblk):
+        s = lax.dot_general(
+            q, k_refs[j][...], (((1,), (1,)), ((), ())),
+            preferred_element_type=jnp.float32,
+        ) * HEAD_DIM ** (-0.5)
+        if j == 0:
+            s = jnp.where((col > row) & (valid_ref[0] > 0), s, NEG)
+        elif j == nblk - 1:
+            s = jnp.where(col <= row, s, NEG)
+        else:
+            s = jnp.where(valid_ref[j] > 0, s, NEG)
+        scores.append(s)
+    largest = scores[0].max(axis=1, keepdims=True)
+    for s in scores[1:]:
+        largest = jnp.maximum(largest, s.max(axis=1, keepdims=True))
+    expos = [jnp.exp(s - largest) for s in scores]
+    total = expos[0].sum(axis=1, keepdims=True)
+    for e in expos[1:]:
+        total = total + e.sum(axis=1, keepdims=True)
+    inv = 1.0 / total
+    out = None
+    for j in range(nblk):
+        w = (expos[j] * inv).astype(jnp.bfloat16)
+        part = jnp.dot(w, v_refs[j][...], preferred_element_type=jnp.float32)
+        out = part if out is None else out + part
     for a in range(group):
-        qa = q_ref[:, a * HEAD_DIM:(a + 1) * HEAD_DIM]
-        scores = []
-        for j in range(nblk):
-            s = lax.dot_general(
-                qa, k_refs[j][...], (((1,), (1,)), ((), ())),
-                preferred_element_type=jnp.float32,
-            ) * HEAD_DIM ** (-0.5)
-            if j == 0:
-                s = jnp.where((col > row) & (valid_ref[0] > 0), s, NEG)
-            elif j == nblk - 1:
-                s = jnp.where(col <= row, s, NEG)
-            else:
-                s = jnp.where(valid_ref[j] > 0, s, NEG)
-            scores.append(s)
-        largest = scores[0].max(axis=1, keepdims=True)
-        for s in scores[1:]:
-            largest = jnp.maximum(largest, s.max(axis=1, keepdims=True))
-        expos = [jnp.exp(s - largest) for s in scores]
-        total = expos[0].sum(axis=1, keepdims=True)
-        for e in expos[1:]:
-            total = total + e.sum(axis=1, keepdims=True)
-        inv = 1.0 / total
-        out = None
-        for j in range(nblk):
-            w = (expos[j] * inv).astype(jnp.bfloat16)
-            part = jnp.dot(w, v_refs[j][...], preferred_element_type=jnp.float32)
-            out = part if out is None else out + part
-        o_ref[:, a * HEAD_DIM:(a + 1) * HEAD_DIM] = out.astype(o_ref.dtype)
+        o_ref[:, a * HEAD_DIM:(a + 1) * HEAD_DIM] = out[a * tok:(a + 1) * tok].astype(o_ref.dtype)
 
 
 def attend(valid, queries, k_blocks, v_blocks):

time: 109 us -> 111 us (1.018)
  the two profiles are of different devices: /device:TPU:484 before, /device:TPU:180 now
where the time goes in v14:
time: 111 us
  waiting for transfers between devices  54.1 us (49%)
  starting transfers between devices  33.9 us (31%)
  Pallas kernels  17.7 us (16%)
  other arithmetic  5.04 us (5%)
    ppermute x12, waiting for transfers between devices, shifted(): return lax.ppermute(x, axis, pairs)  54.1 us
    ppermute x12, starting transfers between devices, shifted(): return lax.ppermute(x, axis, pairs)  33.9 us
    pallas_call x1, Pallas kernels, attend(): pl.pallas_call(attend_kernel, grid=(KV_HEADS,), in_specs=[pl.BlockSpec(me...  17.7 us
    select_n x2, other arithmetic, body(): b1 = [jnp.where(odd, a, b) for a, b in zip(y1, y2)]  4.4 us
  transfers between devices with their start and end apart: 12, of which 9 were waited for; matrix products, arithmetic and copies ran while one was open for 3% of the time, Pallas kernels for 0%

profile of v14, /device:TPU:180, one launch (start us, length us, event | category | flops | bytes accessed | tf_op | source)
XLA Modules:
  0.0 110.9 jit_solution(14868531600445911686)
XLA Ops:
  0.0 3.1 %collective-permute-start.1 = (bf16[256,1024]{1,0:T(8,128)(2,1)}, bf16[256,1024]{1,0:T(8,128)(2,1)}, u32[]{:S(2)}, u32[]{:S(2)}) collective-permute-start(bf16[256,1024]{1,0:T(8,128)(2,1)} %refs_4_.1), channel_id=1, source_target_pairs={{0,2},{1,3},{2,4},{3,5},{4,6},{5,7},{6,8},{7,9},{8,10},{9,11},{10,... | collective-permute-start | bytes 1572872 | tf_op jit(solution)/shard_map/ppermute | solution.py:83
  3.1 1.9 %collective-permute-start.7 = (bf16[256,1024]{1,0:T(8,128)(2,1)}, bf16[256,1024]{1,0:T(8,128)(2,1)}, u32[]{:S(2)}, u32[]{:S(2)}) collective-permute-start(bf16[256,1024]{1,0:T(8,128)(2,1)} %refs_9_.1), channel_id=1, source_target_pairs={{0,2},{1,3},{2,4},{3,5},{4,6},{5,7},{6,8},{7,9},{8,10},{9,11},{10,... | collective-permute-start | bytes 1572872 | tf_op jit(solution)/shard_map/ppermute | solution.py:83
  5.0 0.7 collective-permute-start
  5.7 15.2 %collective-permute-done.1.refs_2_ = bf16[256,1024]{1,0:T(8,128)(2,1)} collective-permute-done((bf16[256,1024]{1,0:T(8,128)(2,1)}, bf16[256,1024]{1,0:T(8,128)(2,1)}, u32[]{:S(2)}, u32[]{:S(2)}) %collective-permute-start.1) | collective-permute-done | bytes 524320 | tf_op jit(solution)/shard_map/ppermute | solution.py:83
  21.0 8.1 %collective-permute-start.2 = (bf16[256,1024]{1,0:T(8,128)(2,1)}, bf16[256,1024]{1,0:T(8,128)(2,1)S(1)}, u32[]{:S(2)}, u32[]{:S(2)}) collective-permute-start(bf16[256,1024]{1,0:T(8,128)(2,1)} %collective-permute-done.1.refs_2_), channel_id=1, source_target_pairs={{0,2},{1,3},{2,4},{3,5},{4,6},{5,7},{6,8},{7,9},{8,10},{9,11},{10,... | collective-permute-start | bytes 1572872 | tf_op jit(solution)/shard_map/ppermute | solution.py:83
  29.0 0.7 collective-permute-start.6
  29.7 8.5 %collective-permute-done.7.refs_7_ = bf16[256,1024]{1,0:T(8,128)(2,1)} collective-permute-done((bf16[256,1024]{1,0:T(8,128)(2,1)}, bf16[256,1024]{1,0:T(8,128)(2,1)}, u32[]{:S(2)}, u32[]{:S(2)}) %collective-permute-start.7) | collective-permute-done | bytes 524320 | tf_op jit(solution)/shard_map/ppermute | solution.py:83
  38.2 4.4 %collective-permute-start.8 = (bf16[256,1024]{1,0:T(8,128)(2,1)}, bf16[256,1024]{1,0:T(8,128)(2,1)S(1)}, u32[]{:S(2)}, u32[]{:S(2)}) collective-permute-start(bf16[256,1024]{1,0:T(8,128)(2,1)} %collective-permute-done.7.refs_7_), channel_id=1, source_target_pairs={{0,2},{1,3},{2,4},{3,5},{4,6},{5,7},{6,8},{7,9},{8,10},{9,11},{10,... | collective-permute-start | bytes 1572872 | tf_op jit(solution)/shard_map/ppermute | solution.py:83
  42.6 2.6 %collective-permute-start.5 = (bf16[256,1024]{1,0:T(8,128)(2,1)}, bf16[256,1024]{1,0:T(8,128)(2,1)S(1)}, u32[]{:S(2)}, u32[]{:S(2)}) collective-permute-start(bf16[256,1024]{1,0:T(8,128)(2,1)} %refs_4_.1), channel_id=1, source_target_pairs={{0,1},{2,3},{4,5},{6,7},{8,9},{10,11},{12,13},{14,15},{16,17},{18,... | collective-permute-start | bytes 1572872 | tf_op jit(solution)/shard_map/ppermute | solution.py:83
  45.2 0.0 collective-permute-done
  45.2 1.9 %collective-permute-start.3 = (bf16[256,1024]{1,0:T(8,128)(2,1)}, bf16[256,1024]{1,0:T(8,128)(2,1)}, u32[]{:S(2)}, u32[]{:S(2)}) collective-permute-start(bf16[256,1024]{1,0:T(8,128)(2,1)} %collective-permute-done.1.refs_2_), channel_id=1, source_target_pairs={{0,1},{1,0},{2,3},{3,2},{4,5},{5,4},{6,7},{7,6},{8,9},{9,8},{10,11... | collective-permute-start | bytes 1572872 | tf_op jit(solution)/shard_map/ppermute | solution.py:83
  47.1 2.3 %collective-permute-done.2 = bf16[256,1024]{1,0:T(8,128)(2,1)S(1)} collective-permute-done((bf16[256,1024]{1,0:T(8,128)(2,1)}, bf16[256,1024]{1,0:T(8,128)(2,1)S(1)}, u32[]{:S(2)}, u32[]{:S(2)}) %collective-permute-start.2) | collective-permute-done | bytes 524320 | tf_op jit(solution)/shard_map/ppermute | solution.py:83
  49.4 0.1 broadcast_select_fusion.5.refs_0_
  49.5 0.0 copy-start
  49.5 1.3 %collective-permute-start.4 = (bf16[256,1024]{1,0:T(8,128)(2,1)S(1)}, bf16[256,1024]{1,0:T(8,128)(2,1)}, u32[]{:S(2)}, u32[]{:S(2)}) collective-permute-start(bf16[256,1024]{1,0:T(8,128)(2,1)S(1)} %broadcast_select_fusion.5.refs_0_), channel_id=1, source_target_pairs={{1,0},{3,2},{5,4},{7,6},{9,8},{11,10},{13,12},{15,14},{17,16},{19,... | collective-permute-start | bytes 1572872 | tf_op jit(solution)/shard_map/ppermute | solution.py:83
  50.8 0.0 collective-permute-done.6
  50.8 5.4 %collective-permute-start.11 = (bf16[256,1024]{1,0:T(8,128)(2,1)}, bf16[256,1024]{1,0:T(8,128)(2,1)S(1)}, u32[]{:S(2)}, u32[]{:S(2)}) collective-permute-start(bf16[256,1024]{1,0:T(8,128)(2,1)} %refs_9_.1), channel_id=1, source_target_pairs={{0,1},{2,3},{4,5},{6,7},{8,9},{10,11},{12,13},{14,15},{16,17},{18,... | collective-permute-start | bytes 1572872 | tf_op jit(solution)/shard_map/ppermute | solution.py:83
  56.2 3.4 %collective-permute-done.8 = bf16[256,1024]{1,0:T(8,128)(2,1)S(1)} collective-permute-done((bf16[256,1024]{1,0:T(8,128)(2,1)}, bf16[256,1024]{1,0:T(8,128)(2,1)S(1)}, u32[]{:S(2)}, u32[]{:S(2)}) %collective-permute-start.8) | collective-permute-done | bytes 524320 | tf_op jit(solution)/shard_map/ppermute | solution.py:83
  59.5 2.6 %collective-permute-start.9 = (bf16[256,1024]{1,0:T(8,128)(2,1)}, bf16[256,1024]{1,0:T(8,128)(2,1)}, u32[]{:S(2)}, u32[]{:S(2)}) collective-permute-start(bf16[256,1024]{1,0:T(8,128)(2,1)} %collective-permute-done.7.refs_7_), channel_id=1, source_target_pairs={{0,1},{1,0},{2,3},{3,2},{4,5},{5,4},{6,7},{7,6},{8,9},{9,8},{10,11... | collective-permute-start | bytes 1572872 | tf_op jit(solution)/shard_map/ppermute | solution.py:83
  62.1 0.1 broadcast_select_fusion.4.refs_5_
  62.2 0.0 copy-done
  62.2 0.0 copy-start.1
  62.2 0.0 collective-permute-done.5
  62.2 1.3 %collective-permute-start.10 = (bf16[256,1024]{1,0:T(8,128)(2,1)S(1)}, bf16[256,1024]{1,0:T(8,128)(2,1)S(1)}, u32[]{:S(2)}, u32[]{:S(2)}) collective-permute-start(bf16[256,1024]{1,0:T(8,128)(2,1)S(1)} %broadcast_select_fusion.4.refs_5_), channel_id=1, source_target_pairs={{1,0},{3,2},{5,4},{7,6},{9,8},{11,10},{13,12},{15,14},{17,16},{19,... | collective-permute-start | bytes 1572872 | tf_op jit(solution)/shard_map/ppermute | solution.py:83
  63.5 0.5 compare_convert_fusion.valid_ref
  64.0 5.0 %collective-permute-done.3 = bf16[256,1024]{1,0:T(8,128)(2,1)} collective-permute-done((bf16[256,1024]{1,0:T(8,128)(2,1)}, bf16[256,1024]{1,0:T(8,128)(2,1)}, u32[]{:S(2)}, u32[]{:S(2)}) %collective-permute-start.3) | collective-permute-done | bytes 524320 | tf_op jit(solution)/shard_map/ppermute | solution.py:83
  69.0 4.5 %collective-permute-done.4 = bf16[256,1024]{1,0:T(8,128)(2,1)} collective-permute-done((bf16[256,1024]{1,0:T(8,128)(2,1)S(1)}, bf16[256,1024]{1,0:T(8,128)(2,1)}, u32[]{:S(2)}, u32[]{:S(2)}) %collective-permute-start.4) | collective-permute-done | bytes 524320 | tf_op jit(solution)/shard_map/ppermute | solution.py:83
  73.5 2.3 %broadcast_select_fusion.2 = (bf16[256,1024]{1,0:T(8,128)(2,1)}, bf16[256,1024]{1,0:T(8,128)(2,1)}) fusion(bf16[256,1024]{1,0:T(8,128)(2,1)S(1)} %collective-permute-done.5, bf16[256,1024]{1,0:T(8,128)(2,1)} %collective-permute-done.3, pred[]{:T(512)S(6)} %eq.6, bf16[256,1024]{1,0:T(8,128)(2,1)} %collective-permute-done.4), kind=kLoop, calls=%fused_computation.2 | loop fusion | flops 524288 | bytes 2621441 | tf_op jit(solution)/shard_map/jit(_where)/select_n | solution.py:106
  75.7 0.0 copy-done.1
  75.7 4.5 %collective-permute-done.11 = bf16[256,1024]{1,0:T(8,128)(2,1)S(1)} collective-permute-done((bf16[256,1024]{1,0:T(8,128)(2,1)}, bf16[256,1024]{1,0:T(8,128)(2,1)S(1)}, u32[]{:S(2)}, u32[]{:S(2)}) %collective-permute-start.11) | collective-permute-done | bytes 524320 | tf_op jit(solution)/shard_map/ppermute | solution.py:83
  80.2 6.8 %collective-permute-done.9 = bf16[256,1024]{1,0:T(8,128)(2,1)} collective-permute-done((bf16[256,1024]{1,0:T(8,128)(2,1)}, bf16[256,1024]{1,0:T(8,128)(2,1)}, u32[]{:S(2)}, u32[]{:S(2)}) %collective-permute-start.9) | collective-permute-done | bytes 524320 | tf_op jit(solution)/shard_map/ppermute | solution.py:83
  87.1 4.1 %collective-permute-done.10 = bf16[256,1024]{1,0:T(8,128)(2,1)S(1)} collective-permute-done((bf16[256,1024]{1,0:T(8,128)(2,1)S(1)}, bf16[256,1024]{1,0:T(8,128)(2,1)S(1)}, u32[]{:S(2)}, u32[]{:S(2)}) %collective-permute-start.10) | collective-permute-done | bytes 524320 | tf_op jit(solution)/shard_map/ppermute | solution.py:83
  91.1 2.1 %broadcast_select_fusion = (bf16[256,1024]{1,0:T(8,128)(2,1)}, bf16[256,1024]{1,0:T(8,128)(2,1)}) fusion(bf16[256,1024]{1,0:T(8,128)(2,1)S(1)} %collective-permute-done.11, bf16[256,1024]{1,0:T(8,128)(2,1)} %collective-permute-done.9, pred[]{:T(512)S(6)} %eq.6, bf16[256,1024]{1,0:T(8,128)(2,1)S(1)} %collective-permute-done.10), kind=kLoop, calls=%fused_computation | loop fusion | flops 524288 | bytes 2621441 | tf_op jit(solution)/shard_map/jit(_where)/select_n | solution.py:106
  93.3 17.7 %shard_map.37 = bf16[256,2048]{1,0:T(8,128)(2,1)} custom-call(s32[5]{0:T(128)} %compare_convert_fusion.valid_ref, bf16[256,2048]{1,0:T(8,128)(2,1)} %q_ref.1, bf16[256,1024]{1,0:T(8,128)(2,1)} %copy-done, bf16[256,1024]{1,0:T(8,128)(2,1)} %get-tuple-element.8.refs_1_, bf16[256,1024]{1,0:T(8,128)(2,1)} %collective-permute-done.1.refs_2_, ...), custom_call_target="tpu_custom_call" | custom-call | flops 2684354560 | bytes 7340032 | tf_op jit(solution)/shard_map/pallas_call | solution.py:69
Async XLA Ops:
  0.0 21.0 %collective-permute-start.1 = (bf16[256,1024]{1,0:T(8,128)(2,1)}, bf16[256,1024]{1,0:T(8,128)(2,1)}, u32[]{:S(2)}, u32[]{:S(2)}) collective-permute-start(bf16[256,1024]{1,0:T(8,128)(2,1)} %refs_4_.1), channel_id=1, source_target_pairs={{0,2},{1,3},{2,4},{3,5},{4,6},{5,7},{6,8},{7,9},{8,10},{9,11},{10,... | collective-permute-start | bytes 1572872 | tf_op jit(solution)/shard_map/ppermute | solution.py:83
  3.1 35.1 %collective-permute-start.7 = (bf16[256,1024]{1,0:T(8,128)(2,1)}, bf16[256,1024]{1,0:T(8,128)(2,1)}, u32[]{:S(2)}, u32[]{:S(2)}) collective-permute-start(bf16[256,1024]{1,0:T(8,128)(2,1)} %refs_9_.1), channel_id=1, source_target_pairs={{0,2},{1,3},{2,4},{3,5},{4,6},{5,7},{6,8},{7,9},{8,10},{9,11},{10,... | collective-permute-start | bytes 1572872 | tf_op jit(solution)/shard_map/ppermute | solution.py:83
  5.0 40.2 %collective-permute-start = (bf16[256,1024]{1,0:T(8,128)(2,1)}, bf16[256,1024]{1,0:T(8,128)(2,1)S(1)}, u32[]{:S(2)}, u32[]{:S(2)}) collective-permute-start(bf16[256,1024]{1,0:T(8,128)(2,1)} %refs_4_.1), channel_id=1, source_target_pairs={{12,16},{13,17},{28,32},{29,33},{44,48},{45,49},{60,64},{61,65},{7... | collective-permute-start | bytes 1572872 | tf_op jit(solution)/shard_map/ppermute | solution.py:83
  21.0 28.5 %collective-permute-start.2 = (bf16[256,1024]{1,0:T(8,128)(2,1)}, bf16[256,1024]{1,0:T(8,128)(2,1)S(1)}, u32[]{:S(2)}, u32[]{:S(2)}) collective-permute-start(bf16[256,1024]{1,0:T(8,128)(2,1)} %collective-permute-done.1.refs_2_), channel_id=1, source_target_pairs={{0,2},{1,3},{2,4},{3,5},{4,6},{5,7},{6,8},{7,9},{8,10},{9,11},{10,... | collective-permute-start | bytes 1572872 | tf_op jit(solution)/shard_map/ppermute | solution.py:83
  29.0 21.8 %collective-permute-start.6 = (bf16[256,1024]{1,0:T(8,128)(2,1)}, bf16[256,1024]{1,0:T(8,128)(2,1)S(1)}, u32[]{:S(2)}, u32[]{:S(2)}) collective-permute-start(bf16[256,1024]{1,0:T(8,128)(2,1)} %refs_9_.1), channel_id=1, source_target_pairs={{12,16},{13,17},{28,32},{29,33},{44,48},{45,49},{60,64},{61,65},{7... | collective-permute-start | bytes 1572872 | tf_op jit(solution)/shard_map/ppermute | solution.py:83
  38.2 21.3 %collective-permute-start.8 = (bf16[256,1024]{1,0:T(8,128)(2,1)}, bf16[256,1024]{1,0:T(8,128)(2,1)S(1)}, u32[]{:S(2)}, u32[]{:S(2)}) collective-permute-start(bf16[256,1024]{1,0:T(8,128)(2,1)} %collective-permute-done.7.refs_7_), channel_id=1, source_target_pairs={{0,2},{1,3},{2,4},{3,5},{4,6},{5,7},{6,8},{7,9},{8,10},{9,11},{10,... | collective-permute-start | bytes 1572872 | tf_op jit(solution)/shard_map/ppermute | solution.py:83
  42.6 19.6 %collective-permute-start.5 = (bf16[256,1024]{1,0:T(8,128)(2,1)}, bf16[256,1024]{1,0:T(8,128)(2,1)S(1)}, u32[]{:S(2)}, u32[]{:S(2)}) collective-permute-start(bf16[256,1024]{1,0:T(8,128)(2,1)} %refs_4_.1), channel_id=1, source_target_pairs={{0,1},{2,3},{4,5},{6,7},{8,9},{10,11},{12,13},{14,15},{16,17},{18,... | collective-permute-start | bytes 1572872 | tf_op jit(solution)/shard_map/ppermute | solution.py:83
  45.2 23.8 %collective-permute-start.3 = (bf16[256,1024]{1,0:T(8,128)(2,1)}, bf16[256,1024]{1,0:T(8,128)(2,1)}, u32[]{:S(2)}, u32[]{:S(2)}) collective-permute-start(bf16[256,1024]{1,0:T(8,128)(2,1)} %collective-permute-done.1.refs_2_), channel_id=1, source_target_pairs={{0,1},{1,0},{2,3},{3,2},{4,5},{5,4},{6,7},{7,6},{8,9},{9,8},{10,11... | collective-permute-start | bytes 1572872 | tf_op jit(solution)/shard_map/ppermute | solution.py:83
  49.5 12.7 %copy-start = (bf16[256,1024]{1,0:T(8,128)(2,1)}, bf16[256,1024]{1,0:T(8,128)(2,1)S(1)}, u32[]{:S(2)}) copy-start(bf16[256,1024]{1,0:T(8,128)(2,1)S(1)} %broadcast_select_fusion.5.refs_0_) | copy-start | bytes 1572868
  49.5 24.0 %collective-permute-start.4 = (bf16[256,1024]{1,0:T(8,128)(2,1)S(1)}, bf16[256,1024]{1,0:T(8,128)(2,1)}, u32[]{:S(2)}, u32[]{:S(2)}) collective-permute-start(bf16[256,1024]{1,0:T(8,128)(2,1)S(1)} %broadcast_select_fusion.5.refs_0_), channel_id=1, source_target_pairs={{1,0},{3,2},{5,4},{7,6},{9,8},{11,10},{13,12},{15,14},{17,16},{19,... | collective-permute-start | bytes 1572872 | tf_op jit(solution)/shard_map/ppermute | solution.py:83
  50.8 29.4 %collective-permute-start.11 = (bf16[256,1024]{1,0:T(8,128)(2,1)}, bf16[256,1024]{1,0:T(8,128)(2,1)S(1)}, u32[]{:S(2)}, u32[]{:S(2)}) collective-permute-start(bf16[256,1024]{1,0:T(8,128)(2,1)} %refs_9_.1), channel_id=1, source_target_pairs={{0,1},{2,3},{4,5},{6,7},{8,9},{10,11},{12,13},{14,15},{16,17},{18,... | collective-permute-start | bytes 1572872 | tf_op jit(solution)/shard_map/ppermute | solution.py:83
  59.5 27.5 %collective-permute-start.9 = (bf16[256,1024]{1,0:T(8,128)(2,1)}, bf16[256,1024]{1,0:T(8,128)(2,1)}, u32[]{:S(2)}, u32[]{:S(2)}) collective-permute-start(bf16[256,1024]{1,0:T(8,128)(2,1)} %collective-permute-done.7.refs_7_), channel_id=1, source_target_pairs={{0,1},{1,0},{2,3},{3,2},{4,5},{5,4},{6,7},{7,6},{8,9},{9,8},{10,11... | collective-permute-start | bytes 1572872 | tf_op jit(solution)/shard_map/ppermute | solution.py:83
  62.2 13.6 %copy-start.1 = (bf16[256,1024]{1,0:T(8,128)(2,1)}, bf16[256,1024]{1,0:T(8,128)(2,1)S(1)}, u32[]{:S(2)}) copy-start(bf16[256,1024]{1,0:T(8,128)(2,1)S(1)} %broadcast_select_fusion.4.refs_5_) | copy-start | bytes 1572868
  62.2 28.9 %collective-permute-start.10 = (bf16[256,1024]{1,0:T(8,128)(2,1)S(1)}, bf16[256,1024]{1,0:T(8,128)(2,1)S(1)}, u32[]{:S(2)}, u32[]{:S(2)}) collective-permute-start(bf16[256,1024]{1,0:T(8,128)(2,1)S(1)} %broadcast_select_fusion.4.refs_5_), channel_id=1, source_target_pairs={{1,0},{3,2},{5,4},{7,6},{9,8},{11,10},{13,12},{15,14},{17,16},{19,... | collective-permute-start | bytes 1572872 | tf_op jit(solution)/shard_map/ppermute | solution.py:83

commit v15 on v9

--- a/solution.py
+++ b/solution.py
@@ -98,7 +98,8 @@
     x2 = shifted(x1, axis, [(i, i + 2) for i in range(n) if i + 2 < n and not crossing(i + 2)])
     first_two = (block_index % plane) < 2
     b4 = [jnp.where(first_two, a, b) for a, b in zip(far, x2)]
-    y2 = shifted(x1, axis, [(i, i ^ 1) for i in range(n)])
+    x1_fenced = tuple(lax.optimization_barrier((a, b))[0] for a, b in zip(x1, y1))
+    y2 = shifted(x1_fenced, axis, [(i, i ^ 1) for i in range(n)])
     y3 = shifted(b4, axis, [(i, i - 1) for i in range(1, n, 2)])
     odd = (block_index % 2) == 1
     b1 = [jnp.where(odd, a, b) for a, b in zip(y1, y2)]

time: 109 us -> 110 us (level)
  the two profiles are of different devices: /device:TPU:484 before, /device:TPU:389 now
where the time goes in v15:
time: 110 us; the launch traced here: 109 us
  starting transfers between devices  56.8 us (52%)
  waiting for transfers between devices  32.8 us (30%)
  Pallas kernels  15.5 us (14%)
  other arithmetic  3.98 us (4%)
    ppermute x12, starting transfers between devices, shifted(): return lax.ppermute(x, axis, pairs)  56.8 us
    ppermute x12, waiting for transfers between devices, shifted(): return lax.ppermute(x, axis, pairs)  32.8 us
    pallas_call x1, Pallas kernels, attend(): pl.pallas_call(attend_kernel, grid=(KV_HEADS,), in_specs=[pl.BlockSpec(me...  15.5 us
    select_n x2, other arithmetic, body(): b1 = [jnp.where(odd, a, b) for a, b in zip(y1, y2)]  3.35 us
  transfers between devices with their start and end apart: 12, of which 6 were waited for; matrix products, arithmetic and copies ran while one was open for 3% of the time, Pallas kernels for 0%

profile of v15, /device:TPU:389, one launch (start us, length us, event | category | flops | bytes accessed | tf_op | source)
XLA Modules:
  0.0 109.4 jit_solution(12069408586238488122)
XLA Ops:
  0.0 2.8 %collective-permute-start.1 = (bf16[256,1024]{1,0:T(8,128)(2,1)}, bf16[256,1024]{1,0:T(8,128)(2,1)}, u32[]{:S(2)}, u32[]{:S(2)}) collective-permute-start(bf16[256,1024]{1,0:T(8,128)(2,1)} %refs_4_.1), channel_id=1, source_target_pairs={{0,2},{1,3},{2,4},{3,5},{4,6},{5,7},{6,8},{7,9},{8,10},{9,11},{10,... | collective-permute-start | bytes 1572872 | tf_op jit(solution)/shard_map/ppermute | solution.py:81
  2.8 3.2 %collective-permute-start.3 = (bf16[256,1024]{1,0:T(8,128)(2,1)}, bf16[256,1024]{1,0:T(8,128)(2,1)S(1)}, u32[]{:S(2)}, u32[]{:S(2)}) collective-permute-start(bf16[256,1024]{1,0:T(8,128)(2,1)} %refs_4_.1), channel_id=1, source_target_pairs={{0,1},{2,3},{4,5},{6,7},{8,9},{10,11},{12,13},{14,15},{16,17},{18,... | collective-permute-start | bytes 1572872 | tf_op jit(solution)/shard_map/ppermute | solution.py:81
  6.1 4.7 %collective-permute-start.7 = (bf16[256,1024]{1,0:T(8,128)(2,1)}, bf16[256,1024]{1,0:T(8,128)(2,1)}, u32[]{:S(2)}, u32[]{:S(2)}) collective-permute-start(bf16[256,1024]{1,0:T(8,128)(2,1)} %refs_9_.1), channel_id=1, source_target_pairs={{0,2},{1,3},{2,4},{3,5},{4,6},{5,7},{6,8},{7,9},{8,10},{9,11},{10,... | collective-permute-start | bytes 1572872 | tf_op jit(solution)/shard_map/ppermute | solution.py:81
  10.8 4.3 %collective-permute-start = (bf16[256,1024]{1,0:T(8,128)(2,1)}, bf16[256,1024]{1,0:T(8,128)(2,1)S(1)}, u32[]{:S(2)}, u32[]{:S(2)}) collective-permute-start(bf16[256,1024]{1,0:T(8,128)(2,1)} %refs_4_.1), channel_id=1, source_target_pairs={{12,16},{13,17},{28,32},{29,33},{44,48},{45,49},{60,64},{61,65},{7... | collective-permute-start | bytes 1572872 | tf_op jit(solution)/shard_map/ppermute | solution.py:81
  15.1 0.0 collective-permute-done.1.refs_2_
  15.1 14.1 %collective-permute-start.2 = (bf16[256,1024]{1,0:T(8,128)(2,1)}, bf16[256,1024]{1,0:T(8,128)(2,1)S(1)}, u32[]{:S(2)}, u32[]{:S(2)}) collective-permute-start(bf16[256,1024]{1,0:T(8,128)(2,1)} %collective-permute-done.1.refs_2_), channel_id=1, source_target_pairs={{0,2},{1,3},{2,4},{3,5},{4,6},{5,7},{6,8},{7,9},{8,10},{9,11},{10,... | collective-permute-start | bytes 1572872 | tf_op jit(solution)/shard_map/ppermute | solution.py:81
  29.2 2.1 %collective-permute-start.9 = (bf16[256,1024]{1,0:T(8,128)(2,1)}, bf16[256,1024]{1,0:T(8,128)(2,1)}, u32[]{:S(2)}, u32[]{:S(2)}) collective-permute-start(bf16[256,1024]{1,0:T(8,128)(2,1)} %refs_9_.1), channel_id=1, source_target_pairs={{0,1},{2,3},{4,5},{6,7},{8,9},{10,11},{12,13},{14,15},{16,17},{18,... | collective-permute-start | bytes 1572872 | tf_op jit(solution)/shard_map/ppermute | solution.py:81
  31.3 0.0 collective-permute-done.3
  31.3 6.4 %collective-permute-start.6 = (bf16[256,1024]{1,0:T(8,128)(2,1)}, bf16[256,1024]{1,0:T(8,128)(2,1)S(1)}, u32[]{:S(2)}, u32[]{:S(2)}) collective-permute-start(bf16[256,1024]{1,0:T(8,128)(2,1)} %refs_9_.1), channel_id=1, source_target_pairs={{12,16},{13,17},{28,32},{29,33},{44,48},{45,49},{60,64},{61,65},{7... | collective-permute-start | bytes 1572872 | tf_op jit(solution)/shard_map/ppermute | solution.py:81
  37.8 0.0 collective-permute-done.7.refs_7_
  37.8 9.9 %collective-permute-start.8 = (bf16[256,1024]{1,0:T(8,128)(2,1)}, bf16[256,1024]{1,0:T(8,128)(2,1)S(1)}, u32[]{:S(2)}, u32[]{:S(2)}) collective-permute-start(bf16[256,1024]{1,0:T(8,128)(2,1)} %collective-permute-done.7.refs_7_), channel_id=1, source_target_pairs={{0,2},{1,3},{2,4},{3,5},{4,6},{5,7},{6,8},{7,9},{8,10},{9,11},{10,... | collective-permute-start | bytes 1572872 | tf_op jit(solution)/shard_map/ppermute | solution.py:81
  47.7 0.0 collective-permute-done
  47.7 1.9 %collective-permute-start.4 = (bf16[256,1024]{1,0:T(8,128)(2,1)}, bf16[256,1024]{1,0:T(8,128)(2,1)}, u32[]{:S(2)}, u32[]{:S(2)}) collective-permute-start(bf16[256,1024]{1,0:T(8,128)(2,1)} %collective-permute-done.1.refs_2_), channel_id=1, source_target_pairs={{0,1},{1,0},{2,3},{3,2},{4,5},{5,4},{6,7},{7,6},{8,9},{9,8},{10,11... | collective-permute-start | bytes 1572872 | tf_op jit(solution)/shard_map/ppermute | solution.py:81
  49.6 0.0 collective-permute-done.2
  49.6 0.1 broadcast_select_fusion.5.refs_0_
  49.7 0.0 copy-start
  49.7 1.3 %collective-permute-start.5 = (bf16[256,1024]{1,0:T(8,128)(2,1)S(1)}, bf16[256,1024]{1,0:T(8,128)(2,1)}, u32[]{:S(2)}, u32[]{:S(2)}) collective-permute-start(bf16[256,1024]{1,0:T(8,128)(2,1)S(1)} %broadcast_select_fusion.5.refs_0_), channel_id=1, source_target_pairs={{1,0},{3,2},{5,4},{7,6},{9,8},{11,10},{13,12},{15,14},{17,16},{19,... | collective-permute-start | bytes 1572872 | tf_op jit(solution)/shard_map/ppermute | solution.py:81
  51.0 0.0 collective-permute-done.9
  51.0 4.8 %collective-permute-start.10 = (bf16[256,1024]{1,0:T(8,128)(2,1)}, bf16[256,1024]{1,0:T(8,128)(2,1)S(1)}, u32[]{:S(2)}, u32[]{:S(2)}) collective-permute-start(bf16[256,1024]{1,0:T(8,128)(2,1)} %collective-permute-done.7.refs_7_), channel_id=1, source_target_pairs={{0,1},{1,0},{2,3},{3,2},{4,5},{5,4},{6,7},{7,6},{8,9},{9,8},{10,11... | collective-permute-start | bytes 1572872 | tf_op jit(solution)/shard_map/ppermute | solution.py:81
  55.8 0.1 collective-permute-done.6
  55.8 3.4 %collective-permute-done.8 = bf16[256,1024]{1,0:T(8,128)(2,1)S(1)} collective-permute-done((bf16[256,1024]{1,0:T(8,128)(2,1)}, bf16[256,1024]{1,0:T(8,128)(2,1)S(1)}, u32[]{:S(2)}, u32[]{:S(2)}) %collective-permute-start.8) | collective-permute-done | bytes 524320 | tf_op jit(solution)/shard_map/ppermute | solution.py:81
  59.2 0.1 broadcast_select_fusion.4.refs_5_
  59.3 0.0 copy-done
  59.3 0.0 copy-start.1
  59.3 1.3 %collective-permute-start.11 = (bf16[256,1024]{1,0:T(8,128)(2,1)S(1)}, bf16[256,1024]{1,0:T(8,128)(2,1)S(1)}, u32[]{:S(2)}, u32[]{:S(2)}) collective-permute-start(bf16[256,1024]{1,0:T(8,128)(2,1)S(1)} %broadcast_select_fusion.4.refs_5_), channel_id=1, source_target_pairs={{1,0},{3,2},{5,4},{7,6},{9,8},{11,10},{13,12},{15,14},{17,16},{19,... | collective-permute-start | bytes 1572872 | tf_op jit(solution)/shard_map/ppermute | solution.py:81
  60.6 0.5 compare_convert_fusion.valid_ref
  61.2 5.9 %collective-permute-done.4 = bf16[256,1024]{1,0:T(8,128)(2,1)} collective-permute-done((bf16[256,1024]{1,0:T(8,128)(2,1)}, bf16[256,1024]{1,0:T(8,128)(2,1)}, u32[]{:S(2)}, u32[]{:S(2)}) %collective-permute-start.4) | collective-permute-done | bytes 524320 | tf_op jit(solution)/shard_map/ppermute | solution.py:81
  67.1 7.9 %collective-permute-done.5 = bf16[256,1024]{1,0:T(8,128)(2,1)} collective-permute-done((bf16[256,1024]{1,0:T(8,128)(2,1)S(1)}, bf16[256,1024]{1,0:T(8,128)(2,1)}, u32[]{:S(2)}, u32[]{:S(2)}) %collective-permute-start.5) | collective-permute-done | bytes 524320 | tf_op jit(solution)/shard_map/ppermute | solution.py:81
  75.0 2.3 %broadcast_select_fusion.2 = (bf16[256,1024]{1,0:T(8,128)(2,1)}, bf16[256,1024]{1,0:T(8,128)(2,1)}) fusion(bf16[256,1024]{1,0:T(8,128)(2,1)S(1)} %collective-permute-done.3, bf16[256,1024]{1,0:T(8,128)(2,1)} %collective-permute-done.4, pred[]{:T(512)S(6)} %eq.6, bf16[256,1024]{1,0:T(8,128)(2,1)} %collective-permute-done.5), kind=kLoop, calls=%fused_computation.2 | loop fusion | flops 524288 | bytes 2621441 | tf_op jit(solution)/shard_map/jit(_where)/select_n | solution.py:105
  77.2 0.0 copy-done.1
  77.2 9.0 %collective-permute-done.10 = bf16[256,1024]{1,0:T(8,128)(2,1)S(1)} collective-permute-done((bf16[256,1024]{1,0:T(8,128)(2,1)}, bf16[256,1024]{1,0:T(8,128)(2,1)S(1)}, u32[]{:S(2)}, u32[]{:S(2)}) %collective-permute-start.10) | collective-permute-done | bytes 524320 | tf_op jit(solution)/shard_map/ppermute | solution.py:81
  86.2 6.6 %collective-permute-done.11 = bf16[256,1024]{1,0:T(8,128)(2,1)S(1)} collective-permute-done((bf16[256,1024]{1,0:T(8,128)(2,1)S(1)}, bf16[256,1024]{1,0:T(8,128)(2,1)S(1)}, u32[]{:S(2)}, u32[]{:S(2)}) %collective-permute-start.11) | collective-permute-done | bytes 524320 | tf_op jit(solution)/shard_map/ppermute | solution.py:81
  92.8 1.1 broadcast_select_fusion
  93.8 15.5 %shard_map.37 = bf16[256,2048]{1,0:T(8,128)(2,1)} custom-call(s32[5]{0:T(128)} %compare_convert_fusion.valid_ref, bf16[256,2048]{1,0:T(8,128)(2,1)} %q_ref.1, bf16[256,1024]{1,0:T(8,128)(2,1)} %copy-done, bf16[256,1024]{1,0:T(8,128)(2,1)} %get-tuple-element.12.refs_1_, bf16[256,1024]{1,0:T(8,128)(2,1)} %collective-permute-done.1.refs_2_, ...), custom_call_target="tpu_custom_call" | custom-call | flops 2684354560 | bytes 7340032 | tf_op jit(solution)/shard_map/pallas_call | solution.py:67
Async XLA Ops:
  0.0 15.1 %collective-permute-start.1 = (bf16[256,1024]{1,0:T(8,128)(2,1)}, bf16[256,1024]{1,0:T(8,128)(2,1)}, u32[]{:S(2)}, u32[]{:S(2)}) collective-permute-start(bf16[256,1024]{1,0:T(8,128)(2,1)} %refs_4_.1), channel_id=1, source_target_pairs={{0,2},{1,3},{2,4},{3,5},{4,6},{5,7},{6,8},{7,9},{8,10},{9,11},{10,... | collective-permute-start | bytes 1572872 | tf_op jit(solution)/shard_map/ppermute | solution.py:81
  2.8 28.5 %collective-permute-start.3 = (bf16[256,1024]{1,0:T(8,128)(2,1)}, bf16[256,1024]{1,0:T(8,128)(2,1)S(1)}, u32[]{:S(2)}, u32[]{:S(2)}) collective-permute-start(bf16[256,1024]{1,0:T(8,128)(2,1)} %refs_4_.1), channel_id=1, source_target_pairs={{0,1},{2,3},{4,5},{6,7},{8,9},{10,11},{12,13},{14,15},{16,17},{18,... | collective-permute-start | bytes 1572872 | tf_op jit(solution)/shard_map/ppermute | solution.py:81
  6.1 31.7 %collective-permute-start.7 = (bf16[256,1024]{1,0:T(8,128)(2,1)}, bf16[256,1024]{1,0:T(8,128)(2,1)}, u32[]{:S(2)}, u32[]{:S(2)}) collective-permute-start(bf16[256,1024]{1,0:T(8,128)(2,1)} %refs_9_.1), channel_id=1, source_target_pairs={{0,2},{1,3},{2,4},{3,5},{4,6},{5,7},{6,8},{7,9},{8,10},{9,11},{10,... | collective-permute-start | bytes 1572872 | tf_op jit(solution)/shard_map/ppermute | solution.py:81
  10.8 36.9 %collective-permute-start = (bf16[256,1024]{1,0:T(8,128)(2,1)}, bf16[256,1024]{1,0:T(8,128)(2,1)S(1)}, u32[]{:S(2)}, u32[]{:S(2)}) collective-permute-start(bf16[256,1024]{1,0:T(8,128)(2,1)} %refs_4_.1), channel_id=1, source_target_pairs={{12,16},{13,17},{28,32},{29,33},{44,48},{45,49},{60,64},{61,65},{7... | collective-permute-start | bytes 1572872 | tf_op jit(solution)/shard_map/ppermute | solution.py:81
  15.1 34.5 %collective-permute-start.2 = (bf16[256,1024]{1,0:T(8,128)(2,1)}, bf16[256,1024]{1,0:T(8,128)(2,1)S(1)}, u32[]{:S(2)}, u32[]{:S(2)}) collective-permute-start(bf16[256,1024]{1,0:T(8,128)(2,1)} %collective-permute-done.1.refs_2_), channel_id=1, source_target_pairs={{0,2},{1,3},{2,4},{3,5},{4,6},{5,7},{6,8},{7,9},{8,10},{9,11},{10,... | collective-permute-start | bytes 1572872 | tf_op jit(solution)/shard_map/ppermute | solution.py:81
  29.2 21.8 %collective-permute-start.9 = (bf16[256,1024]{1,0:T(8,128)(2,1)}, bf16[256,1024]{1,0:T(8,128)(2,1)}, u32[]{:S(2)}, u32[]{:S(2)}) collective-permute-start(bf16[256,1024]{1,0:T(8,128)(2,1)} %refs_9_.1), channel_id=1, source_target_pairs={{0,1},{2,3},{4,5},{6,7},{8,9},{10,11},{12,13},{14,15},{16,17},{18,... | collective-permute-start | bytes 1572872 | tf_op jit(solution)/shard_map/ppermute | solution.py:81
  31.3 24.5 %collective-permute-start.6 = (bf16[256,1024]{1,0:T(8,128)(2,1)}, bf16[256,1024]{1,0:T(8,128)(2,1)S(1)}, u32[]{:S(2)}, u32[]{:S(2)}) collective-permute-start(bf16[256,1024]{1,0:T(8,128)(2,1)} %refs_9_.1), channel_id=1, source_target_pairs={{12,16},{13,17},{28,32},{29,33},{44,48},{45,49},{60,64},{61,65},{7... | collective-permute-start | bytes 1572872 | tf_op jit(solution)/shard_map/ppermute | solution.py:81
  37.8 21.5 %collective-permute-start.8 = (bf16[256,1024]{1,0:T(8,128)(2,1)}, bf16[256,1024]{1,0:T(8,128)(2,1)S(1)}, u32[]{:S(2)}, u32[]{:S(2)}) collective-permute-start(bf16[256,1024]{1,0:T(8,128)(2,1)} %collective-permute-done.7.refs_7_), channel_id=1, source_target_pairs={{0,2},{1,3},{2,4},{3,5},{4,6},{5,7},{6,8},{7,9},{8,10},{9,11},{10,... | collective-permute-start | bytes 1572872 | tf_op jit(solution)/shard_map/ppermute | solution.py:81
  47.7 19.4 %collective-permute-start.4 = (bf16[256,1024]{1,0:T(8,128)(2,1)}, bf16[256,1024]{1,0:T(8,128)(2,1)}, u32[]{:S(2)}, u32[]{:S(2)}) collective-permute-start(bf16[256,1024]{1,0:T(8,128)(2,1)} %collective-permute-done.1.refs_2_), channel_id=1, source_target_pairs={{0,1},{1,0},{2,3},{3,2},{4,5},{5,4},{6,7},{7,6},{8,9},{9,8},{10,11... | collective-permute-start | bytes 1572872 | tf_op jit(solution)/shard_map/ppermute | solution.py:81
  49.7 9.6 %copy-start = (bf16[256,1024]{1,0:T(8,128)(2,1)}, bf16[256,1024]{1,0:T(8,128)(2,1)S(1)}, u32[]{:S(2)}) copy-start(bf16[256,1024]{1,0:T(8,128)(2,1)S(1)} %broadcast_select_fusion.5.refs_0_) | copy-start | bytes 1572868
  49.7 25.3 %collective-permute-start.5 = (bf16[256,1024]{1,0:T(8,128)(2,1)S(1)}, bf16[256,1024]{1,0:T(8,128)(2,1)}, u32[]{:S(2)}, u32[]{:S(2)}) collective-permute-start(bf16[256,1024]{1,0:T(8,128)(2,1)S(1)} %broadcast_select_fusion.5.refs_0_), channel_id=1, source_target_pairs={{1,0},{3,2},{5,4},{7,6},{9,8},{11,10},{13,12},{15,14},{17,16},{19,... | collective-permute-start | bytes 1572872 | tf_op jit(solution)/shard_map/ppermute | solution.py:81
  51.0 35.2 %collective-permute-start.10 = (bf16[256,1024]{1,0:T(8,128)(2,1)}, bf16[256,1024]{1,0:T(8,128)(2,1)S(1)}, u32[]{:S(2)}, u32[]{:S(2)}) collective-permute-start(bf16[256,1024]{1,0:T(8,128)(2,1)} %collective-permute-done.7.refs_7_), channel_id=1, source_target_pairs={{0,1},{1,0},{2,3},{3,2},{4,5},{5,4},{6,7},{7,6},{8,9},{9,8},{10,11... | collective-permute-start | bytes 1572872 | tf_op jit(solution)/shard_map/ppermute | solution.py:81
  59.3 17.9 %copy-start.1 = (bf16[256,1024]{1,0:T(8,128)(2,1)}, bf16[256,1024]{1,0:T(8,128)(2,1)S(1)}, u32[]{:S(2)}) copy-start(bf16[256,1024]{1,0:T(8,128)(2,1)S(1)} %broadcast_select_fusion.4.refs_5_) | copy-start | bytes 1572868
  59.3 33.4 %collective-permute-start.11 = (bf16[256,1024]{1,0:T(8,128)(2,1)S(1)}, bf16[256,1024]{1,0:T(8,128)(2,1)S(1)}, u32[]{:S(2)}, u32[]{:S(2)}) collective-permute-start(bf16[256,1024]{1,0:T(8,128)(2,1)S(1)} %broadcast_select_fusion.4.refs_5_), channel_id=1, source_target_pairs={{1,0},{3,2},{5,4},{7,6},{9,8},{11,10},{13,12},{15,14},{17,16},{19,... | collective-permute-start | bytes 1572872 | tf_op jit(solution)/shard_map/ppermute | solution.py:81
